TPU v7x, 512 devices: a whole 4x4x16 slice. The times are simulated.
512 devices in a mesh: dp: 32 (over y, x, core), wide: 16 (over z).
Axes of the slice: x: 4, y: 4, z: 16, core: 2. Of those that a mesh axis runs over, the one named last changes fastest.
Arguments:
- trunk_out: bfloat16 [16384, 1024], P('dp'), may hold values from -6 to 6
- projection: bfloat16 [1024, 4096], P(None, 'wide'), may hold values from -0.1875 to 0.1875
- transform: bfloat16 [4096, 4096], P('wide'), may hold values from -0.125 to 0.125
- block_mask: int32 [32, 32], P('wide'), may hold values from 0 to 1, as said below
- old_index: bfloat16 [16384, 4096], P('dp', 'wide'), may hold values from -6 to 6
- doc_ids: int32 [16384, 4], P('dp'), may hold values from 0 to 16383, as said below
- labels: int32 [16384, 4], P('dp'), may hold values 0 or 1
Outputs:
- new_embed: bfloat16 [16384, 4096], P('dp', 'wide')
- pair_loss: float32 [16384, 4], P('dp')
- trunk_grad: bfloat16 [16384, 4096], P('dp', 'wide')
Inputs may be any that keep to these rules, and one draw needn't show every extreme that they name: `doc_ids`: in each aligned block of 512 rows, no shard id // 512 is named more than 128 times, and one shard is named exactly 128 times. `block_mask`: each block row has 4 to 24 nonzero entries, and some block row has exactly 24.
All inputs are finite; a program needn't handle non-finite values. No bound on the sum of `labels` on one device may be relied on, other than what follows from the above.
Results may differ from a plain program's by a relative error of at most 0.015.
Values may be sent and summed in bfloat16 or wider, within the bound.
No kernel may reach another device: no remote copies, remote signals or barrier semaphores. Data moves between devices by JAX's collectives and lax.ppermute only.
A program may use at most 128 MiB of HBM per device.

v0:
```python
import math

import jax
import jax.numpy as jnp
from jax import lax
from jax.sharding import PartitionSpec as P

E = 4096
K = 4


def local(trunk_out, projection, transform, block_mask, old_index, doc_ids, labels):
    rows = trunk_out.shape[0]
    e_local = transform.shape[0]
    width = transform.shape[1]
    local_blocks, nblocks = block_mask.shape
    side = e_local // local_blocks
    query = jnp.dot(trunk_out, projection, preferred_element_type=jnp.float32).astype(jnp.bfloat16)
    blocks = transform.reshape(local_blocks, side, nblocks, side)
    masked = (blocks * block_mask[:, None, :, None].astype(jnp.bfloat16)).reshape(e_local, width)
    term = jnp.dot(query, masked, preferred_element_type=jnp.float32)
    new = lax.psum_scatter(
        term.astype(jnp.bfloat16), "wide", scatter_dimension=1, tiled=True
    ).astype(jnp.float32)
    flat = doc_ids.reshape(-1)
    whole = lax.all_gather(old_index, "dp", axis=0, tiled=True)
    old_vec = whole[flat].reshape(rows, K, e_local)
    old_wide = old_vec.astype(jnp.float32)
    scale = 1.0 / math.sqrt(E)
    partial_scores = jnp.einsum("re,rke->rk", new, old_wide)
    score = lax.psum(partial_scores, "wide") * scale
    sign = 2.0 * labels.astype(jnp.float32) - 1.0
    pair_loss = jax.nn.softplus(-sign * score)
    dscore = -sign * jax.nn.sigmoid(-sign * score)
    grad_local = (jnp.einsum("rk,rke->re", dscore, old_wide) * scale).astype(jnp.bfloat16)
    grad_full = lax.all_gather(grad_local, "wide", axis=1, tiled=True)
    trunk_grad = lax.dot_general(
        grad_full, masked, (((1,), (1,)), ((), ())), preferred_element_type=jnp.float32
    )
    return (new.astype(jnp.bfloat16), pair_loss, trunk_grad.astype(jnp.bfloat16))


def solution(mesh):
    return jax.shard_map(
        local,
        mesh=mesh,
        in_specs=(
            P("dp", None),
            P(None, "wide"),
            P("wide", None),
            P("wide", None),
            P("dp", "wide"),
            P("dp", None),
            P("dp", None),
        ),
        out_specs=(P("dp", "wide"), P("dp", None), P("dp", "wide")),
        check_vma=False,
    )
```

profile of v0, /device:TPU:6, one launch (start us, length us, event | category | flops | bytes accessed | tf_op | source)
XLA Modules:
  0.0 241.0 jit_solution(8100249756165127333)
XLA Ops:
  8.0 0.0 copy-start
  8.0 0.0 all-gather.3.cloned.1.call-start
  8.1 0.7 all-gather.3.cloned.1.call-update
  8.7 0.0 reduce-scatter.2.cloned.1.call-start
  8.8 0.7 convert_element_type.23
  9.5 0.3 mul.36
  9.8 0.0 copy-done
  9.8 5.8 %convolution_convert_fusion = bf16[512,4096]{1,0:T(8,128)(2,1)} fusion(bf16[512,1024]{1,0:T(8,128)(2,1)S(1)} %copy-done, bf16[1024,256]{1,0:T(8,128)(2,1)} %param.8, bf16[256,4096]{1,0:T(8,128)(2,1)} %param.9, bf16[32,8,32,128]{3,2,1,0:T(8,128)(2,1)S(1)} %bitcast.21), kind=kOutput, calls=%fused_computation.1 | convolution fusion | flops 1345454080 | bytes 9961472 | tf_op jit(solution)/shard_map/dot_general | solution.py:21
  15.7 0.0 copy-start.2
  15.7 0.0 reduce-scatter.2.cloned.1.call-update
  15.7 0.0 all-gather.5.cloned.1.call-start
  15.7 0.6 copy-done.2
  16.4 0.1 copy.10
  16.5 0.2 reshape.45
  16.7 67.9 %all-gather.3.cloned.1.call-done = bf16[16384,256]{1,0:T(8,128)(2,1)} async-done(((bf16[512,256]{1,0:T(8,128)(2,1)}), bf16[16384,256]{1,0:T(8,128)(2,1)}) %all-gather.3.cloned.1.call-update) | async-done | bytes 8388624 | tf_op jit(solution)/shard_map/all_gather | solution.py:26
  84.6 13.0 %gather_fusion = bf16[2048,256]{1,0:T(8,128)(2,1)} fusion(bf16[16384,256]{1,0:T(8,128)(2,1)} %all-gather.3.cloned.1.call-done, s32[2048]{0:T(1024)S(1)} %broadcast_clamp_fusion), kind=kCustom, calls=%fused_computation | custom fusion | bytes 2105344 | tf_op jit(solution)/shard_map/gather | solution.py:27
  97.6 2.1 reshape.46
  99.8 0.1 reduce-scatter.2.cloned.1.call-done
  99.9 0.0 copy-start.1
  99.9 2.0 fusion.1
  101.9 0.1 copy.12
  102.0 31.7 %psum.7 = f32[512,4]{0,1:T(4,128)S(1)} all-reduce(f32[512,4]{0,1:T(4,128)S(1)} %bitcast.23), channel_id=1, replica_groups=mesh['dp'=32,'wide'=16] {'wide'}, use_global_device_ids=true, to_apply=%region_1.0 | all-reduce | flops 2048 | bytes 16384 | tf_op jit(solution)/shard_map/psum | solution.py:31
  133.7 0.0 copy-done.1
  133.7 0.2 copy.13
  134.0 1.9 fusion.4
  135.9 0.7 fusion
  136.6 0.0 all-gather.5.cloned.1.call-update
  136.6 0.6 compare_select_fusion.1
  137.3 91.4 %all-gather.5.cloned.1.call-done = bf16[512,4096]{1,0:T(8,128)(2,1)} async-done(((bf16[512,256]{1,0:T(8,128)(2,1)}), bf16[512,4096]{1,0:T(8,128)(2,1)}) %all-gather.5.cloned.1.call-update) | async-done | bytes 4194320 | tf_op jit(solution)/shard_map/all_gather | solution.py:36
  228.7 4.9 %convolution_convert_fusion.1 = bf16[512,256]{1,0:T(8,128)(2,1)} fusion(bf16[512,4096]{1,0:T(8,128)(2,1)} %all-gather.5.cloned.1.call-done, bf16[256,4096]{1,0:T(8,128)(2,1)} %param.9, bf16[32,8,32,128]{3,2,1,0:T(8,128)(2,1)S(1)} %bitcast.22), kind=kOutput, calls=%fused_computation.3 | convolution fusion | flops 1074921472 | bytes 8650752 | tf_op jit(solution)/shard_map/dot_general | solution.py:37
  (3 shorter events, 0.0 us)
Async XLA Ops:
  8.0 1.8 copy-start
  8.0 76.6 %all-gather.3.cloned.1.call-start = ((), (), s32[]{:S(2)}) async-start(), calls=%async_computation.2 | async-start | bytes 8650752 | tf_op jit(solution)/shard_map/all_gather | solution.py:26
  8.7 91.2 %reduce-scatter.2.cloned.1.call-start = ((), (), s32[]{:S(2)}) async-start(), calls=%async_computation.1 | async-start | bytes 4456448 | tf_op jit(solution)/shard_map/reduce_scatter | solution.py:22
  15.7 0.7 copy-start.2
  15.7 213.0 %all-gather.5.cloned.1.call-start = ((), (), s32[]{:S(2)}) async-start(), calls=%async_computation.3 | async-start | bytes 4456448 | tf_op jit(solution)/shard_map/all_gather | solution.py:36
  99.9 33.8 %copy-start.1 = (s32[512,4]{0,1:T(4,128)S(1)}, s32[512,4]{0,1:T(4,128)}, u32[]{:S(2)}) copy-start(s32[512,4]{0,1:T(4,128)} %param.13) | copy-start | bytes 24580
Sparse Core Ops, SparseCore 0:
  12.0 72.5 all-gather.2
Sparse Core Ops, SparseCore 1:
  15.8 84.1 reduce-scatter.1
  136.7 91.9 all-gather.4
where the time goes:
time: 241 us
  waiting for transfers between devices  160 us (66%)
  blocking collectives  31.7 us (13%)
  local copies, waits for them, and re-layouts  16.8 us (7%)
  between operations  15.6 us (6%)
  matrix products  14.6 us (6%)
    all_gather x1, waiting for transfers between devices, local(): grad_full = lax.all_gather(grad_local, 'wide', axis=1, tiled=True)  91.4 us
    all_gather x1, waiting for transfers between devices, local(): whole = lax.all_gather(old_index, 'dp', axis=0, tiled=True)  67.9 us
    psum x1, blocking collectives, local(): score = lax.psum(partial_scores, 'wide') * scale  31.7 us
    gather x1, local copies, waits for them, and re-layouts, local(): old_vec = whole[flat].reshape(rows, K, e_local)  13 us
    dot_general x1, matrix products, local(): term = jnp.dot(query, masked, preferred_element_type=jnp.float32)  5.83 us
    dot_general x1, matrix products, local(): lax.dot_general(grad_full, masked, (((1,), (1,)), ((), ())), preferred_el...  4.9 us
  transfers between devices with their start and end apart: 3, of which 3 were waited for; matrix products, arithmetic and copies ran while one was open for 10% of the time, Pallas kernels for 0%

commit v1 on v0

--- a/solution.py
+++ b/solution.py
@@ -7,24 +7,39 @@
 
 E = 4096
 K = 4
+CAP = 128
 
 
-def local(trunk_out, projection, transform, block_mask, old_index, doc_ids, labels):
-    rows = trunk_out.shape[0]
-    e_local = transform.shape[0]
-    width = transform.shape[1]
+def local(n_dp, trunk_out, projection, transform, block_mask, old_index, doc_ids, labels):
+    rows, dmodel = trunk_out.shape
+    e_local, width = transform.shape
     local_blocks, nblocks = block_mask.shape
     side = e_local // local_blocks
-    query = jnp.dot(trunk_out, projection, preferred_element_type=jnp.float32).astype(jnp.bfloat16)
+    doc_shard = old_index.shape[0]
     blocks = transform.reshape(local_blocks, side, nblocks, side)
     masked = (blocks * block_mask[:, None, :, None].astype(jnp.bfloat16)).reshape(e_local, width)
-    term = jnp.dot(query, masked, preferred_element_type=jnp.float32)
-    new = lax.psum_scatter(
-        term.astype(jnp.bfloat16), "wide", scatter_dimension=1, tiled=True
-    ).astype(jnp.float32)
+
+    chunk = dmodel // n_dp
+    me = lax.axis_index("dp")
+    proj_rows = lax.dynamic_slice_in_dim(projection, me * chunk, chunk, 0)
+    w_part = jnp.dot(proj_rows, masked, preferred_element_type=jnp.float32)
+    w_blk = lax.psum_scatter(w_part, "wide", scatter_dimension=1, tiled=True)
+    w_cols = lax.all_gather(w_blk.astype(jnp.bfloat16), "dp", axis=0, tiled=True)
+    new = jnp.dot(trunk_out, w_cols, preferred_element_type=jnp.float32)
+
     flat = doc_ids.reshape(-1)
-    whole = lax.all_gather(old_index, "dp", axis=0, tiled=True)
-    old_vec = whole[flat].reshape(rows, K, e_local)
+    owner = flat // doc_shard
+    loc = flat - owner * doc_shard
+    onehot = (owner[:, None] == jnp.arange(n_dp, dtype=jnp.int32)[None, :]).astype(jnp.int32)
+    before = jnp.cumsum(onehot, axis=0) - onehot
+    rank = jnp.sum(before * onehot, axis=1)
+    slot = owner * CAP + rank
+    req = jnp.zeros((n_dp * CAP,), jnp.int32).at[slot].set(loc, unique_indices=True)
+    asked = lax.all_to_all(req.reshape(n_dp, CAP), "dp", 0, 0, tiled=True)
+    served = old_index[asked.reshape(-1)].reshape(n_dp, CAP, e_local)
+    back = lax.all_to_all(served, "dp", 0, 0, tiled=True).reshape(n_dp * CAP, e_local)
+    old_vec = back[slot].reshape(rows, K, e_local)
+
     old_wide = old_vec.astype(jnp.float32)
     scale = 1.0 / math.sqrt(E)
     partial_scores = jnp.einsum("re,rke->rk", new, old_wide)
@@ -41,8 +56,9 @@
 
 
 def solution(mesh):
+    n_dp = mesh.shape["dp"]
     return jax.shard_map(
-        local,
+        lambda *a: local(n_dp, *a),
         mesh=mesh,
         in_specs=(
             P("dp", None),

time: 241 us -> 319 us (1.32)
  blocking collectives: 31.7 us -> 67.4 us
  local copies, waits for them, and re-layouts: 16.8 us -> 43.3 us
  other arithmetic: 2.09 us -> 12.4 us
  starting transfers between devices: 0.13 us -> 5.98 us
  waiting for transfers between devices: 160 us -> 164 us
  matrix products: 14.6 us -> 10.7 us
    reduce_scatter x1, waiting for transfers between devices: 0.13 us -> 72.5 us  [local(): w_blk = lax.psum_scatter(w_part, 'wide', scatter_dimension=1, tiled=True)]
    all_gather x1 -> x0, waiting for transfers between devices: 67.9 us -> none  [local(): whole = lax.all_gather(old_index, 'dp', axis=0, tiled=True)]
    all_gather x0 -> x1, blocking collectives: none -> 24.4 us  [local(): lax.all_gather(w_blk.astype(jnp.bfloat16), 'dp', axis=0, tiled=True)]
    all_to_all x0 -> x1, blocking collectives: none -> 14.1 us  [local(): asked = lax.all_to_all(req.reshape(n_dp, CAP), 'dp', 0, 0, tiled=True)]
    gather x1 -> x2, local copies, waits for them, and re-layouts: 13 us -> 25.9 us  [the longest x1 16.9 us: local(): served = old_index[asked.reshape(-1)].reshape(n_dp, CAP, e_local)]
    another operation x0 -> x3, other arithmetic: none -> 9.41 us
    scatter x0 -> x1, local copies, waits for them, and re-layouts: none -> 8.06 us  [local(): jnp.zeros((n_dp * CAP,), jnp.int32).at[slot].set(loc, unique_indices=True)]
    all_to_all x0 -> x1, starting transfers between devices: none -> 5.89 us  [local(): lax.all_to_all(served, 'dp', 0, 0, tiled=True).reshape(n_dp * CAP, e_local)]
  transfers between devices with their start and end apart: 3 -> 3, of which waited for: 3 -> 2; matrix products, arithmetic and copies ran while one was open for 10% -> 3% of each run, Pallas kernels for 0% -> 0%
where the time goes in v1:
time: 319 us; the launch traced here: 318 us
  waiting for transfers between devices  164 us (51%)
  blocking collectives  67.4 us (21%)
  local copies, waits for them, and re-layouts  43.3 us (14%)
  between operations  14.3 us (4%)
  other arithmetic  12.4 us (4%)
  matrix products  10.7 us (3%)
  starting transfers between devices  5.98 us (2%)
    all_gather x1, waiting for transfers between devices, local(): grad_full = lax.all_gather(grad_local, 'wide', axis=1, tiled=True)  91.9 us
    reduce_scatter x1, waiting for transfers between devices, local(): w_blk = lax.psum_scatter(w_part, 'wide', scatter_dimension=1, tiled=True)  72.5 us
    psum x1, blocking collectives, local(): score = lax.psum(partial_scores, 'wide') * scale  28.9 us
    all_gather x1, blocking collectives, local(): lax.all_gather(w_blk.astype(jnp.bfloat16), 'dp', axis=0, tiled=True)  24.4 us
    gather x1, local copies, waits for them, and re-layouts, local(): served = old_index[asked.reshape(-1)].reshape(n_dp, CAP, e_local)  16.9 us
    all_to_all x1, blocking collectives, local(): asked = lax.all_to_all(req.reshape(n_dp, CAP), 'dp', 0, 0, tiled=True)  14.1 us
    another operation x3, other arithmetic  9.41 us
    gather x1, local copies, waits for them, and re-layouts, local(): old_vec = back[slot].reshape(rows, K, e_local)  9 us
  transfers between devices with their start and end apart: 3, of which 2 were waited for; matrix products, arithmetic and copies ran while one was open for 3% of the time, Pallas kernels for 0%

profile of v1, /device:TPU:6, one launch (start us, length us, event | category | flops | bytes accessed | tf_op | source)
XLA Modules:
  0.0 318.5 jit_solution(10625858685940429330)
XLA Ops:
  7.2 0.9 copy.11
  8.1 0.2 reshape.183
  8.3 0.2 reshape.182
  8.5 0.2 reshape.181
  8.7 9.1 %reduce-window.6 = s32[32,16,128]{2,1,0:T(8,128)S(1)} reduce-window(s32[32,16,128]{2,1,0:T(8,128)S(1)} %fusion.5, s32[]{:T(128)} %constant.20.clone.1), window={size=1x1x128 pad=0_0x0_0x127_0}, to_apply=%region_1.2 | reduce-window | flops 8323072 | bytes 524292 | tf_op jit(solution)/shard_map/reduce-window
  17.9 0.2 copy.24
  18.2 0.2 reduce-window.9
  18.4 0.1 broadcast_add_fusion
  18.7 8.1 %scatter_custom_fusion = s32[4096]{0:T(1024)S(1)} fusion(s32[2048]{0:T(1024)S(1)} %bitcast.60, s32[2048]{0:T(1024)S(1)} %get-tuple-element.9, s32[]{:T(128)} %constant.20.clone.1), kind=kCustom, calls=%fused_computation.42 | custom fusion | bytes 16388 | tf_op jit(solution)/shard_map/scatter | solution.py:37
  26.7 14.1 %all_to_all.14 = s32[32,1,128]{2,1,0:T(1,128)S(1)} all-to-all(s32[32,1,128]{2,1,0:T(1,128)S(1)} %bitcast.57), channel_id=1, replica_groups=mesh['dp'=32,'wide'=16] {'dp'}, dimensions={0} | all-to-all | bytes 32768 | tf_op jit(solution)/shard_map/all_to_all | solution.py:38
  40.9 16.9 %gather_fusion = bf16[4096,256]{1,0:T(8,128)(2,1)} fusion(bf16[512,256]{1,0:T(8,128)(2,1)S(1)} %copy-done.1, s32[4096]{0:T(1024)S(1)} %broadcast_clamp_fusion), kind=kCustom, calls=%fused_computation | custom fusion | bytes 4210688 | tf_op jit(solution)/shard_map/gather | solution.py:39
  57.8 5.9 %all-to-all-start.1 = ((bf16[32,128,256]{2,1,0:T(8,128)(2,1)}), bf16[32,128,256]{2,1,0:T(8,128)(2,1)S(1)}, u32[]{:S(2)}, u32[]{:S(2)}) async-start(bf16[32,128,256]{2,1,0:T(8,128)(2,1)} %bitcast.53), calls=%async_computation.2 | async-start | bytes 4194304 | tf_op jit(solution)/shard_map/all_to_all | solution.py:40
  63.8 0.3 mul.60
  64.2 1.3 copy-done.2
  65.5 0.5 copy-done.5
  66.0 2.4 fusion
  68.5 72.5 %reduce-scatter.2.cloned.1.call-done = f32[32,256]{1,0:T(8,128)} async-done(((f32[32,4096]{1,0:T(8,128)}), f32[32,256]{1,0:T(8,128)}) %reduce-scatter.2.cloned.1.call-update) | async-done | bytes 32784 | tf_op jit(solution)/shard_map/reduce_scatter | solution.py:26
  141.0 0.8 convert_element_type.28
  141.7 24.4 %all_gather.6 = bf16[1024,256]{1,0:T(8,128)(2,1)S(1)} all-gather(bf16[32,256]{1,0:T(8,128)(2,1)S(1)} %convert_element_type.28), channel_id=1, replica_groups=mesh['dp'=32,'wide'=16] {'dp'}, dimensions={0}, use_global_device_ids=true | all-gather | bytes 540672 | tf_op jit(solution)/shard_map/all_gather | solution.py:27
  166.1 1.3 fusion.15
  167.4 2.0 copy.26
  169.5 9.0 %gather_fusion.1 = bf16[2048,256]{1,0:T(8,128)(2,1)} fusion(bf16[4096,256]{1,0:T(8,128)(2,1)S(1)} %bitcast.50, s32[2048]{0:T(1024)S(1)} %broadcast_clamp_fusion.1), kind=kCustom, calls=%fused_computation.1 | custom fusion | bytes 2105344 | tf_op jit(solution)/shard_map/gather | solution.py:41
  178.5 1.4 reshape.188
  179.9 0.6 multiply_reduce_fusion
  180.6 28.9 %psum.7 = f32[512,4]{0,1:T(4,128)S(1)} all-reduce(f32[512,4]{0,1:T(4,128)S(1)} %copy.21), channel_id=1, replica_groups=mesh['dp'=32,'wide'=16] {'wide'}, use_global_device_ids=true, to_apply=%region_5.6 | all-reduce | flops 2048 | bytes 16384 | tf_op jit(solution)/shard_map/psum | solution.py:46
  209.6 0.9 copy.22
  210.5 2.1 fusion.16
  212.6 0.7 fusion.1
  213.4 0.8 copy.16
  214.2 0.6 compare_select_fusion.2
  214.9 91.9 %all-gather.2.cloned.1.call-done = bf16[512,4096]{1,0:T(8,128)(2,1)} async-done(((bf16[512,256]{1,0:T(8,128)(2,1)}), bf16[512,4096]{1,0:T(8,128)(2,1)}) %all-gather.2.cloned.1.call-update) | async-done | bytes 4194320 | tf_op jit(solution)/shard_map/all_gather | solution.py:51
  306.7 4.9 %convolution_convert_fusion = bf16[512,256]{1,0:T(8,128)(2,1)} fusion(bf16[512,4096]{1,0:T(8,128)(2,1)} %all-gather.2.cloned.1.call-done, bf16[256,4096]{1,0:T(8,128)(2,1)} %param.9, bf16[32,8,32,128]{3,2,1,0:T(8,128)(2,1)S(1)} %bitcast.52), kind=kOutput, calls=%fused_computation.6 | convolution fusion | flops 1074921472 | bytes 8650752 | tf_op jit(solution)/shard_map/dot_general | solution.py:52
  (33 shorter events, 0.7 us)
Async XLA Ops:
  7.2 159.0 %copy-start = (bf16[512,1024]{1,0:T(8,128)(2,1)S(1)}, bf16[512,1024]{1,0:T(8,128)(2,1)}, u32[]{:S(2)}) copy-start(bf16[512,1024]{1,0:T(8,128)(2,1)} %param.7) | copy-start | bytes 3145732
  7.2 33.7 %copy-start.1 = (bf16[512,256]{1,0:T(8,128)(2,1)S(1)}, bf16[512,256]{1,0:T(8,128)(2,1)}, u32[]{:S(2)}) copy-start(bf16[512,256]{1,0:T(8,128)(2,1)} %param.11) | copy-start | bytes 786436
  57.8 6.0 %copy-start.8 = (s32[2,32]{1,0:T(2,128)S(1)}, s32[2,32]{1,0:T(2,128)}, u32[]{:S(2)}) copy-start(s32[2,32]{1,0:T(2,128)} %param.10) | copy-start | bytes 772
  57.8 111.6 %all-to-all-start.1 = ((bf16[32,128,256]{2,1,0:T(8,128)(2,1)}), bf16[32,128,256]{2,1,0:T(8,128)(2,1)S(1)}, u32[]{:S(2)}, u32[]{:S(2)}) async-start(bf16[32,128,256]{2,1,0:T(8,128)(2,1)} %bitcast.53), calls=%async_computation.2 | async-start | bytes 4194304 | tf_op jit(solution)/shard_map/all_to_all | solution.py:40
  63.7 77.3 %reduce-scatter.2.cloned.1.call-start = ((), (), s32[]{:S(2)}) async-start(), calls=%async_computation.3 | async-start | bytes 557056 | tf_op jit(solution)/shard_map/reduce_scatter | solution.py:26
  63.8 2.2 copy-start.5
  64.2 1.3 copy-start.2
  68.4 238.3 %all-gather.2.cloned.1.call-start = ((), (), s32[]{:S(2)}) async-start(), calls=%async_computation.4 | async-start | bytes 4456448 | tf_op jit(solution)/shard_map/all_gather | solution.py:51
  178.5 1.4 copy-start.6
  178.5 31.1 %copy-start.7 = (s32[512,4]{0,1:T(4,128)S(1)}, s32[512,4]{0,1:T(4,128)}, u32[]{:S(2)}) copy-start(s32[512,4]{0,1:T(4,128)} %param.13) | copy-start | bytes 24580
  179.9 29.7 %copy-start.4 = (bf16[512,4,256]{2,1,0:T(4,128)(2,1)}, bf16[512,4,256]{2,1,0:T(4,128)(2,1)S(1)}, u32[]{:S(2)}) copy-start(bf16[512,4,256]{2,1,0:T(4,128)(2,1)S(1)} %reshape.188) | copy-start | bytes 3145732
  210.5 96.3 %copy-start.3 = (bf16[2,128,32,128]{3,2,1,0:T(8,128)(2,1)S(1)}, bf16[2,128,32,128]{3,2,1,0:T(8,128)(2,1)}, u32[]{:S(2)}) copy-start(bf16[2,128,32,128]{3,2,1,0:T(8,128)(2,1)} %copy-done.2) | copy-start | bytes 6291460
Sparse Core Ops, SparseCore 0:
  68.6 72.3 reduce-scatter.1
  213.5 93.1 all-gather.1

commit v2 on v0

--- a/solution.py
+++ b/solution.py
@@ -7,14 +7,24 @@
 
 E = 4096
 K = 4
+CAP = 128
 
 
-def local(trunk_out, projection, transform, block_mask, old_index, doc_ids, labels):
+def one_hot(index, size, dtype=jnp.bfloat16):
+    return (index[:, None] == jnp.arange(size, dtype=jnp.int32)[None, :]).astype(dtype)
+
+
+def pick_rows(index, table):
+    picked = jnp.dot(one_hot(index, table.shape[0]), table, preferred_element_type=jnp.float32)
+    return picked.astype(table.dtype)
+
+
+def local(n_dp, n_wide, trunk_out, projection, transform, block_mask, old_index, doc_ids, labels):
     rows = trunk_out.shape[0]
-    e_local = transform.shape[0]
-    width = transform.shape[1]
+    e_local, width = transform.shape
     local_blocks, nblocks = block_mask.shape
     side = e_local // local_blocks
+    doc_shard = old_index.shape[0]
     query = jnp.dot(trunk_out, projection, preferred_element_type=jnp.float32).astype(jnp.bfloat16)
     blocks = transform.reshape(local_blocks, side, nblocks, side)
     masked = (blocks * block_mask[:, None, :, None].astype(jnp.bfloat16)).reshape(e_local, width)
@@ -22,13 +32,33 @@
     new = lax.psum_scatter(
         term.astype(jnp.bfloat16), "wide", scatter_dimension=1, tiled=True
     ).astype(jnp.float32)
+
     flat = doc_ids.reshape(-1)
-    whole = lax.all_gather(old_index, "dp", axis=0, tiled=True)
-    old_vec = whole[flat].reshape(rows, K, e_local)
+    count = flat.shape[0]
+    owner = flat // doc_shard
+    loc = flat - owner * doc_shard
+    by_owner = one_hot(owner, n_dp)
+    ids = jnp.arange(count, dtype=jnp.int32)
+    earlier = (ids[None, :] < ids[:, None]).astype(jnp.bfloat16)
+    before = jnp.dot(earlier, by_owner, preferred_element_type=jnp.float32)
+    rank = jnp.sum(before * by_owner.astype(jnp.float32), axis=1).astype(jnp.int32)
+    slot = owner * CAP + rank
+    by_rank = one_hot(rank, CAP)
+    digits = jnp.stack([loc // 32, loc % 32], axis=0).astype(jnp.bfloat16)
+    placed = jnp.einsum("di,io,ic->doc", digits, by_owner, by_rank,
+                        preferred_element_type=jnp.float32).astype(jnp.int32)
+    req = placed[0] * 32 + placed[1]
+    asked = lax.all_to_all(req, "dp", 0, 0, tiled=True)
+    served = pick_rows(asked.reshape(-1), old_index).reshape(n_dp, CAP, e_local)
+    back = lax.all_to_all(served, "dp", 0, 0, tiled=True).reshape(n_dp * CAP, e_local)
+    old_vec = pick_rows(slot, back).reshape(rows, K, e_local)
+
     old_wide = old_vec.astype(jnp.float32)
     scale = 1.0 / math.sqrt(E)
     partial_scores = jnp.einsum("re,rke->rk", new, old_wide)
-    score = lax.psum(partial_scores, "wide") * scale
+    spread = jnp.broadcast_to(partial_scores[None], (n_wide,) + partial_scores.shape)
+    gathered = lax.all_to_all(spread, "wide", 0, 0, tiled=True)
+    score = jnp.sum(gathered, axis=0) * scale
     sign = 2.0 * labels.astype(jnp.float32) - 1.0
     pair_loss = jax.nn.softplus(-sign * score)
     dscore = -sign * jax.nn.sigmoid(-sign * score)
@@ -41,8 +71,9 @@
 
 
 def solution(mesh):
+    n_dp, n_wide = mesh.shape["dp"], mesh.shape["wide"]
     return jax.shard_map(
-        local,
+        lambda *a: local(n_dp, n_wide, *a),
         mesh=mesh,
         in_specs=(
             P("dp", None),

time: 241 us -> 227 us (0.942)
  waiting for transfers between devices: 160 us -> 134 us
  matrix products: 14.6 us -> 28.6 us
  local copies, waits for them, and re-layouts: 16.8 us -> 4.09 us
  starting transfers between devices: 0.13 us -> 6.7 us
  blocking collectives: 31.7 us -> 35.7 us
    all_gather x1 -> x0, waiting for transfers between devices: 67.9 us -> none  [local(): whole = lax.all_gather(old_index, 'dp', axis=0, tiled=True)]
    all_to_all x0 -> x2, blocking collectives: none -> 35.7 us  [the longest x1 21.6 us: local(): gathered = lax.all_to_all(spread, 'wide', 0, 0, tiled=True)]
    psum x1 -> x0, blocking collectives: 31.7 us -> none  [local(): score = lax.psum(partial_scores, 'wide') * scale]
    all_to_all x0 -> x1, waiting for transfers between devices: none -> 25.4 us  [local(): lax.all_to_all(served, 'dp', 0, 0, tiled=True).reshape(n_dp * CAP, e_local)]
    reduce_scatter x1, waiting for transfers between devices: 0.13 us -> 20.2 us  [local(): lax.psum_scatter(term.astype(jnp.bfloat16), 'wide', scatter_dimension=1,...]
    dot_general x0 -> x4, matrix products: none -> 14 us  [the longest x2 12.1 us: pick_rows(): jnp.dot(one_hot(index, table.shape[0]), table, preferred_element_type=jnp...]
    gather x1 -> x0, local copies, waits for them, and re-layouts: 13 us -> none  [local(): old_vec = whole[flat].reshape(rows, K, e_local)]
    all_to_all x0 -> x1, starting transfers between devices: none -> 6.44 us  [local(): lax.all_to_all(served, 'dp', 0, 0, tiled=True).reshape(n_dp * CAP, e_local)]
  transfers between devices with their start and end apart: 3 -> 3, of which waited for: 3 -> 3; matrix products, arithmetic and copies ran while one was open for 10% -> 8% of each run, Pallas kernels for 0% -> 0%
where the time goes in v2:
time: 227 us; the launch traced here: 226 us
  waiting for transfers between devices  134 us (59%)
  blocking collectives  35.7 us (16%)
  matrix products  28.6 us (13%)
  between operations  14.2 us (6%)
  starting transfers between devices  6.7 us (3%)
  local copies, waits for them, and re-layouts  4.09 us (2%)
  other arithmetic  2.38 us (1%)
    all_gather x1, waiting for transfers between devices, local(): grad_full = lax.all_gather(grad_local, 'wide', axis=1, tiled=True)  88.7 us
    all_to_all x1, waiting for transfers between devices, local(): lax.all_to_all(served, 'dp', 0, 0, tiled=True).reshape(n_dp * CAP, e_local)  25.4 us
    all_to_all x1, blocking collectives, local(): gathered = lax.all_to_all(spread, 'wide', 0, 0, tiled=True)  21.6 us
    reduce_scatter x1, waiting for transfers between devices, local(): lax.psum_scatter(term.astype(jnp.bfloat16), 'wide', scatter_dimension=1,...  20.2 us
    all_to_all x1, blocking collectives, local(): asked = lax.all_to_all(req, 'dp', 0, 0, tiled=True)  14.1 us
    dot_general x2, matrix products, pick_rows(): jnp.dot(one_hot(index, table.shape[0]), table, preferred_element_type=jnp...  12.1 us
    all_to_all x1, starting transfers between devices, local(): lax.all_to_all(served, 'dp', 0, 0, tiled=True).reshape(n_dp * CAP, e_local)  6.44 us
    dot_general x1, matrix products, local(): term = jnp.dot(query, masked, preferred_element_type=jnp.float32)  5.79 us
  transfers between devices with their start and end apart: 3, of which 3 were waited for; matrix products, arithmetic and copies ran while one was open for 8% of the time, Pallas kernels for 0%

profile of v2, /device:TPU:6, one launch (start us, length us, event | category | flops | bytes accessed | tf_op | source)
XLA Modules:
  0.0 226.0 jit_solution(8037420799444914392)
XLA Ops:
  7.2 0.0 copy-start
  7.2 0.0 reduce-scatter.2.cloned.1.call-start
  7.2 0.8 convert_element_type.56
  8.0 0.3 mul.78
  8.3 0.1 copy-done
  8.4 5.8 %convolution_convert_fusion = bf16[512,4096]{1,0:T(8,128)(2,1)} fusion(bf16[512,1024]{1,0:T(8,128)(2,1)S(1)} %copy-done, bf16[1024,256]{1,0:T(8,128)(2,1)} %param.8, bf16[256,4096]{1,0:T(8,128)(2,1)} %param.9, bf16[32,8,32,128]{3,2,1,0:T(8,128)(2,1)S(1)} %bitcast.35), kind=kOutput, calls=%fused_computation.7 | convolution fusion | flops 1345454080 | bytes 9961472 | tf_op jit(solution)/shard_map/dot_general | solution.py:31
  14.2 0.0 reduce-scatter.2.cloned.1.call-update
  14.2 0.7 copy-done.2
  14.9 0.1 copy.12
  15.1 0.2 reshape.259
  15.2 0.2 reshape.260
  15.4 1.5 fusion.8
  16.9 0.1 fusion.26
  17.1 0.5 fusion.9
  17.6 14.1 %all_to_all.16 = s32[32,1,128]{2,1,0:T(1,128)S(1)} all-to-all(s32[32,1,128]{2,1,0:T(1,128)S(1)} %bitcast.38), channel_id=1, replica_groups=mesh['dp'=32,'wide'=16] {'dp'}, dimensions={0} | all-to-all | bytes 32768 | tf_op jit(solution)/shard_map/all_to_all | solution.py:51
  31.7 3.3 %fusion.4 = bf16[4096,256]{1,0:T(8,128)(2,1)} fusion(bf16[512,256]{1,0:T(8,128)(2,1)S(1)} %copy-done.3, s32[4096]{0:T(1024)S(1)} %bitcast.40), kind=kOutput, calls=%fused_computation.8 | convolution fusion | flops 1076887552 | bytes 2375680 | tf_op jit(solution)/shard_map/dot_general | solution.py:18
  35.0 6.4 %all-to-all-start.1 = ((bf16[32,128,256]{2,1,0:T(8,128)(2,1)}), bf16[32,128,256]{2,1,0:T(8,128)(2,1)}, u32[]{:S(2)}, u32[]{:S(2)}) async-start(bf16[32,128,256]{2,1,0:T(8,128)(2,1)} %bitcast.37), calls=%async_computation.2 | async-start | bytes 4194304 | tf_op jit(solution)/shard_map/all_to_all | solution.py:53
  41.5 0.2 all-gather.2.cloned.1.call-start
  41.7 25.4 %all-to-all-done.1 = bf16[32,128,256]{2,1,0:T(8,128)(2,1)} async-done(((bf16[32,128,256]{2,1,0:T(8,128)(2,1)}), bf16[32,128,256]{2,1,0:T(8,128)(2,1)}, u32[]{:S(2)}, u32[]{:S(2)}) %all-to-all-start.1) | async-done | bytes 2097184 | tf_op jit(solution)/shard_map/all_to_all | solution.py:53
  67.1 8.8 %fusion.6 = bf16[2048,256]{1,0:T(8,128)(2,1)} fusion(bf16[4096,256]{1,0:T(8,128)(2,1)} %bitcast.8, s32[2048]{0:T(1024)S(1)} %multiply_add_fusion), kind=kOutput, calls=%fused_computation.10 | convolution fusion | flops 4303880192 | bytes 3153920 | tf_op jit(solution)/shard_map/dot_general | solution.py:18
  75.9 2.2 reshape.263
  78.1 20.2 %reduce-scatter.2.cloned.1.call-done = bf16[512,256]{1,0:T(8,128)(2,1)} async-done(((bf16[512,4096]{1,0:T(8,128)(2,1)}), bf16[512,256]{1,0:T(8,128)(2,1)}) %reduce-scatter.2.cloned.1.call-update) | async-done | bytes 262160 | tf_op jit(solution)/shard_map/reduce_scatter | solution.py:32
  98.3 2.0 fusion.15
  100.3 0.1 copy.16
  100.5 21.6 %all_to_all.17 = f32[16,512,4]{1,2,0:T(4,128)S(1)} all-to-all(f32[16,512,4]{1,2,0:T(4,128)S(1)} %broadcast_in_dim.2), channel_id=1, replica_groups=mesh['dp'=32,'wide'=16] {'wide'}, dimensions={0} | all-to-all | bytes 262144 | tf_op jit(solution)/shard_map/all_to_all | solution.py:60
  122.1 0.2 copy.17
  122.3 1.9 fusion.27
  124.2 0.7 fusion.12
  125.0 0.0 all-gather.2.cloned.1.call-update
  125.0 0.6 compare_select_fusion
  125.6 88.7 %all-gather.2.cloned.1.call-done = bf16[512,4096]{1,0:T(8,128)(2,1)} async-done(((bf16[512,256]{1,0:T(8,128)(2,1)}), bf16[512,4096]{1,0:T(8,128)(2,1)}) %all-gather.2.cloned.1.call-update) | async-done | bytes 4194320 | tf_op jit(solution)/shard_map/all_gather | solution.py:66
  214.3 4.9 %convolution_convert_fusion.1 = bf16[512,256]{1,0:T(8,128)(2,1)} fusion(bf16[512,4096]{1,0:T(8,128)(2,1)} %all-gather.2.cloned.1.call-done, bf16[256,4096]{1,0:T(8,128)(2,1)} %param.9, bf16[32,8,32,128]{3,2,1,0:T(8,128)(2,1)S(1)} %bitcast.36), kind=kOutput, calls=%fused_computation.13 | convolution fusion | flops 1074921472 | bytes 8650752 | tf_op jit(solution)/shard_map/dot_general | solution.py:67
  (15 shorter events, 0.2 us)
Async XLA Ops:
  7.2 1.2 copy-start
  7.2 91.1 %reduce-scatter.2.cloned.1.call-start = ((), (), s32[]{:S(2)}) async-start(), calls=%async_computation.4 | async-start | bytes 4456448 | tf_op jit(solution)/shard_map/reduce_scatter | solution.py:32
  14.2 0.7 copy-start.2
  15.4 16.3 %copy-start.3 = (bf16[512,256]{1,0:T(8,128)(2,1)S(1)}, bf16[512,256]{1,0:T(8,128)(2,1)}, u32[]{:S(2)}) copy-start(bf16[512,256]{1,0:T(8,128)(2,1)} %param.11) | copy-start | bytes 786436
  35.0 32.1 %all-to-all-start.1 = ((bf16[32,128,256]{2,1,0:T(8,128)(2,1)}), bf16[32,128,256]{2,1,0:T(8,128)(2,1)}, u32[]{:S(2)}, u32[]{:S(2)}) async-start(bf16[32,128,256]{2,1,0:T(8,128)(2,1)} %bitcast.37), calls=%async_computation.2 | async-start | bytes 4194304 | tf_op jit(solution)/shard_map/all_to_all | solution.py:53
  41.5 172.8 %all-gather.2.cloned.1.call-start = ((), (), s32[]{:S(2)}) async-start(), calls=%async_computation.5 | async-start | bytes 4456448 | tf_op jit(solution)/shard_map/all_gather | solution.py:66
  98.3 23.8 %copy-start.1 = (s32[512,4]{0,1:T(4,128)S(1)}, s32[512,4]{0,1:T(4,128)}, u32[]{:S(2)}) copy-start(s32[512,4]{0,1:T(4,128)} %param.13) | copy-start | bytes 24580
Sparse Core Ops, SparseCore 0:
  14.4 83.9 reduce-scatter.1
  125.1 89.1 all-gather.1

commit v3 on v2

--- a/solution.py
+++ b/solution.py
@@ -48,10 +48,18 @@
     placed = jnp.einsum("di,io,ic->doc", digits, by_owner, by_rank,
                         preferred_element_type=jnp.float32).astype(jnp.int32)
     req = placed[0] * 32 + placed[1]
-    asked = lax.all_to_all(req, "dp", 0, 0, tiled=True)
-    served = pick_rows(asked.reshape(-1), old_index).reshape(n_dp, CAP, e_local)
+    asked = lax.all_to_all(req, "dp", 0, 0, tiled=True).reshape(-1)
+    served = pick_rows(asked, old_index).reshape(n_dp, CAP, e_local)
     back = lax.all_to_all(served, "dp", 0, 0, tiled=True).reshape(n_dp * CAP, e_local)
     old_vec = pick_rows(slot, back).reshape(rows, K, e_local)
+
+    old_full = lax.all_gather(old_index, "wide", axis=1, tiled=True)
+    g_own = lax.dot_general(
+        old_full, masked, (((1,), (1,)), ((), ())), preferred_element_type=jnp.float32
+    ).astype(jnp.bfloat16)
+    served_g = pick_rows(asked, g_own).reshape(n_dp, CAP, e_local)
+    back_g = lax.all_to_all(served_g, "dp", 0, 0, tiled=True).reshape(n_dp * CAP, e_local)
+    g_vec = pick_rows(slot, back_g).reshape(rows, K, e_local).astype(jnp.float32)
 
     old_wide = old_vec.astype(jnp.float32)
     scale = 1.0 / math.sqrt(E)
@@ -62,11 +70,7 @@
     sign = 2.0 * labels.astype(jnp.float32) - 1.0
     pair_loss = jax.nn.softplus(-sign * score)
     dscore = -sign * jax.nn.sigmoid(-sign * score)
-    grad_local = (jnp.einsum("rk,rke->re", dscore, old_wide) * scale).astype(jnp.bfloat16)
-    grad_full = lax.all_gather(grad_local, "wide", axis=1, tiled=True)
-    trunk_grad = lax.dot_general(
-        grad_full, masked, (((1,), (1,)), ((), ())), preferred_element_type=jnp.float32
-    )
+    trunk_grad = jnp.einsum("rk,rke->re", dscore, g_vec) * scale
     return (new.astype(jnp.bfloat16), pair_loss, trunk_grad.astype(jnp.bfloat16))
 
 

time: 227 us -> 256 us (1.13); the launches traced: 226 us -> 252 us
  waiting for transfers between devices: 134 us -> 156 us
  blocking collectives: 35.7 us -> 14.1 us
  starting transfers between devices: 6.7 us -> 22.9 us
  matrix products: 28.6 us -> 37 us
    all_to_all x0 -> x2, waiting for transfers between devices: none -> 24.7 us  [the longest x1 24.7 us: local(): lax.all_to_all(served_g, 'dp', 0, 0, tiled=True)]
    all_to_all x2 -> x1, blocking collectives: 35.7 us -> 14.1 us  [local(): asked = lax.all_to_all(req, 'dp', 0, 0, tiled=True).reshape(-1)]
    all_to_all x0 -> x2, starting transfers between devices: none -> 16.3 us  [the longest x1 8.42 us: local(): gathered = lax.all_to_all(spread, 'wide', 0, 0, tiled=True)]
    dot_general x2 -> x4, matrix products: 12.1 us -> 26.5 us  [pick_rows(): jnp.dot(one_hot(index, table.shape[0]), table, preferred_element_type=jnp...]
    dot_general x2 -> x1, matrix products: 6.81 us -> 0.69 us  [local(): trunk_grad = jnp.einsum('rk,rke->re', dscore, g_vec) * scale]
    all_gather x1, waiting for transfers between devices: 88.7 us -> 84.5 us  [local(): old_full = lax.all_gather(old_index, 'wide', axis=1, tiled=True)]
  transfers between devices with their start and end apart: 3 -> 5, of which waited for: 3 -> 4; matrix products, arithmetic and copies ran while one was open for 8% -> 11% of each run, Pallas kernels for 0% -> 0%
where the time goes in v3:
time: 256 us; the launch traced here: 252 us
  waiting for transfers between devices  156 us (61%)
  matrix products  37 us (14%)
  starting transfers between devices  22.9 us (9%)
  between operations  14.2 us (6%)
  blocking collectives  14.1 us (6%)
  local copies, waits for them, and re-layouts  5.51 us (2%)
    all_gather x1, waiting for transfers between devices, local(): old_full = lax.all_gather(old_index, 'wide', axis=1, tiled=True)  84.5 us
    dot_general x4, matrix products, pick_rows(): jnp.dot(one_hot(index, table.shape[0]), table, preferred_element_type=jnp...  26.5 us
    all_to_all x1, waiting for transfers between devices, local(): lax.all_to_all(served, 'dp', 0, 0, tiled=True).reshape(n_dp * CAP, e_local)  25.6 us
    all_to_all x1, waiting for transfers between devices, local(): lax.all_to_all(served_g, 'dp', 0, 0, tiled=True)  24.7 us
    reduce_scatter x1, waiting for transfers between devices, local(): lax.psum_scatter(term.astype(jnp.bfloat16), 'wide', scatter_dimension=1,...  20.1 us
    all_to_all x1, blocking collectives, local(): asked = lax.all_to_all(req, 'dp', 0, 0, tiled=True).reshape(-1)  14.1 us
    all_to_all x1, starting transfers between devices, local(): gathered = lax.all_to_all(spread, 'wide', 0, 0, tiled=True)  8.42 us
    all_to_all x1, starting transfers between devices, local(): lax.all_to_all(served_g, 'dp', 0, 0, tiled=True)  7.91 us
  transfers between devices with their start and end apart: 5, of which 4 were waited for; matrix products, arithmetic and copies ran while one was open for 11% of the time, Pallas kernels for 0%

profile of v3, /device:TPU:6, one launch (start us, length us, event | category | flops | bytes accessed | tf_op | source)
XLA Modules:
  0.0 251.7 jit_solution(3416995019528271138)
XLA Ops:
  7.2 0.8 convert_element_type.66
  8.0 0.3 mul.78
  8.3 0.1 copy-done
  8.4 5.8 %convolution_convert_fusion = bf16[512,4096]{1,0:T(8,128)(2,1)} fusion(bf16[512,1024]{1,0:T(8,128)(2,1)S(1)} %copy-done, bf16[1024,256]{1,0:T(8,128)(2,1)} %param.8, bf16[256,4096]{1,0:T(8,128)(2,1)} %param.9, bf16[32,8,32,128]{3,2,1,0:T(8,128)(2,1)S(1)} %bitcast.39), kind=kOutput, calls=%fused_computation.10 | convolution fusion | flops 1345454080 | bytes 9961472 | tf_op jit(solution)/shard_map/dot_general | solution.py:31
  14.3 0.7 all-gather.2.cloned.1.call-update
  15.0 0.1 copy.12
  15.2 0.2 reshape.268
  15.3 0.2 reshape.269
  15.6 1.5 fusion.14
  17.1 0.1 fusion.32
  17.2 0.5 fusion.15
  17.7 14.1 %all_to_all.21 = s32[32,1,128]{2,1,0:T(1,128)S(1)} all-to-all(s32[32,1,128]{2,1,0:T(1,128)S(1)} %bitcast.44), channel_id=1, replica_groups=mesh['dp'=32,'wide'=16] {'dp'}, dimensions={0} | all-to-all | bytes 32768 | tf_op jit(solution)/shard_map/all_to_all | solution.py:51
  31.9 3.2 %fusion.7 = bf16[4096,256]{1,0:T(8,128)(2,1)} fusion(bf16[512,256]{1,0:T(8,128)(2,1)S(1)} %copy-done.1, s32[4096]{0:T(1024)S(1)} %bitcast.46), kind=kOutput, calls=%fused_computation.11 | convolution fusion | flops 1076887552 | bytes 2375680 | tf_op jit(solution)/shard_map/dot_general | solution.py:18
  35.1 6.5 %all-to-all-start.1 = ((bf16[32,128,256]{2,1,0:T(8,128)(2,1)}), bf16[32,128,256]{2,1,0:T(8,128)(2,1)}, u32[]{:S(2)}, u32[]{:S(2)}) async-start(bf16[32,128,256]{2,1,0:T(8,128)(2,1)} %bitcast.43), calls=%async_computation.2 | async-start | bytes 4194304 | tf_op jit(solution)/shard_map/all_to_all | solution.py:53
  41.6 25.6 %all-to-all-done.1 = bf16[32,128,256]{2,1,0:T(8,128)(2,1)} async-done(((bf16[32,128,256]{2,1,0:T(8,128)(2,1)}), bf16[32,128,256]{2,1,0:T(8,128)(2,1)}, u32[]{:S(2)}, u32[]{:S(2)}) %all-to-all-start.1) | async-done | bytes 2097184 | tf_op jit(solution)/shard_map/all_to_all | solution.py:53
  67.2 8.8 %fusion.11 = bf16[2048,256]{1,0:T(8,128)(2,1)} fusion(bf16[4096,256]{1,0:T(8,128)(2,1)} %bitcast.8, s32[2048]{0:T(1024)S(1)} %multiply_add_fusion), kind=kOutput, calls=%fused_computation.15 | convolution fusion | flops 4303880192 | bytes 3153920 | tf_op jit(solution)/shard_map/dot_general | solution.py:18
  76.0 2.2 reshape.272
  78.3 20.1 %reduce-scatter.2.cloned.1.call-done = bf16[512,256]{1,0:T(8,128)(2,1)} async-done(((bf16[512,4096]{1,0:T(8,128)(2,1)}), bf16[512,256]{1,0:T(8,128)(2,1)}) %reduce-scatter.2.cloned.1.call-update) | async-done | bytes 262160 | tf_op jit(solution)/shard_map/reduce_scatter | solution.py:32
  98.4 2.0 fusion.21
  100.4 0.1 copy.16
  100.5 0.7 broadcast_in_dim.2
  101.2 8.4 %all-to-all-start.2 = ((f32[16,512,4]{1,2,0:T(4,128)}), f32[16,512,4]{1,2,0:T(4,128)S(1)}, u32[]{:S(2)}, u32[]{:S(2)}) async-start(f32[16,512,4]{1,2,0:T(4,128)} %broadcast_in_dim.2), calls=%async_computation.3 | async-start | bytes 262144 | tf_op jit(solution)/shard_map/all_to_all | solution.py:68
  109.6 84.5 %all-gather.2.cloned.1.call-done = bf16[512,4096]{1,0:T(8,128)(2,1)} async-done(((bf16[512,256]{1,0:T(8,128)(2,1)}), bf16[512,4096]{1,0:T(8,128)(2,1)}) %all-gather.2.cloned.1.call-update) | async-done | bytes 4194320 | tf_op jit(solution)/shard_map/all_gather | solution.py:56
  194.1 7.3 %fusion.8 = bf16[4096,256]{1,0:T(8,128)(2,1)} fusion(s32[4096]{0:T(1024)S(1)} %bitcast.47, bf16[512,4096]{1,0:T(8,128)(2,1)} %all-gather.2.cloned.1.call-done, bf16[256,4096]{1,0:T(8,128)(2,1)} %param.9, bf16[32,8,32,128]{3,2,1,0:T(8,128)(2,1)S(1)} %bitcast.40), kind=kOutput, calls=%fused_computation.12 | convolution fusion | flops 2151809024 | bytes 10502144 | tf_op jit(solution)/shard_map/dot_general | solution.py:18
  201.4 7.9 %all-to-all-start.3 = ((bf16[32,128,256]{2,1,0:T(8,128)(2,1)}), bf16[32,128,256]{2,1,0:T(8,128)(2,1)S(1)}, u32[]{:S(2)}, u32[]{:S(2)}) async-start(bf16[32,128,256]{2,1,0:T(8,128)(2,1)} %bitcast.41), calls=%async_computation.4 | async-start | bytes 4194304 | tf_op jit(solution)/shard_map/all_to_all | solution.py:61
  209.4 0.2 copy.17
  209.6 0.6 compare_select_fusion
  210.2 24.7 %all-to-all-done.3 = bf16[32,128,256]{2,1,0:T(8,128)(2,1)S(1)} async-done(((bf16[32,128,256]{2,1,0:T(8,128)(2,1)}), bf16[32,128,256]{2,1,0:T(8,128)(2,1)S(1)}, u32[]{:S(2)}, u32[]{:S(2)}) %all-to-all-start.3) | async-done | bytes 2097184 | tf_op jit(solution)/shard_map/all_to_all | solution.py:61
  234.9 7.2 %fusion.12 = bf16[2048,256]{1,0:T(8,128)(2,1)} fusion(bf16[4096,256]{1,0:T(8,128)(2,1)S(1)} %bitcast.42, s32[2048]{0:T(1024)S(1)} %multiply_add_fusion), kind=kOutput, calls=%fused_computation.16 | convolution fusion | flops 4303880192 | bytes 3153920 | tf_op jit(solution)/shard_map/dot_general | solution.py:18
  242.1 1.3 reshape.275
  243.4 0.7 fusion.33
  244.1 0.7 fusion.18
  (24 shorter events, 0.3 us)
Async XLA Ops:
  7.2 1.2 copy-start
  7.2 91.2 %reduce-scatter.2.cloned.1.call-start = ((), (), s32[]{:S(2)}) async-start(), calls=%async_computation.5 | async-start | bytes 4456448 | tf_op jit(solution)/shard_map/reduce_scatter | solution.py:32
  14.2 0.8 copy-start.5
  14.3 179.8 %all-gather.2.cloned.1.call-start = ((), (), s32[]{:S(2)}) async-start(), calls=%async_computation.6 | async-start | bytes 4456448 | tf_op jit(solution)/shard_map/all_gather | solution.py:56
  15.5 16.3 %copy-start.1 = (bf16[512,256]{1,0:T(8,128)(2,1)S(1)}, bf16[512,256]{1,0:T(8,128)(2,1)}, u32[]{:S(2)}) copy-start(bf16[512,256]{1,0:T(8,128)(2,1)} %param.11) | copy-start | bytes 786436
  31.9 3.2 %copy-start.3 = (s32[32,1,128]{2,1,0:T(1,128)}, s32[32,1,128]{2,1,0:T(1,128)S(1)}, u32[]{:S(2)}) copy-start(s32[32,1,128]{2,1,0:T(1,128)S(1)} %all_to_all.21) | copy-start | bytes 49156
  35.1 32.1 %all-to-all-start.1 = ((bf16[32,128,256]{2,1,0:T(8,128)(2,1)}), bf16[32,128,256]{2,1,0:T(8,128)(2,1)}, u32[]{:S(2)}, u32[]{:S(2)}) async-start(bf16[32,128,256]{2,1,0:T(8,128)(2,1)} %bitcast.43), calls=%async_computation.2 | async-start | bytes 4194304 | tf_op jit(solution)/shard_map/all_to_all | solution.py:53
  98.4 95.8 %copy-start.4 = (s32[32,1,128]{2,1,0:T(1,128)S(1)}, s32[32,1,128]{2,1,0:T(1,128)}, u32[]{:S(2)}) copy-start(s32[32,1,128]{2,1,0:T(1,128)} %copy-done.3) | copy-start | bytes 49156
  101.2 100.2 %all-to-all-start.2 = ((f32[16,512,4]{1,2,0:T(4,128)}), f32[16,512,4]{1,2,0:T(4,128)S(1)}, u32[]{:S(2)}, u32[]{:S(2)}) async-start(f32[16,512,4]{1,2,0:T(4,128)} %broadcast_in_dim.2), calls=%async_computation.3 | async-start | bytes 262144 | tf_op jit(solution)/shard_map/all_to_all | solution.py:68
  201.4 8.0 %copy-start.2 = (s32[512,4]{0,1:T(4,128)S(1)}, s32[512,4]{0,1:T(4,128)}, u32[]{:S(2)}) copy-start(s32[512,4]{0,1:T(4,128)} %param.13) | copy-start | bytes 24580
  201.4 33.5 %all-to-all-start.3 = ((bf16[32,128,256]{2,1,0:T(8,128)(2,1)}), bf16[32,128,256]{2,1,0:T(8,128)(2,1)S(1)}, u32[]{:S(2)}, u32[]{:S(2)}) async-start(bf16[32,128,256]{2,1,0:T(8,128)(2,1)} %bitcast.41), calls=%async_computation.4 | async-start | bytes 4194304 | tf_op jit(solution)/shard_map/all_to_all | solution.py:61
Sparse Core Ops, SparseCore 0:
  14.4 83.9 reduce-scatter.1
  100.4 93.6 all-gather.1

commit v4 on v3

--- a/solution.py
+++ b/solution.py
@@ -53,7 +53,21 @@
     back = lax.all_to_all(served, "dp", 0, 0, tiled=True).reshape(n_dp * CAP, e_local)
     old_vec = pick_rows(slot, back).reshape(rows, K, e_local)
 
-    old_full = lax.all_gather(old_index, "wide", axis=1, tiled=True)
+    me_w = lax.axis_index("wide")
+    right = [(i, (i + 1) % n_wide) for i in range(n_wide)]
+    left = [(i, (i - 1) % n_wide) for i in range(n_wide)]
+
+    def place(full, block, source):
+        return lax.dynamic_update_slice_in_dim(full, block, source * e_local, 1)
+
+    old_full = place(jnp.zeros((doc_shard, width), old_index.dtype), old_index, me_w)
+    to_right, to_left = old_index, old_index
+    for step in range(1, n_wide // 2 + 1):
+        to_right = lax.ppermute(to_right, "wide", right)
+        old_full = place(old_full, to_right, (me_w - step) % n_wide)
+        if step < n_wide - n_wide // 2:
+            to_left = lax.ppermute(to_left, "wide", left)
+            old_full = place(old_full, to_left, (me_w + step) % n_wide)
     g_own = lax.dot_general(
         old_full, masked, (((1,), (1,)), ((), ())), preferred_element_type=jnp.float32
     ).astype(jnp.bfloat16)

time: 256 us -> 216 us (0.84)
  the two profiles are of different devices: /device:TPU:6 before, /device:TPU:32 now
where the time goes in v4:
time: 216 us; the launch traced here: 215 us
  starting transfers between devices  91.7 us (42%)
  waiting for transfers between devices  39.9 us (18%)
  matrix products  39.4 us (18%)
  local copies, waits for them, and re-layouts  26.6 us (12%)
  between operations  14.4 us (7%)
  other arithmetic  2.99 us (1%)
    ppermute x7, starting transfers between devices, local(): to_left = lax.ppermute(to_left, 'wide', left)  40.7 us
    dot_general x4, matrix products, pick_rows(): jnp.dot(one_hot(index, table.shape[0]), table, preferred_element_type=jnp...  28.9 us
    dynamic_update_slice x16, local copies, waits for them, and re-layouts, place(): return lax.dynamic_update_slice_in_dim(full, block, source * e_local, 1)  18.7 us
    ppermute x8, starting transfers between devices, local(): to_right = lax.ppermute(to_right, 'wide', right)  17.5 us
    all_to_all x1, waiting for transfers between devices, local(): lax.all_to_all(served_g, 'dp', 0, 0, tiled=True)  16.9 us
    ppermute x8, waiting for transfers between devices, local(): to_right = lax.ppermute(to_right, 'wide', right)  12.9 us
    all_to_all x1, starting transfers between devices, local(): gathered = lax.all_to_all(spread, 'wide', 0, 0, tiled=True)  10.8 us
    all_to_all x1, starting transfers between devices, local(): lax.all_to_all(served_g, 'dp', 0, 0, tiled=True)  7.65 us
  transfers between devices with their start and end apart: 20, of which 8 were waited for; matrix products, arithmetic and copies ran while one was open for 27% of the time, Pallas kernels for 0%

profile of v4, /device:TPU:32, one launch (start us, length us, event | category | flops | bytes accessed | tf_op | source)
XLA Modules:
  0.0 215.0 jit_solution(1904078051976563613)
XLA Ops:
  8.4 5.8 %convolution_convert_fusion = bf16[512,4096]{1,0:T(8,128)(2,1)} fusion(bf16[512,1024]{1,0:T(8,128)(2,1)S(1)} %copy-done, bf16[1024,256]{1,0:T(8,128)(2,1)} %param.8, bf16[256,4096]{1,0:T(8,128)(2,1)} %param.9, bf16[32,8,32,128]{3,2,1,0:T(8,128)(2,1)S(1)} %bitcast.39), kind=kOutput, calls=%fused_computation.10 | convolution fusion | flops 1345454080 | bytes 9961472 | tf_op jit(solution)/shard_map/dot_general | solution.py:31
  14.2 3.8 %collective-permute-start = (bf16[512,256]{1,0:T(8,128)(2,1)}, bf16[512,256]{1,0:T(8,128)(2,1)}, u32[]{:S(2)}, u32[]{:S(2)}) collective-permute-start(bf16[512,256]{1,0:T(8,128)(2,1)} %param.11), channel_id=1, source_target_pairs={{0,1},{1,2},{2,3},{3,4},{4,5},{5,6},{6,7},{7,8},{8,9},{9,10},{10,1... | collective-permute-start | bytes 786440 | tf_op jit(solution)/shard_map/ppermute | solution.py:66
  18.1 5.5 %collective-permute-start.1 = (bf16[512,256]{1,0:T(8,128)(2,1)}, bf16[512,256]{1,0:T(8,128)(2,1)}, u32[]{:S(2)}, u32[]{:S(2)}) collective-permute-start(bf16[512,256]{1,0:T(8,128)(2,1)} %param.11), channel_id=1, source_target_pairs={{0,15},{1,0},{2,1},{3,2},{4,3},{5,4},{6,5},{7,6},{8,7},{9,8},{10,9... | collective-permute-start | bytes 786440 | tf_op jit(solution)/shard_map/ppermute | solution.py:69
  26.3 2.0 collective-permute-start.2
  28.9 7.9 %collective-permute-start.3 = (bf16[512,256]{1,0:T(8,128)(2,1)}, bf16[512,256]{1,0:T(8,128)(2,1)}, u32[]{:S(2)}, u32[]{:S(2)}) collective-permute-start(bf16[512,256]{1,0:T(8,128)(2,1)} %collective-permute-done.1), channel_id=1, source_target_pairs={{0,15},{1,0},{2,1},{3,2},{4,3},{5,4},{6,5},{7,6},{8,7},{9,8},{10,9... | collective-permute-start | bytes 786440 | tf_op jit(solution)/shard_map/ppermute | solution.py:69
  36.7 7.0 %collective-permute-done.2 = bf16[512,256]{1,0:T(8,128)(2,1)S(1)} collective-permute-done((bf16[512,256]{1,0:T(8,128)(2,1)}, bf16[512,256]{1,0:T(8,128)(2,1)S(1)}, u32[]{:S(2)}, u32[]{:S(2)}) %collective-permute-start.2) | collective-permute-done | bytes 262176 | tf_op jit(solution)/shard_map/ppermute | solution.py:66
  43.7 1.9 collective-permute-start.4
  46.3 7.5 %all-to-all-start = ((s32[32,1,128]{2,1,0:T(1,128)}), s32[32,1,128]{2,1,0:T(1,128)S(1)}, u32[]{:S(2)}, u32[]{:S(2)}) async-start(s32[32,1,128]{2,1,0:T(1,128)} %bitcast.5), calls=%async_computation.1 | async-start | bytes 32768 | tf_op jit(solution)/shard_map/all_to_all | solution.py:51
  53.8 2.5 %broadcast_in_dim.5 = bf16[512,4096]{1,0:T(8,128)(2,1)} broadcast(bf16[]{:T(256)} %constant.146.clone.1), dimensions={} | broadcast | bytes 4194306 | tf_op jit(solution)/shard_map/broadcast_in_dim | solution.py:63
  58.0 6.6 %collective-permute-start.5 = (bf16[512,256]{1,0:T(8,128)(2,1)}, bf16[512,256]{1,0:T(8,128)(2,1)}, u32[]{:S(2)}, u32[]{:S(2)}) collective-permute-start(bf16[512,256]{1,0:T(8,128)(2,1)} %collective-permute-done.3), channel_id=1, source_target_pairs={{0,15},{1,0},{2,1},{3,2},{4,3},{5,4},{6,5},{7,6},{8,7},{9,8},{10,9... | collective-permute-start | bytes 786440 | tf_op jit(solution)/shard_map/ppermute | solution.py:69
  64.6 1.9 collective-permute-start.6
  66.5 4.2 %fusion.7 = bf16[4096,256]{1,0:T(8,128)(2,1)} fusion(bf16[512,256]{1,0:T(8,128)(2,1)} %param.11, s32[4096]{0:T(1024)S(1)} %bitcast.45), kind=kOutput, calls=%fused_computation.11 | convolution fusion | flops 1076887552 | bytes 2375680 | tf_op jit(solution)/shard_map/dot_general | solution.py:18
  70.7 7.5 %all-to-all-start.1 = ((bf16[32,128,256]{2,1,0:T(8,128)(2,1)}), bf16[32,128,256]{2,1,0:T(8,128)(2,1)}, u32[]{:S(2)}, u32[]{:S(2)}) async-start(bf16[32,128,256]{2,1,0:T(8,128)(2,1)} %bitcast.41), calls=%async_computation.2 | async-start | bytes 4194304 | tf_op jit(solution)/shard_map/all_to_all | solution.py:53
  79.9 5.1 %collective-permute-start.7 = (bf16[512,256]{1,0:T(8,128)(2,1)}, bf16[512,256]{1,0:T(8,128)(2,1)S(1)}, u32[]{:S(2)}, u32[]{:S(2)}) collective-permute-start(bf16[512,256]{1,0:T(8,128)(2,1)} %collective-permute-done.5), channel_id=1, source_target_pairs={{0,15},{1,0},{2,1},{3,2},{4,3},{5,4},{6,5},{7,6},{8,7},{9,8},{10,9... | collective-permute-start | bytes 786440 | tf_op jit(solution)/shard_map/ppermute | solution.py:69
  86.7 1.9 collective-permute-start.8
  91.1 5.9 %collective-permute-done.7 = bf16[512,256]{1,0:T(8,128)(2,1)S(1)} collective-permute-done((bf16[512,256]{1,0:T(8,128)(2,1)}, bf16[512,256]{1,0:T(8,128)(2,1)S(1)}, u32[]{:S(2)}, u32[]{:S(2)}) %collective-permute-start.7) | collective-permute-done | bytes 262176 | tf_op jit(solution)/shard_map/ppermute | solution.py:69
  97.0 5.2 %collective-permute-start.9 = (bf16[512,256]{1,0:T(8,128)(2,1)S(1)}, bf16[512,256]{1,0:T(8,128)(2,1)S(1)}, u32[]{:S(2)}, u32[]{:S(2)}) collective-permute-start(bf16[512,256]{1,0:T(8,128)(2,1)S(1)} %collective-permute-done.7), channel_id=1, source_target_pairs={{0,15},{1,0},{2,1},{3,2},{4,3},{5,4},{6,5},{7,6},{8,7},{9,8},{10,9... | collective-permute-start | bytes 786440 | tf_op jit(solution)/shard_map/ppermute | solution.py:69
  103.9 1.9 collective-permute-start.10
  109.3 5.5 %collective-permute-start.11 = (bf16[512,256]{1,0:T(8,128)(2,1)S(1)}, bf16[512,256]{1,0:T(8,128)(2,1)S(1)}, u32[]{:S(2)}, u32[]{:S(2)}) collective-permute-start(bf16[512,256]{1,0:T(8,128)(2,1)S(1)} %collective-permute-done.9), channel_id=1, source_target_pairs={{0,15},{1,0},{2,1},{3,2},{4,3},{5,4},{6,5},{7,6},{8,7},{9,8},{10,9... | collective-permute-start | bytes 786440 | tf_op jit(solution)/shard_map/ppermute | solution.py:69
  115.6 1.9 collective-permute-start.12
  119.1 5.0 %collective-permute-start.13 = (bf16[512,256]{1,0:T(8,128)(2,1)S(1)}, bf16[512,256]{1,0:T(8,128)(2,1)S(1)}, u32[]{:S(2)}, u32[]{:S(2)}) collective-permute-start(bf16[512,256]{1,0:T(8,128)(2,1)S(1)} %collective-permute-done.11), channel_id=1, source_target_pairs={{0,15},{1,0},{2,1},{3,2},{4,3},{5,4},{6,5},{7,6},{8,7},{9,8},{10,9... | collective-permute-start | bytes 786440 | tf_op jit(solution)/shard_map/ppermute | solution.py:69
  125.2 2.1 collective-permute-start.14
  129.6 5.1 %collective-permute-done.14 = bf16[512,256]{1,0:T(8,128)(2,1)S(1)} collective-permute-done((bf16[512,256]{1,0:T(8,128)(2,1)S(1)}, bf16[512,256]{1,0:T(8,128)(2,1)S(1)}, u32[]{:S(2)}, u32[]{:S(2)}) %collective-permute-start.14) | collective-permute-done | bytes 262176 | tf_op jit(solution)/shard_map/ppermute | solution.py:66
  135.4 8.8 %fusion.8 = bf16[4096,256]{1,0:T(8,128)(2,1)} fusion(s32[4096]{0:T(1024)S(1)} %bitcast.46, bf16[512,4096]{1,0:T(8,128)(2,1)} %constant_dynamic-update-slice_fusion, bf16[256,4096]{1,0:T(8,128)(2,1)} %param.9, bf16[32,8,32,128]{3,2,1,0:T(8,128)(2,1)S(1)} %bitcast.40), kind=kOutput, calls=%fused_computation.12 | convolution fusion | flops 2151809024 | bytes 10502144 | tf_op jit(solution)/shard_map/dot_general | solution.py:18
  144.2 7.7 %all-to-all-start.3 = ((bf16[32,128,256]{2,1,0:T(8,128)(2,1)}), bf16[32,128,256]{2,1,0:T(8,128)(2,1)S(1)}, u32[]{:S(2)}, u32[]{:S(2)}) async-start(bf16[32,128,256]{2,1,0:T(8,128)(2,1)} %bitcast.43), calls=%async_computation.4 | async-start | bytes 4194304 | tf_op jit(solution)/shard_map/all_to_all | solution.py:75
  151.9 8.8 %fusion.11 = bf16[2048,256]{1,0:T(8,128)(2,1)} fusion(bf16[4096,256]{1,0:T(8,128)(2,1)} %bitcast.8, s32[2048]{0:T(1024)S(1)} %multiply_add_fusion), kind=kOutput, calls=%fused_computation.15 | convolution fusion | flops 4303880192 | bytes 3153920 | tf_op jit(solution)/shard_map/dot_general | solution.py:18
  160.6 2.2 %reshape.272 = bf16[512,4,256]{2,1,0:T(4,128)(2,1)} reshape(bf16[2048,256]{1,0:T(8,128)(2,1)} %fusion.11) | data formatting | bytes 2097152 | tf_op jit(solution)/shard_map/reshape | solution.py:54
  162.8 2.0 fusion.21
  164.9 16.9 %all-to-all-done.3 = bf16[32,128,256]{2,1,0:T(8,128)(2,1)S(1)} async-done(((bf16[32,128,256]{2,1,0:T(8,128)(2,1)}), bf16[32,128,256]{2,1,0:T(8,128)(2,1)S(1)}, u32[]{:S(2)}, u32[]{:S(2)}) %all-to-all-start.3) | async-done | bytes 2097184 | tf_op jit(solution)/shard_map/all_to_all | solution.py:75
  182.5 10.8 %all-to-all-start.2 = ((f32[16,512,4]{1,2,0:T(4,128)}), f32[16,512,4]{1,2,0:T(4,128)S(1)}, u32[]{:S(2)}, u32[]{:S(2)}) async-start(f32[16,512,4]{1,2,0:T(4,128)} %broadcast_in_dim.4), calls=%async_computation.3 | async-start | bytes 262144 | tf_op jit(solution)/shard_map/all_to_all | solution.py:82
  193.3 7.2 %fusion.12 = bf16[2048,256]{1,0:T(8,128)(2,1)} fusion(bf16[4096,256]{1,0:T(8,128)(2,1)S(1)} %bitcast.42, s32[2048]{0:T(1024)S(1)} %multiply_add_fusion), kind=kOutput, calls=%fused_computation.16 | convolution fusion | flops 4303880192 | bytes 3153920 | tf_op jit(solution)/shard_map/dot_general | solution.py:18
  201.8 4.0 %all-to-all-done.2 = f32[16,512,4]{1,2,0:T(4,128)S(1)} async-done(((f32[16,512,4]{1,2,0:T(4,128)}), f32[16,512,4]{1,2,0:T(4,128)S(1)}, u32[]{:S(2)}, u32[]{:S(2)}) %all-to-all-start.2) | async-done | bytes 131104 | tf_op jit(solution)/shard_map/all_to_all | solution.py:82
  (63 shorter events, 28.7 us)
Async XLA Ops:
  7.2 1.2 copy-start
  7.2 155.6 %reduce-scatter.2.cloned.1.call-start = ((), (), s32[]{:S(2)}) async-start(), calls=%async_computation.5 | async-start | bytes 4456448 | tf_op jit(solution)/shard_map/reduce_scatter | solution.py:32
  14.2 9.4 %copy-start.2 = (s32[512,4]{0,1:T(4,128)S(1)}, s32[512,4]{0,1:T(4,128)}, u32[]{:S(2)}) copy-start(s32[512,4]{0,1:T(4,128)} %param.12) | copy-start | bytes 24580
  14.2 12.1 %collective-permute-start = (bf16[512,256]{1,0:T(8,128)(2,1)}, bf16[512,256]{1,0:T(8,128)(2,1)}, u32[]{:S(2)}, u32[]{:S(2)}) collective-permute-start(bf16[512,256]{1,0:T(8,128)(2,1)} %param.11), channel_id=1, source_target_pairs={{0,1},{1,2},{2,3},{3,4},{4,5},{5,6},{6,7},{7,8},{8,9},{9,10},{10,1... | collective-permute-start | bytes 786440 | tf_op jit(solution)/shard_map/ppermute | solution.py:66
  18.1 10.8 %collective-permute-start.1 = (bf16[512,256]{1,0:T(8,128)(2,1)}, bf16[512,256]{1,0:T(8,128)(2,1)}, u32[]{:S(2)}, u32[]{:S(2)}) collective-permute-start(bf16[512,256]{1,0:T(8,128)(2,1)} %param.11), channel_id=1, source_target_pairs={{0,15},{1,0},{2,1},{3,2},{4,3},{5,4},{6,5},{7,6},{8,7},{9,8},{10,9... | collective-permute-start | bytes 786440 | tf_op jit(solution)/shard_map/ppermute | solution.py:69
  26.3 17.4 %collective-permute-start.2 = (bf16[512,256]{1,0:T(8,128)(2,1)}, bf16[512,256]{1,0:T(8,128)(2,1)S(1)}, u32[]{:S(2)}, u32[]{:S(2)}) collective-permute-start(bf16[512,256]{1,0:T(8,128)(2,1)} %collective-permute-done), channel_id=1, source_target_pairs={{0,1},{1,2},{2,3},{3,4},{4,5},{5,6},{6,7},{7,8},{8,9},{9,10},{10,1... | collective-permute-start | bytes 786440 | tf_op jit(solution)/shard_map/ppermute | solution.py:66
  28.9 29.1 %collective-permute-start.3 = (bf16[512,256]{1,0:T(8,128)(2,1)}, bf16[512,256]{1,0:T(8,128)(2,1)}, u32[]{:S(2)}, u32[]{:S(2)}) collective-permute-start(bf16[512,256]{1,0:T(8,128)(2,1)} %collective-permute-done.1), channel_id=1, source_target_pairs={{0,15},{1,0},{2,1},{3,2},{4,3},{5,4},{6,5},{7,6},{8,7},{9,8},{10,9... | collective-permute-start | bytes 786440 | tf_op jit(solution)/shard_map/ppermute | solution.py:69
  43.7 20.8 %collective-permute-start.4 = (bf16[512,256]{1,0:T(8,128)(2,1)S(1)}, bf16[512,256]{1,0:T(8,128)(2,1)}, u32[]{:S(2)}, u32[]{:S(2)}) collective-permute-start(bf16[512,256]{1,0:T(8,128)(2,1)S(1)} %collective-permute-done.2), channel_id=1, source_target_pairs={{0,1},{1,2},{2,3},{3,4},{4,5},{5,6},{6,7},{7,8},{8,9},{9,10},{10,1... | collective-permute-start | bytes 786440 | tf_op jit(solution)/shard_map/ppermute | solution.py:66
  46.3 20.2 %all-to-all-start = ((s32[32,1,128]{2,1,0:T(1,128)}), s32[32,1,128]{2,1,0:T(1,128)S(1)}, u32[]{:S(2)}, u32[]{:S(2)}) async-start(s32[32,1,128]{2,1,0:T(1,128)} %bitcast.5), calls=%async_computation.1 | async-start | bytes 32768 | tf_op jit(solution)/shard_map/all_to_all | solution.py:51
  58.0 22.0 %collective-permute-start.5 = (bf16[512,256]{1,0:T(8,128)(2,1)}, bf16[512,256]{1,0:T(8,128)(2,1)}, u32[]{:S(2)}, u32[]{:S(2)}) collective-permute-start(bf16[512,256]{1,0:T(8,128)(2,1)} %collective-permute-done.3), channel_id=1, source_target_pairs={{0,15},{1,0},{2,1},{3,2},{4,3},{5,4},{6,5},{7,6},{8,7},{9,8},{10,9... | collective-permute-start | bytes 786440 | tf_op jit(solution)/shard_map/ppermute | solution.py:69
  64.6 22.2 %collective-permute-start.6 = (bf16[512,256]{1,0:T(8,128)(2,1)}, bf16[512,256]{1,0:T(8,128)(2,1)}, u32[]{:S(2)}, u32[]{:S(2)}) collective-permute-start(bf16[512,256]{1,0:T(8,128)(2,1)} %collective-permute-done.4), channel_id=1, source_target_pairs={{0,1},{1,2},{2,3},{3,4},{4,5},{5,6},{6,7},{7,8},{8,9},{9,10},{10,1... | collective-permute-start | bytes 786440 | tf_op jit(solution)/shard_map/ppermute | solution.py:66
  70.7 73.5 %all-to-all-start.1 = ((bf16[32,128,256]{2,1,0:T(8,128)(2,1)}), bf16[32,128,256]{2,1,0:T(8,128)(2,1)}, u32[]{:S(2)}, u32[]{:S(2)}) async-start(bf16[32,128,256]{2,1,0:T(8,128)(2,1)} %bitcast.41), calls=%async_computation.2 | async-start | bytes 4194304 | tf_op jit(solution)/shard_map/all_to_all | solution.py:53
  79.9 17.1 %collective-permute-start.7 = (bf16[512,256]{1,0:T(8,128)(2,1)}, bf16[512,256]{1,0:T(8,128)(2,1)S(1)}, u32[]{:S(2)}, u32[]{:S(2)}) collective-permute-start(bf16[512,256]{1,0:T(8,128)(2,1)} %collective-permute-done.5), channel_id=1, source_target_pairs={{0,15},{1,0},{2,1},{3,2},{4,3},{5,4},{6,5},{7,6},{8,7},{9,8},{10,9... | collective-permute-start | bytes 786440 | tf_op jit(solution)/shard_map/ppermute | solution.py:69
  86.7 17.2 %collective-permute-start.8 = (bf16[512,256]{1,0:T(8,128)(2,1)}, bf16[512,256]{1,0:T(8,128)(2,1)S(1)}, u32[]{:S(2)}, u32[]{:S(2)}) collective-permute-start(bf16[512,256]{1,0:T(8,128)(2,1)} %collective-permute-done.6), channel_id=1, source_target_pairs={{0,1},{1,2},{2,3},{3,4},{4,5},{5,6},{6,7},{7,8},{8,9},{9,10},{10,1... | collective-permute-start | bytes 786440 | tf_op jit(solution)/shard_map/ppermute | solution.py:66
  97.0 12.2 %collective-permute-start.9 = (bf16[512,256]{1,0:T(8,128)(2,1)S(1)}, bf16[512,256]{1,0:T(8,128)(2,1)S(1)}, u32[]{:S(2)}, u32[]{:S(2)}) collective-permute-start(bf16[512,256]{1,0:T(8,128)(2,1)S(1)} %collective-permute-done.7), channel_id=1, source_target_pairs={{0,15},{1,0},{2,1},{3,2},{4,3},{5,4},{6,5},{7,6},{8,7},{9,8},{10,9... | collective-permute-start | bytes 786440 | tf_op jit(solution)/shard_map/ppermute | solution.py:69
  103.9 11.6 %collective-permute-start.10 = (bf16[512,256]{1,0:T(8,128)(2,1)S(1)}, bf16[512,256]{1,0:T(8,128)(2,1)S(1)}, u32[]{:S(2)}, u32[]{:S(2)}) collective-permute-start(bf16[512,256]{1,0:T(8,128)(2,1)S(1)} %collective-permute-done.8), channel_id=1, source_target_pairs={{0,1},{1,2},{2,3},{3,4},{4,5},{5,6},{6,7},{7,8},{8,9},{9,10},{10,1... | collective-permute-start | bytes 786440 | tf_op jit(solution)/shard_map/ppermute | solution.py:66
  109.3 9.8 %collective-permute-start.11 = (bf16[512,256]{1,0:T(8,128)(2,1)S(1)}, bf16[512,256]{1,0:T(8,128)(2,1)S(1)}, u32[]{:S(2)}, u32[]{:S(2)}) collective-permute-start(bf16[512,256]{1,0:T(8,128)(2,1)S(1)} %collective-permute-done.9), channel_id=1, source_target_pairs={{0,15},{1,0},{2,1},{3,2},{4,3},{5,4},{6,5},{7,6},{8,7},{9,8},{10,9... | collective-permute-start | bytes 786440 | tf_op jit(solution)/shard_map/ppermute | solution.py:69
  115.6 9.6 %collective-permute-start.12 = (bf16[512,256]{1,0:T(8,128)(2,1)S(1)}, bf16[512,256]{1,0:T(8,128)(2,1)S(1)}, u32[]{:S(2)}, u32[]{:S(2)}) collective-permute-start(bf16[512,256]{1,0:T(8,128)(2,1)S(1)} %collective-permute-done.10), channel_id=1, source_target_pairs={{0,1},{1,2},{2,3},{3,4},{4,5},{5,6},{6,7},{7,8},{8,9},{9,10},{10,1... | collective-permute-start | bytes 786440 | tf_op jit(solution)/shard_map/ppermute | solution.py:66
  119.1 9.7 %collective-permute-start.13 = (bf16[512,256]{1,0:T(8,128)(2,1)S(1)}, bf16[512,256]{1,0:T(8,128)(2,1)S(1)}, u32[]{:S(2)}, u32[]{:S(2)}) collective-permute-start(bf16[512,256]{1,0:T(8,128)(2,1)S(1)} %collective-permute-done.11), channel_id=1, source_target_pairs={{0,15},{1,0},{2,1},{3,2},{4,3},{5,4},{6,5},{7,6},{8,7},{9,8},{10,9... | collective-permute-start | bytes 786440 | tf_op jit(solution)/shard_map/ppermute | solution.py:69
  125.2 9.5 %collective-permute-start.14 = (bf16[512,256]{1,0:T(8,128)(2,1)S(1)}, bf16[512,256]{1,0:T(8,128)(2,1)S(1)}, u32[]{:S(2)}, u32[]{:S(2)}) collective-permute-start(bf16[512,256]{1,0:T(8,128)(2,1)S(1)} %collective-permute-done.12), channel_id=1, source_target_pairs={{0,1},{1,2},{2,3},{3,4},{4,5},{5,6},{6,7},{7,8},{8,9},{9,10},{10,1... | collective-permute-start | bytes 786440 | tf_op jit(solution)/shard_map/ppermute | solution.py:66
  144.2 37.6 %all-to-all-start.3 = ((bf16[32,128,256]{2,1,0:T(8,128)(2,1)}), bf16[32,128,256]{2,1,0:T(8,128)(2,1)S(1)}, u32[]{:S(2)}, u32[]{:S(2)}) async-start(bf16[32,128,256]{2,1,0:T(8,128)(2,1)} %bitcast.43), calls=%async_computation.4 | async-start | bytes 4194304 | tf_op jit(solution)/shard_map/all_to_all | solution.py:75
  182.5 23.3 %all-to-all-start.2 = ((f32[16,512,4]{1,2,0:T(4,128)}), f32[16,512,4]{1,2,0:T(4,128)S(1)}, u32[]{:S(2)}, u32[]{:S(2)}) async-start(f32[16,512,4]{1,2,0:T(4,128)} %broadcast_in_dim.4), calls=%async_computation.3 | async-start | bytes 262144 | tf_op jit(solution)/shard_map/all_to_all | solution.py:82
  193.3 12.6 %copy-start.1 = (s32[512,4]{0,1:T(4,128)S(1)}, s32[512,4]{0,1:T(4,128)}, u32[]{:S(2)}) copy-start(s32[512,4]{0,1:T(4,128)} %param.13) | copy-start | bytes 24580
Sparse Core Ops, SparseCore 0:
  14.4 95.7 reduce-scatter.1

commit v5 on v4

--- a/solution.py
+++ b/solution.py
@@ -71,15 +71,16 @@
     g_own = lax.dot_general(
         old_full, masked, (((1,), (1,)), ((), ())), preferred_element_type=jnp.float32
     ).astype(jnp.bfloat16)
-    served_g = pick_rows(asked, g_own).reshape(n_dp, CAP, e_local)
-    back_g = lax.all_to_all(served_g, "dp", 0, 0, tiled=True).reshape(n_dp * CAP, e_local)
-    g_vec = pick_rows(slot, back_g).reshape(rows, K, e_local).astype(jnp.float32)
 
     old_wide = old_vec.astype(jnp.float32)
     scale = 1.0 / math.sqrt(E)
     partial_scores = jnp.einsum("re,rke->rk", new, old_wide)
     spread = jnp.broadcast_to(partial_scores[None], (n_wide,) + partial_scores.shape)
     gathered = lax.all_to_all(spread, "wide", 0, 0, tiled=True)
+    g_own, gathered = lax.optimization_barrier((g_own, gathered))
+    served_g = pick_rows(asked, g_own).reshape(n_dp, CAP, e_local)
+    back_g = lax.all_to_all(served_g, "dp", 0, 0, tiled=True).reshape(n_dp * CAP, e_local)
+    g_vec = pick_rows(slot, back_g).reshape(rows, K, e_local).astype(jnp.float32)
     score = jnp.sum(gathered, axis=0) * scale
     sign = 2.0 * labels.astype(jnp.float32) - 1.0
     pair_loss = jax.nn.softplus(-sign * score)

time: 216 us -> 228 us (1.056)
  waiting for transfers between devices: 39.9 us -> 54.4 us
  starting transfers between devices: 91.7 us -> 88.1 us
    all_to_all x1, waiting for transfers between devices: 16.9 us -> 28.9 us  [local(): lax.all_to_all(served_g, 'dp', 0, 0, tiled=True)]
    ppermute x7, waiting for transfers between devices: 6.09 us -> 0.02 us  [local(): to_left = lax.ppermute(to_left, 'wide', left)]
    ppermute x8, waiting for transfers between devices: 12.9 us -> 17.9 us  [local(): to_right = lax.ppermute(to_right, 'wide', right)]
    dot_general x0 -> x1, matrix products: none -> 4.9 us  [local(): lax.dot_general(old_full, masked, (((1,), (1,)), ((), ())), preferred_ele...]
    ppermute x7, starting transfers between devices: 40.7 us -> 35.9 us  [local(): to_left = lax.ppermute(to_left, 'wide', left)]
    dot_general x4, matrix products: 28.9 us -> 24.4 us  [pick_rows(): jnp.dot(one_hot(index, table.shape[0]), table, preferred_element_type=jnp...]
    all_to_all x1, waiting for transfers between devices: 3.98 us -> 7.64 us  [local(): gathered = lax.all_to_all(spread, 'wide', 0, 0, tiled=True)]
    all_to_all x1, starting transfers between devices: 7.51 us -> 3.86 us  [local(): asked = lax.all_to_all(req, 'dp', 0, 0, tiled=True).reshape(-1)]
  transfers between devices with their start and end apart: 20 -> 20, of which waited for: 8 -> 7; matrix products, arithmetic and copies ran while one was open for 27% -> 20% of each run, Pallas kernels for 0% -> 0%
where the time goes in v5:
time: 228 us; the launch traced here: 227 us
  starting transfers between devices  88.1 us (39%)
  waiting for transfers between devices  54.4 us (24%)
  matrix products  39.7 us (17%)
  local copies, waits for them, and re-layouts  26.7 us (12%)
  between operations  14.7 us (6%)
  other arithmetic  2.99 us (1%)
    ppermute x7, starting transfers between devices, local(): to_left = lax.ppermute(to_left, 'wide', left)  35.9 us
    all_to_all x1, waiting for transfers between devices, local(): lax.all_to_all(served_g, 'dp', 0, 0, tiled=True)  28.9 us
    dot_general x4, matrix products, pick_rows(): jnp.dot(one_hot(index, table.shape[0]), table, preferred_element_type=jnp...  24.4 us
    ppermute x8, starting transfers between devices, local(): to_right = lax.ppermute(to_right, 'wide', right)  19.6 us
    dynamic_update_slice x16, local copies, waits for them, and re-layouts, place(): return lax.dynamic_update_slice_in_dim(full, block, source * e_local, 1)  18.7 us
    ppermute x8, waiting for transfers between devices, local(): to_right = lax.ppermute(to_right, 'wide', right)  17.9 us
    all_to_all x1, starting transfers between devices, local(): gathered = lax.all_to_all(spread, 'wide', 0, 0, tiled=True)  13.7 us
    all_to_all x1, waiting for transfers between devices, local(): gathered = lax.all_to_all(spread, 'wide', 0, 0, tiled=True)  7.64 us
  transfers between devices with their start and end apart: 20, of which 7 were waited for; matrix products, arithmetic and copies ran while one was open for 20% of the time, Pallas kernels for 0%

profile of v5, /device:TPU:32, one launch (start us, length us, event | category | flops | bytes accessed | tf_op | source)
XLA Modules:
  0.0 226.6 jit_solution(5664914673671029992)
XLA Ops:
  8.4 5.8 %convolution_convert_fusion = bf16[512,4096]{1,0:T(8,128)(2,1)} fusion(bf16[512,1024]{1,0:T(8,128)(2,1)S(1)} %copy-done, bf16[1024,256]{1,0:T(8,128)(2,1)} %param.8, bf16[256,4096]{1,0:T(8,128)(2,1)} %param.9, bf16[32,8,32,128]{3,2,1,0:T(8,128)(2,1)S(1)} %bitcast.39), kind=kOutput, calls=%fused_computation.10 | convolution fusion | flops 1345454080 | bytes 9961472 | tf_op jit(solution)/shard_map/dot_general | solution.py:31
  14.2 3.8 %collective-permute-start = (bf16[512,256]{1,0:T(8,128)(2,1)}, bf16[512,256]{1,0:T(8,128)(2,1)}, u32[]{:S(2)}, u32[]{:S(2)}) collective-permute-start(bf16[512,256]{1,0:T(8,128)(2,1)} %param.11), channel_id=1, source_target_pairs={{0,1},{1,2},{2,3},{3,4},{4,5},{5,6},{6,7},{7,8},{8,9},{9,10},{10,1... | collective-permute-start | bytes 786440 | tf_op jit(solution)/shard_map/ppermute | solution.py:66
  18.1 5.5 %collective-permute-start.1 = (bf16[512,256]{1,0:T(8,128)(2,1)}, bf16[512,256]{1,0:T(8,128)(2,1)}, u32[]{:S(2)}, u32[]{:S(2)}) collective-permute-start(bf16[512,256]{1,0:T(8,128)(2,1)} %param.11), channel_id=1, source_target_pairs={{0,15},{1,0},{2,1},{3,2},{4,3},{5,4},{6,5},{7,6},{8,7},{9,8},{10,9... | collective-permute-start | bytes 786440 | tf_op jit(solution)/shard_map/ppermute | solution.py:69
  26.9 3.9 %all-to-all-start = ((s32[32,1,128]{2,1,0:T(1,128)}), s32[32,1,128]{2,1,0:T(1,128)S(1)}, u32[]{:S(2)}, u32[]{:S(2)}) async-start(s32[32,1,128]{2,1,0:T(1,128)} %bitcast.5), calls=%async_computation.1 | async-start | bytes 32768 | tf_op jit(solution)/shard_map/all_to_all | solution.py:51
  30.8 3.8 %collective-permute-start.2 = (bf16[512,256]{1,0:T(8,128)(2,1)}, bf16[512,256]{1,0:T(8,128)(2,1)}, u32[]{:S(2)}, u32[]{:S(2)}) collective-permute-start(bf16[512,256]{1,0:T(8,128)(2,1)} %collective-permute-done), channel_id=1, source_target_pairs={{0,1},{1,2},{2,3},{3,4},{4,5},{5,6},{6,7},{7,8},{8,9},{9,10},{10,1... | collective-permute-start | bytes 786440 | tf_op jit(solution)/shard_map/ppermute | solution.py:66
  34.6 7.6 %collective-permute-start.3 = (bf16[512,256]{1,0:T(8,128)(2,1)}, bf16[512,256]{1,0:T(8,128)(2,1)S(1)}, u32[]{:S(2)}, u32[]{:S(2)}) collective-permute-start(bf16[512,256]{1,0:T(8,128)(2,1)} %collective-permute-done.1), channel_id=1, source_target_pairs={{0,15},{1,0},{2,1},{3,2},{4,3},{5,4},{6,5},{7,6},{8,7},{9,8},{10,9... | collective-permute-start | bytes 786440 | tf_op jit(solution)/shard_map/ppermute | solution.py:69
  42.2 4.2 %fusion.7 = bf16[4096,256]{1,0:T(8,128)(2,1)} fusion(bf16[512,256]{1,0:T(8,128)(2,1)} %param.11, s32[4096]{0:T(1024)S(1)} %bitcast.45), kind=kOutput, calls=%fused_computation.11 | convolution fusion | flops 1076887552 | bytes 2375680 | tf_op jit(solution)/shard_map/dot_general | solution.py:18
  46.4 7.5 %all-to-all-start.1 = ((bf16[32,128,256]{2,1,0:T(8,128)(2,1)}), bf16[32,128,256]{2,1,0:T(8,128)(2,1)}, u32[]{:S(2)}, u32[]{:S(2)}) async-start(bf16[32,128,256]{2,1,0:T(8,128)(2,1)} %bitcast.41), calls=%async_computation.2 | async-start | bytes 4194304 | tf_op jit(solution)/shard_map/all_to_all | solution.py:53
  54.0 1.9 collective-permute-start.4
  55.9 5.1 %collective-permute-start.5 = (bf16[512,256]{1,0:T(8,128)(2,1)S(1)}, bf16[512,256]{1,0:T(8,128)(2,1)}, u32[]{:S(2)}, u32[]{:S(2)}) collective-permute-start(bf16[512,256]{1,0:T(8,128)(2,1)S(1)} %collective-permute-done.3), channel_id=1, source_target_pairs={{0,15},{1,0},{2,1},{3,2},{4,3},{5,4},{6,5},{7,6},{8,7},{9,8},{10,9... | collective-permute-start | bytes 786440 | tf_op jit(solution)/shard_map/ppermute | solution.py:69
  61.4 2.5 %broadcast_in_dim.4 = bf16[512,4096]{1,0:T(8,128)(2,1)} broadcast(bf16[]{:T(256)} %constant.133.clone.1), dimensions={} | broadcast | bytes 4194306 | tf_op jit(solution)/shard_map/broadcast_in_dim | solution.py:63
  65.6 6.3 %collective-permute-done.4 = bf16[512,256]{1,0:T(8,128)(2,1)} collective-permute-done((bf16[512,256]{1,0:T(8,128)(2,1)}, bf16[512,256]{1,0:T(8,128)(2,1)}, u32[]{:S(2)}, u32[]{:S(2)}) %collective-permute-start.4) | collective-permute-done | bytes 262176 | tf_op jit(solution)/shard_map/ppermute | solution.py:66
  75.4 4.7 %collective-permute-start.7 = (bf16[512,256]{1,0:T(8,128)(2,1)}, bf16[512,256]{1,0:T(8,128)(2,1)S(1)}, u32[]{:S(2)}, u32[]{:S(2)}) collective-permute-start(bf16[512,256]{1,0:T(8,128)(2,1)} %collective-permute-done.5), channel_id=1, source_target_pairs={{0,15},{1,0},{2,1},{3,2},{4,3},{5,4},{6,5},{7,6},{8,7},{9,8},{10,9... | collective-permute-start | bytes 786440 | tf_op jit(solution)/shard_map/ppermute | solution.py:69
  83.5 5.4 %collective-permute-done.6 = bf16[512,256]{1,0:T(8,128)(2,1)S(1)} collective-permute-done((bf16[512,256]{1,0:T(8,128)(2,1)}, bf16[512,256]{1,0:T(8,128)(2,1)S(1)}, u32[]{:S(2)}, u32[]{:S(2)}) %collective-permute-start.6) | collective-permute-done | bytes 262176 | tf_op jit(solution)/shard_map/ppermute | solution.py:66
  88.9 1.9 collective-permute-start.8
  91.6 5.0 %collective-permute-start.9 = (bf16[512,256]{1,0:T(8,128)(2,1)S(1)}, bf16[512,256]{1,0:T(8,128)(2,1)S(1)}, u32[]{:S(2)}, u32[]{:S(2)}) collective-permute-start(bf16[512,256]{1,0:T(8,128)(2,1)S(1)} %collective-permute-done.7), channel_id=1, source_target_pairs={{0,15},{1,0},{2,1},{3,2},{4,3},{5,4},{6,5},{7,6},{8,7},{9,8},{10,9... | collective-permute-start | bytes 786440 | tf_op jit(solution)/shard_map/ppermute | solution.py:69
  100.0 5.6 %collective-permute-done.8 = bf16[512,256]{1,0:T(8,128)(2,1)S(1)} collective-permute-done((bf16[512,256]{1,0:T(8,128)(2,1)S(1)}, bf16[512,256]{1,0:T(8,128)(2,1)S(1)}, u32[]{:S(2)}, u32[]{:S(2)}) %collective-permute-start.8) | collective-permute-done | bytes 262176 | tf_op jit(solution)/shard_map/ppermute | solution.py:66
  105.6 1.9 collective-permute-start.10
  108.3 3.9 %collective-permute-start.11 = (bf16[512,256]{1,0:T(8,128)(2,1)S(1)}, bf16[512,256]{1,0:T(8,128)(2,1)S(1)}, u32[]{:S(2)}, u32[]{:S(2)}) collective-permute-start(bf16[512,256]{1,0:T(8,128)(2,1)S(1)} %collective-permute-done.9), channel_id=1, source_target_pairs={{0,15},{1,0},{2,1},{3,2},{4,3},{5,4},{6,5},{7,6},{8,7},{9,8},{10,9... | collective-permute-start | bytes 786440 | tf_op jit(solution)/shard_map/ppermute | solution.py:69
  114.3 2.2 collective-permute-start.12
  117.2 4.1 %collective-permute-start.13 = (bf16[512,256]{1,0:T(8,128)(2,1)S(1)}, bf16[512,256]{1,0:T(8,128)(2,1)S(1)}, u32[]{:S(2)}, u32[]{:S(2)}) collective-permute-start(bf16[512,256]{1,0:T(8,128)(2,1)S(1)} %collective-permute-done.11), channel_id=1, source_target_pairs={{0,15},{1,0},{2,1},{3,2},{4,3},{5,4},{6,5},{7,6},{8,7},{9,8},{10,9... | collective-permute-start | bytes 786440 | tf_op jit(solution)/shard_map/ppermute | solution.py:69
  123.0 2.1 collective-permute-start.14
  126.6 8.8 %fusion.11 = bf16[2048,256]{1,0:T(8,128)(2,1)} fusion(bf16[4096,256]{1,0:T(8,128)(2,1)} %bitcast.8, s32[2048]{0:T(1024)S(1)} %multiply_add_fusion), kind=kOutput, calls=%fused_computation.15 | convolution fusion | flops 4303880192 | bytes 3153920 | tf_op jit(solution)/shard_map/dot_general | solution.py:18
  135.3 2.2 reshape.272
  139.3 2.0 fusion.21
  142.1 13.7 %all-to-all-start.2 = ((f32[16,512,4]{1,2,0:T(4,128)}), f32[16,512,4]{1,2,0:T(4,128)S(1)}, u32[]{:S(2)}, u32[]{:S(2)}) async-start(f32[16,512,4]{1,2,0:T(4,128)} %broadcast_in_dim.5), calls=%async_computation.3 | async-start | bytes 262144 | tf_op jit(solution)/shard_map/all_to_all | solution.py:79
  155.8 4.9 %convolution_convert_fusion.1 = bf16[512,256]{1,0:T(8,128)(2,1)} fusion(bf16[512,4096]{1,0:T(8,128)(2,1)} %constant_dynamic-update-slice_fusion, bf16[256,4096]{1,0:T(8,128)(2,1)} %param.9, bf16[32,8,32,128]{3,2,1,0:T(8,128)(2,1)S(1)} %bitcast.40), kind=kOutput, calls=%fused_computation.19 | convolution fusion | flops 1074921472 | bytes 8650752 | tf_op jit(solution)/shard_map/dot_general | solution.py:71
  160.7 7.6 %all-to-all-done.2 = f32[16,512,4]{1,2,0:T(4,128)S(1)} async-done(((f32[16,512,4]{1,2,0:T(4,128)}), f32[16,512,4]{1,2,0:T(4,128)S(1)}, u32[]{:S(2)}, u32[]{:S(2)}) %all-to-all-start.2) | async-done | bytes 131104 | tf_op jit(solution)/shard_map/all_to_all | solution.py:79
  168.3 4.2 %fusion.8 = bf16[4096,256]{1,0:T(8,128)(2,1)} fusion(bf16[512,256]{1,0:T(8,128)(2,1)} %convolution_convert_fusion.1, s32[4096]{0:T(1024)S(1)} %bitcast.46), kind=kOutput, calls=%fused_computation.12 | convolution fusion | flops 1076887552 | bytes 2375680 | tf_op jit(solution)/shard_map/dot_general | solution.py:18
  172.6 7.5 %all-to-all-start.3 = ((bf16[32,128,256]{2,1,0:T(8,128)(2,1)}), bf16[32,128,256]{2,1,0:T(8,128)(2,1)S(1)}, u32[]{:S(2)}, u32[]{:S(2)}) async-start(bf16[32,128,256]{2,1,0:T(8,128)(2,1)} %bitcast.43), calls=%async_computation.4 | async-start | bytes 4194304 | tf_op jit(solution)/shard_map/all_to_all | solution.py:82
  181.0 28.9 %all-to-all-done.3 = bf16[32,128,256]{2,1,0:T(8,128)(2,1)S(1)} async-done(((bf16[32,128,256]{2,1,0:T(8,128)(2,1)}), bf16[32,128,256]{2,1,0:T(8,128)(2,1)S(1)}, u32[]{:S(2)}, u32[]{:S(2)}) %all-to-all-start.3) | async-done | bytes 2097184 | tf_op jit(solution)/shard_map/all_to_all | solution.py:82
  209.8 7.2 %fusion.12 = bf16[2048,256]{1,0:T(8,128)(2,1)} fusion(bf16[4096,256]{1,0:T(8,128)(2,1)S(1)} %bitcast.42, s32[2048]{0:T(1024)S(1)} %multiply_add_fusion), kind=kOutput, calls=%fused_computation.16 | convolution fusion | flops 4303880192 | bytes 3153920 | tf_op jit(solution)/shard_map/dot_general | solution.py:18
  (64 shorter events, 30.2 us)
Async XLA Ops:
  7.2 1.2 copy-start
  7.2 132.1 %reduce-scatter.2.cloned.1.call-start = ((), (), s32[]{:S(2)}) async-start(), calls=%async_computation.5 | async-start | bytes 4456448 | tf_op jit(solution)/shard_map/reduce_scatter | solution.py:32
  14.2 9.4 %copy-start.2 = (s32[512,4]{0,1:T(4,128)S(1)}, s32[512,4]{0,1:T(4,128)}, u32[]{:S(2)}) copy-start(s32[512,4]{0,1:T(4,128)} %param.12) | copy-start | bytes 24580
  14.2 16.5 %collective-permute-start = (bf16[512,256]{1,0:T(8,128)(2,1)}, bf16[512,256]{1,0:T(8,128)(2,1)}, u32[]{:S(2)}, u32[]{:S(2)}) collective-permute-start(bf16[512,256]{1,0:T(8,128)(2,1)} %param.11), channel_id=1, source_target_pairs={{0,1},{1,2},{2,3},{3,4},{4,5},{5,6},{6,7},{7,8},{8,9},{9,10},{10,1... | collective-permute-start | bytes 786440 | tf_op jit(solution)/shard_map/ppermute | solution.py:66
  18.1 16.5 %collective-permute-start.1 = (bf16[512,256]{1,0:T(8,128)(2,1)}, bf16[512,256]{1,0:T(8,128)(2,1)}, u32[]{:S(2)}, u32[]{:S(2)}) collective-permute-start(bf16[512,256]{1,0:T(8,128)(2,1)} %param.11), channel_id=1, source_target_pairs={{0,15},{1,0},{2,1},{3,2},{4,3},{5,4},{6,5},{7,6},{8,7},{9,8},{10,9... | collective-permute-start | bytes 786440 | tf_op jit(solution)/shard_map/ppermute | solution.py:69
  26.9 15.3 %all-to-all-start = ((s32[32,1,128]{2,1,0:T(1,128)}), s32[32,1,128]{2,1,0:T(1,128)S(1)}, u32[]{:S(2)}, u32[]{:S(2)}) async-start(s32[32,1,128]{2,1,0:T(1,128)} %bitcast.5), calls=%async_computation.1 | async-start | bytes 32768 | tf_op jit(solution)/shard_map/all_to_all | solution.py:51
  30.8 23.2 %collective-permute-start.2 = (bf16[512,256]{1,0:T(8,128)(2,1)}, bf16[512,256]{1,0:T(8,128)(2,1)}, u32[]{:S(2)}, u32[]{:S(2)}) collective-permute-start(bf16[512,256]{1,0:T(8,128)(2,1)} %collective-permute-done), channel_id=1, source_target_pairs={{0,1},{1,2},{2,3},{3,4},{4,5},{5,6},{6,7},{7,8},{8,9},{9,10},{10,1... | collective-permute-start | bytes 786440 | tf_op jit(solution)/shard_map/ppermute | solution.py:66
  34.6 21.3 %collective-permute-start.3 = (bf16[512,256]{1,0:T(8,128)(2,1)}, bf16[512,256]{1,0:T(8,128)(2,1)S(1)}, u32[]{:S(2)}, u32[]{:S(2)}) collective-permute-start(bf16[512,256]{1,0:T(8,128)(2,1)} %collective-permute-done.1), channel_id=1, source_target_pairs={{0,15},{1,0},{2,1},{3,2},{4,3},{5,4},{6,5},{7,6},{8,7},{9,8},{10,9... | collective-permute-start | bytes 786440 | tf_op jit(solution)/shard_map/ppermute | solution.py:69
  46.4 80.2 %all-to-all-start.1 = ((bf16[32,128,256]{2,1,0:T(8,128)(2,1)}), bf16[32,128,256]{2,1,0:T(8,128)(2,1)}, u32[]{:S(2)}, u32[]{:S(2)}) async-start(bf16[32,128,256]{2,1,0:T(8,128)(2,1)} %bitcast.41), calls=%async_computation.2 | async-start | bytes 4194304 | tf_op jit(solution)/shard_map/all_to_all | solution.py:53
  54.0 17.9 %collective-permute-start.4 = (bf16[512,256]{1,0:T(8,128)(2,1)}, bf16[512,256]{1,0:T(8,128)(2,1)}, u32[]{:S(2)}, u32[]{:S(2)}) collective-permute-start(bf16[512,256]{1,0:T(8,128)(2,1)} %collective-permute-done.2), channel_id=1, source_target_pairs={{0,1},{1,2},{2,3},{3,4},{4,5},{5,6},{6,7},{7,8},{8,9},{9,10},{10,1... | collective-permute-start | bytes 786440 | tf_op jit(solution)/shard_map/ppermute | solution.py:66
  55.9 19.5 %collective-permute-start.5 = (bf16[512,256]{1,0:T(8,128)(2,1)S(1)}, bf16[512,256]{1,0:T(8,128)(2,1)}, u32[]{:S(2)}, u32[]{:S(2)}) collective-permute-start(bf16[512,256]{1,0:T(8,128)(2,1)S(1)} %collective-permute-done.3), channel_id=1, source_target_pairs={{0,15},{1,0},{2,1},{3,2},{4,3},{5,4},{6,5},{7,6},{8,7},{9,8},{10,9... | collective-permute-start | bytes 786440 | tf_op jit(solution)/shard_map/ppermute | solution.py:69
  71.8 17.1 %collective-permute-start.6 = (bf16[512,256]{1,0:T(8,128)(2,1)}, bf16[512,256]{1,0:T(8,128)(2,1)S(1)}, u32[]{:S(2)}, u32[]{:S(2)}) collective-permute-start(bf16[512,256]{1,0:T(8,128)(2,1)} %collective-permute-done.4), channel_id=1, source_target_pairs={{0,1},{1,2},{2,3},{3,4},{4,5},{5,6},{6,7},{7,8},{8,9},{9,10},{10,1... | collective-permute-start | bytes 786440 | tf_op jit(solution)/shard_map/ppermute | solution.py:66
  75.4 16.2 %collective-permute-start.7 = (bf16[512,256]{1,0:T(8,128)(2,1)}, bf16[512,256]{1,0:T(8,128)(2,1)S(1)}, u32[]{:S(2)}, u32[]{:S(2)}) collective-permute-start(bf16[512,256]{1,0:T(8,128)(2,1)} %collective-permute-done.5), channel_id=1, source_target_pairs={{0,15},{1,0},{2,1},{3,2},{4,3},{5,4},{6,5},{7,6},{8,7},{9,8},{10,9... | collective-permute-start | bytes 786440 | tf_op jit(solution)/shard_map/ppermute | solution.py:69
  88.9 16.7 %collective-permute-start.8 = (bf16[512,256]{1,0:T(8,128)(2,1)S(1)}, bf16[512,256]{1,0:T(8,128)(2,1)S(1)}, u32[]{:S(2)}, u32[]{:S(2)}) collective-permute-start(bf16[512,256]{1,0:T(8,128)(2,1)S(1)} %collective-permute-done.6), channel_id=1, source_target_pairs={{0,1},{1,2},{2,3},{3,4},{4,5},{5,6},{6,7},{7,8},{8,9},{9,10},{10,1... | collective-permute-start | bytes 786440 | tf_op jit(solution)/shard_map/ppermute | solution.py:66
  91.6 16.7 %collective-permute-start.9 = (bf16[512,256]{1,0:T(8,128)(2,1)S(1)}, bf16[512,256]{1,0:T(8,128)(2,1)S(1)}, u32[]{:S(2)}, u32[]{:S(2)}) collective-permute-start(bf16[512,256]{1,0:T(8,128)(2,1)S(1)} %collective-permute-done.7), channel_id=1, source_target_pairs={{0,15},{1,0},{2,1},{3,2},{4,3},{5,4},{6,5},{7,6},{8,7},{9,8},{10,9... | collective-permute-start | bytes 786440 | tf_op jit(solution)/shard_map/ppermute | solution.py:69
  105.6 8.7 %collective-permute-start.10 = (bf16[512,256]{1,0:T(8,128)(2,1)S(1)}, bf16[512,256]{1,0:T(8,128)(2,1)S(1)}, u32[]{:S(2)}, u32[]{:S(2)}) collective-permute-start(bf16[512,256]{1,0:T(8,128)(2,1)S(1)} %collective-permute-done.8), channel_id=1, source_target_pairs={{0,1},{1,2},{2,3},{3,4},{4,5},{5,6},{6,7},{7,8},{8,9},{9,10},{10,1... | collective-permute-start | bytes 786440 | tf_op jit(solution)/shard_map/ppermute | solution.py:66
  108.3 8.9 %collective-permute-start.11 = (bf16[512,256]{1,0:T(8,128)(2,1)S(1)}, bf16[512,256]{1,0:T(8,128)(2,1)S(1)}, u32[]{:S(2)}, u32[]{:S(2)}) collective-permute-start(bf16[512,256]{1,0:T(8,128)(2,1)S(1)} %collective-permute-done.9), channel_id=1, source_target_pairs={{0,15},{1,0},{2,1},{3,2},{4,3},{5,4},{6,5},{7,6},{8,7},{9,8},{10,9... | collective-permute-start | bytes 786440 | tf_op jit(solution)/shard_map/ppermute | solution.py:69
  114.3 8.7 %collective-permute-start.12 = (bf16[512,256]{1,0:T(8,128)(2,1)S(1)}, bf16[512,256]{1,0:T(8,128)(2,1)S(1)}, u32[]{:S(2)}, u32[]{:S(2)}) collective-permute-start(bf16[512,256]{1,0:T(8,128)(2,1)S(1)} %collective-permute-done.10), channel_id=1, source_target_pairs={{0,1},{1,2},{2,3},{3,4},{4,5},{5,6},{6,7},{7,8},{8,9},{9,10},{10,1... | collective-permute-start | bytes 786440 | tf_op jit(solution)/shard_map/ppermute | solution.py:66
  117.2 8.6 %collective-permute-start.13 = (bf16[512,256]{1,0:T(8,128)(2,1)S(1)}, bf16[512,256]{1,0:T(8,128)(2,1)S(1)}, u32[]{:S(2)}, u32[]{:S(2)}) collective-permute-start(bf16[512,256]{1,0:T(8,128)(2,1)S(1)} %collective-permute-done.11), channel_id=1, source_target_pairs={{0,15},{1,0},{2,1},{3,2},{4,3},{5,4},{6,5},{7,6},{8,7},{9,8},{10,9... | collective-permute-start | bytes 786440 | tf_op jit(solution)/shard_map/ppermute | solution.py:69
  123.0 14.6 %collective-permute-start.14 = (bf16[512,256]{1,0:T(8,128)(2,1)S(1)}, bf16[512,256]{1,0:T(8,128)(2,1)}, u32[]{:S(2)}, u32[]{:S(2)}) collective-permute-start(bf16[512,256]{1,0:T(8,128)(2,1)S(1)} %collective-permute-done.12), channel_id=1, source_target_pairs={{0,1},{1,2},{2,3},{3,4},{4,5},{5,6},{6,7},{7,8},{8,9},{9,10},{10,1... | collective-permute-start | bytes 786440 | tf_op jit(solution)/shard_map/ppermute | solution.py:66
  142.1 26.3 %all-to-all-start.2 = ((f32[16,512,4]{1,2,0:T(4,128)}), f32[16,512,4]{1,2,0:T(4,128)S(1)}, u32[]{:S(2)}, u32[]{:S(2)}) async-start(f32[16,512,4]{1,2,0:T(4,128)} %broadcast_in_dim.5), calls=%async_computation.3 | async-start | bytes 262144 | tf_op jit(solution)/shard_map/all_to_all | solution.py:79
  160.7 19.4 %copy-start.1 = (s32[512,4]{0,1:T(4,128)S(1)}, s32[512,4]{0,1:T(4,128)}, u32[]{:S(2)}) copy-start(s32[512,4]{0,1:T(4,128)} %param.13) | copy-start | bytes 24580
  172.6 37.3 %all-to-all-start.3 = ((bf16[32,128,256]{2,1,0:T(8,128)(2,1)}), bf16[32,128,256]{2,1,0:T(8,128)(2,1)S(1)}, u32[]{:S(2)}, u32[]{:S(2)}) async-start(bf16[32,128,256]{2,1,0:T(8,128)(2,1)} %bitcast.43), calls=%async_computation.4 | async-start | bytes 4194304 | tf_op jit(solution)/shard_map/all_to_all | solution.py:82
Sparse Core Ops, SparseCore 0:
  14.4 95.8 reduce-scatter.1

commit v6 on v4

--- a/solution.py
+++ b/solution.py
@@ -25,13 +25,16 @@
     local_blocks, nblocks = block_mask.shape
     side = e_local // local_blocks
     doc_shard = old_index.shape[0]
-    query = jnp.dot(trunk_out, projection, preferred_element_type=jnp.float32).astype(jnp.bfloat16)
     blocks = transform.reshape(local_blocks, side, nblocks, side)
     masked = (blocks * block_mask[:, None, :, None].astype(jnp.bfloat16)).reshape(e_local, width)
-    term = jnp.dot(query, masked, preferred_element_type=jnp.float32)
-    new = lax.psum_scatter(
-        term.astype(jnp.bfloat16), "wide", scatter_dimension=1, tiled=True
-    ).astype(jnp.float32)
+
+    dmodel = trunk_out.shape[1]
+    chunk = dmodel // n_dp
+    proj_rows = lax.dynamic_slice_in_dim(projection, lax.axis_index("dp") * chunk, chunk, 0)
+    w_part = jnp.dot(proj_rows, masked, preferred_element_type=jnp.float32)
+    w_blk = lax.psum_scatter(w_part, "wide", scatter_dimension=1, tiled=True)
+    w_cols = lax.all_gather(w_blk.astype(jnp.bfloat16), "dp", axis=0, tiled=True)
+    new = jnp.dot(trunk_out, w_cols, preferred_element_type=jnp.float32)
 
     flat = doc_ids.reshape(-1)
     count = flat.shape[0]

time: 216 us -> 254 us (1.18)
  the two profiles are of different devices: /device:TPU:32 before, /device:TPU:6 now
where the time goes in v6:
time: 254 us; the launch traced here: 249 us
  starting transfers between devices  87.7 us (35%)
  waiting for transfers between devices  44.9 us (18%)
  matrix products  36.1 us (14%)
  local copies, waits for them, and re-layouts  35.8 us (14%)
  blocking collectives  24.5 us (10%)
  between operations  14.4 us (6%)
  other arithmetic  5.72 us (2%)
    ppermute x7, starting transfers between devices, local(): to_left = lax.ppermute(to_left, 'wide', left)  39.5 us
    dot_general x4, matrix products, pick_rows(): jnp.dot(one_hot(index, table.shape[0]), table, preferred_element_type=jnp...  28.8 us
    all_gather x1, blocking collectives, local(): lax.all_gather(w_blk.astype(jnp.bfloat16), 'dp', axis=0, tiled=True)  24.5 us
    all_to_all x1, waiting for transfers between devices, local(): lax.all_to_all(served_g, 'dp', 0, 0, tiled=True)  23.8 us
    dynamic_update_slice x16, local copies, waits for them, and re-layouts, place(): return lax.dynamic_update_slice_in_dim(full, block, source * e_local, 1)  23.5 us
    ppermute x8, starting transfers between devices, local(): to_right = lax.ppermute(to_right, 'wide', right)  18.3 us
    reduce_scatter x1, waiting for transfers between devices, local(): w_blk = lax.psum_scatter(w_part, 'wide', scatter_dimension=1, tiled=True)  16.1 us
    all_to_all x1, starting transfers between devices, local(): gathered = lax.all_to_all(spread, 'wide', 0, 0, tiled=True)  9.1 us
  transfers between devices with their start and end apart: 20, of which 4 were waited for; matrix products, arithmetic and copies ran while one was open for 27% of the time, Pallas kernels for 0%

profile of v6, /device:TPU:6, one launch (start us, length us, event | category | flops | bytes accessed | tf_op | source)
XLA Modules:
  0.0 249.1 jit_solution(15862489214082232437)
XLA Ops:
  7.2 4.0 %collective-permute-start = (bf16[512,256]{1,0:T(8,128)(2,1)}, bf16[512,256]{1,0:T(8,128)(2,1)}, u32[]{:S(2)}, u32[]{:S(2)}) collective-permute-start(bf16[512,256]{1,0:T(8,128)(2,1)} %param.11), channel_id=1, source_target_pairs={{0,1},{1,2},{2,3},{3,4},{4,5},{5,6},{6,7},{7,8},{8,9},{9,10},{10,1... | collective-permute-start | bytes 786440 | tf_op jit(solution)/shard_map/ppermute | solution.py:69
  11.2 9.5 %collective-permute-start.1 = (bf16[512,256]{1,0:T(8,128)(2,1)}, bf16[512,256]{1,0:T(8,128)(2,1)}, u32[]{:S(2)}, u32[]{:S(2)}) collective-permute-start(bf16[512,256]{1,0:T(8,128)(2,1)} %param.11), channel_id=1, source_target_pairs={{0,15},{1,0},{2,1},{3,2},{4,3},{5,4},{6,5},{7,6},{8,7},{9,8},{10,9... | collective-permute-start | bytes 786440 | tf_op jit(solution)/shard_map/ppermute | solution.py:72
  24.7 7.6 %all-to-all-start = ((s32[32,1,128]{2,1,0:T(1,128)}), s32[32,1,128]{2,1,0:T(1,128)S(1)}, u32[]{:S(2)}, u32[]{:S(2)}) async-start(s32[32,1,128]{2,1,0:T(1,128)} %bitcast.6), calls=%async_computation.1 | async-start | bytes 32768 | tf_op jit(solution)/shard_map/all_to_all | solution.py:54
  32.7 3.4 %fusion.18 = f32[32,4096]{1,0:T(8,128)} fusion(bf16[256,4096]{1,0:T(8,128)(2,1)} %param.9, bf16[32,8,32,128]{3,2,1,0:T(8,128)(2,1)S(1)} %bitcast.40, bf16[1024,256]{1,0:T(8,128)(2,1)} %param.8, s32[]{:T(128)S(6)} %select_n.166), kind=kOutput, calls=%fused_computation.26 | convolution fusion | flops 68157440 | bytes 4734980 | tf_op jit(solution)/shard_map/dot_general | solution.py:34
  36.1 2.5 broadcast_in_dim.5
  39.3 1.9 collective-permute-start.2
  41.3 5.1 %collective-permute-start.3 = (bf16[512,256]{1,0:T(8,128)(2,1)}, bf16[512,256]{1,0:T(8,128)(2,1)}, u32[]{:S(2)}, u32[]{:S(2)}) collective-permute-start(bf16[512,256]{1,0:T(8,128)(2,1)} %collective-permute-done.1), channel_id=1, source_target_pairs={{0,15},{1,0},{2,1},{3,2},{4,3},{5,4},{6,5},{7,6},{8,7},{9,8},{10,9... | collective-permute-start | bytes 786440 | tf_op jit(solution)/shard_map/ppermute | solution.py:72
  46.4 3.3 %fusion.7 = bf16[4096,256]{1,0:T(8,128)(2,1)} fusion(bf16[512,256]{1,0:T(8,128)(2,1)S(1)} %copy-done.1, s32[4096]{0:T(1024)S(1)} %bitcast.45), kind=kOutput, calls=%fused_computation.10 | convolution fusion | flops 1076887552 | bytes 2375680 | tf_op jit(solution)/shard_map/dot_general | solution.py:18
  49.7 7.4 %all-to-all-start.1 = ((bf16[32,128,256]{2,1,0:T(8,128)(2,1)}), bf16[32,128,256]{2,1,0:T(8,128)(2,1)}, u32[]{:S(2)}, u32[]{:S(2)}) async-start(bf16[32,128,256]{2,1,0:T(8,128)(2,1)} %bitcast.42), calls=%async_computation.2 | async-start | bytes 4194304 | tf_op jit(solution)/shard_map/all_to_all | solution.py:56
  57.2 1.9 collective-permute-start.4
  59.1 5.1 %collective-permute-start.5 = (bf16[512,256]{1,0:T(8,128)(2,1)}, bf16[512,256]{1,0:T(8,128)(2,1)S(1)}, u32[]{:S(2)}, u32[]{:S(2)}) collective-permute-start(bf16[512,256]{1,0:T(8,128)(2,1)} %collective-permute-done.3), channel_id=1, source_target_pairs={{0,15},{1,0},{2,1},{3,2},{4,3},{5,4},{6,5},{7,6},{8,7},{9,8},{10,9... | collective-permute-start | bytes 786440 | tf_op jit(solution)/shard_map/ppermute | solution.py:72
  69.5 1.9 collective-permute-start.6
  71.4 5.1 %collective-permute-start.7 = (bf16[512,256]{1,0:T(8,128)(2,1)S(1)}, bf16[512,256]{1,0:T(8,128)(2,1)}, u32[]{:S(2)}, u32[]{:S(2)}) collective-permute-start(bf16[512,256]{1,0:T(8,128)(2,1)S(1)} %collective-permute-done.5), channel_id=1, source_target_pairs={{0,15},{1,0},{2,1},{3,2},{4,3},{5,4},{6,5},{7,6},{8,7},{9,8},{10,9... | collective-permute-start | bytes 786440 | tf_op jit(solution)/shard_map/ppermute | solution.py:72
  81.2 1.9 collective-permute-start.8
  83.1 5.1 %collective-permute-start.9 = (bf16[512,256]{1,0:T(8,128)(2,1)}, bf16[512,256]{1,0:T(8,128)(2,1)}, u32[]{:S(2)}, u32[]{:S(2)}) collective-permute-start(bf16[512,256]{1,0:T(8,128)(2,1)} %collective-permute-done.7), channel_id=1, source_target_pairs={{0,15},{1,0},{2,1},{3,2},{4,3},{5,4},{6,5},{7,6},{8,7},{9,8},{10,9... | collective-permute-start | bytes 786440 | tf_op jit(solution)/shard_map/ppermute | solution.py:72
  88.3 16.1 %reduce-scatter.2.cloned.1.call-done = f32[32,256]{1,0:T(8,128)} async-done(((f32[32,4096]{1,0:T(8,128)}), f32[32,256]{1,0:T(8,128)}) %reduce-scatter.2.cloned.1.call-update) | async-done | bytes 32784 | tf_op jit(solution)/shard_map/reduce_scatter | solution.py:35
  105.1 24.5 %all_gather.3 = bf16[1024,256]{1,0:T(8,128)(2,1)S(1)} all-gather(bf16[32,256]{1,0:T(8,128)(2,1)S(1)} %convert_element_type.63), channel_id=1, replica_groups=mesh['dp'=32,'wide'=16] {'dp'}, dimensions={0}, use_global_device_ids=true | all-gather | bytes 540672 | tf_op jit(solution)/shard_map/all_gather | solution.py:36
  130.9 2.7 %collective-permute-start.10 = (bf16[512,256]{1,0:T(8,128)(2,1)}, bf16[512,256]{1,0:T(8,128)(2,1)}, u32[]{:S(2)}, u32[]{:S(2)}) collective-permute-start(bf16[512,256]{1,0:T(8,128)(2,1)} %collective-permute-done.8), channel_id=1, source_target_pairs={{0,1},{1,2},{2,3},{3,4},{4,5},{5,6},{6,7},{7,8},{8,9},{9,10},{10,1... | collective-permute-start | bytes 786440 | tf_op jit(solution)/shard_map/ppermute | solution.py:69
  135.3 4.4 %collective-permute-start.11 = (bf16[512,256]{1,0:T(8,128)(2,1)}, bf16[512,256]{1,0:T(8,128)(2,1)}, u32[]{:S(2)}, u32[]{:S(2)}) collective-permute-start(bf16[512,256]{1,0:T(8,128)(2,1)} %collective-permute-done.9), channel_id=1, source_target_pairs={{0,15},{1,0},{2,1},{3,2},{4,3},{5,4},{6,5},{7,6},{8,7},{9,8},{10,9... | collective-permute-start | bytes 786440 | tf_op jit(solution)/shard_map/ppermute | solution.py:72
  141.4 2.1 copy.26
  145.2 1.9 collective-permute-start.12
  148.8 5.1 %collective-permute-start.13 = (bf16[512,256]{1,0:T(8,128)(2,1)}, bf16[512,256]{1,0:T(8,128)(2,1)S(1)}, u32[]{:S(2)}, u32[]{:S(2)}) collective-permute-start(bf16[512,256]{1,0:T(8,128)(2,1)} %collective-permute-done.11), channel_id=1, source_target_pairs={{0,15},{1,0},{2,1},{3,2},{4,3},{5,4},{6,5},{7,6},{8,7},{9,8},{10,9... | collective-permute-start | bytes 786440 | tf_op jit(solution)/shard_map/ppermute | solution.py:72
  157.3 2.1 collective-permute-start.14
  161.9 8.8 %fusion.11 = bf16[2048,256]{1,0:T(8,128)(2,1)} fusion(bf16[4096,256]{1,0:T(8,128)(2,1)} %bitcast.9, s32[2048]{0:T(1024)S(1)} %multiply_add_fusion), kind=kOutput, calls=%fused_computation.14 | convolution fusion | flops 4303880192 | bytes 3153920 | tf_op jit(solution)/shard_map/dot_general | solution.py:18
  170.6 2.1 reshape.272
  172.8 2.7 %multiply_reduce_fusion = f32[512,4]{1,0:T(8,128)} fusion(f32[512,256]{1,0:T(8,128)} %copy.26, bf16[512,4,256]{2,1,0:T(4,128)(2,1)} %reshape.272), kind=kLoop, calls=%fused_computation.18 | loop fusion | flops 1570816 | bytes 1581056
  177.3 9.1 %all-to-all-start.2 = ((f32[16,512,4]{1,2,0:T(4,128)}), f32[16,512,4]{1,2,0:T(4,128)S(1)}, u32[]{:S(2)}, u32[]{:S(2)}) async-start(f32[16,512,4]{1,2,0:T(4,128)} %broadcast_in_dim.4), calls=%async_computation.3 | async-start | bytes 262144 | tf_op jit(solution)/shard_map/all_to_all | solution.py:85
  188.1 8.8 %fusion.8 = bf16[4096,256]{1,0:T(8,128)(2,1)} fusion(s32[4096]{0:T(1024)S(1)} %bitcast.46, bf16[512,4096]{1,0:T(8,128)(2,1)} %constant_dynamic-update-slice_fusion, bf16[256,4096]{1,0:T(8,128)(2,1)} %param.9, bf16[32,8,32,128]{3,2,1,0:T(8,128)(2,1)S(1)} %bitcast.41), kind=kOutput, calls=%fused_computation.11 | convolution fusion | flops 2151809024 | bytes 10502144 | tf_op jit(solution)/shard_map/dot_general | solution.py:18
  196.9 3.4 %all-to-all-done.2 = f32[16,512,4]{1,2,0:T(4,128)S(1)} async-done(((f32[16,512,4]{1,2,0:T(4,128)}), f32[16,512,4]{1,2,0:T(4,128)S(1)}, u32[]{:S(2)}, u32[]{:S(2)}) %all-to-all-start.2) | async-done | bytes 131104 | tf_op jit(solution)/shard_map/all_to_all | solution.py:85
  200.3 5.7 %all-to-all-start.3 = ((bf16[32,128,256]{2,1,0:T(8,128)(2,1)}), bf16[32,128,256]{2,1,0:T(8,128)(2,1)S(1)}, u32[]{:S(2)}, u32[]{:S(2)}) async-start(bf16[32,128,256]{2,1,0:T(8,128)(2,1)} %bitcast.43), calls=%async_computation.4 | async-start | bytes 4194304 | tf_op jit(solution)/shard_map/all_to_all | solution.py:78
  207.8 23.8 %all-to-all-done.3 = bf16[32,128,256]{2,1,0:T(8,128)(2,1)S(1)} async-done(((bf16[32,128,256]{2,1,0:T(8,128)(2,1)}), bf16[32,128,256]{2,1,0:T(8,128)(2,1)S(1)}, u32[]{:S(2)}, u32[]{:S(2)}) %all-to-all-start.3) | async-done | bytes 2097184 | tf_op jit(solution)/shard_map/all_to_all | solution.py:78
  231.6 7.9 %fusion.12 = bf16[2048,256]{1,0:T(8,128)(2,1)} fusion(bf16[4096,256]{1,0:T(8,128)(2,1)S(1)} %bitcast.44, s32[2048]{0:T(1024)} %copy-done.3), kind=kOutput, calls=%fused_computation.15 | convolution fusion | flops 4303880192 | bytes 3153920 | tf_op jit(solution)/shard_map/dot_general | solution.py:18
  (72 shorter events, 37.7 us)
Async XLA Ops:
  7.2 122.4 %copy-start = (bf16[512,1024]{1,0:T(8,128)(2,1)S(1)}, bf16[512,1024]{1,0:T(8,128)(2,1)}, u32[]{:S(2)}) copy-start(bf16[512,1024]{1,0:T(8,128)(2,1)} %param.7) | copy-start | bytes 3145732
  7.2 25.1 %copy-start.4 = (s32[2,32]{1,0:T(2,128)S(1)}, s32[2,32]{1,0:T(2,128)}, u32[]{:S(2)}) copy-start(s32[2,32]{1,0:T(2,128)} %param.10) | copy-start | bytes 772
  7.2 32.1 %collective-permute-start = (bf16[512,256]{1,0:T(8,128)(2,1)}, bf16[512,256]{1,0:T(8,128)(2,1)}, u32[]{:S(2)}, u32[]{:S(2)}) collective-permute-start(bf16[512,256]{1,0:T(8,128)(2,1)} %param.11), channel_id=1, source_target_pairs={{0,1},{1,2},{2,3},{3,4},{4,5},{5,6},{6,7},{7,8},{8,9},{9,10},{10,1... | collective-permute-start | bytes 786440 | tf_op jit(solution)/shard_map/ppermute | solution.py:69
  11.2 30.1 %collective-permute-start.1 = (bf16[512,256]{1,0:T(8,128)(2,1)}, bf16[512,256]{1,0:T(8,128)(2,1)}, u32[]{:S(2)}, u32[]{:S(2)}) collective-permute-start(bf16[512,256]{1,0:T(8,128)(2,1)} %param.11), channel_id=1, source_target_pairs={{0,15},{1,0},{2,1},{3,2},{4,3},{5,4},{6,5},{7,6},{8,7},{9,8},{10,9... | collective-permute-start | bytes 786440 | tf_op jit(solution)/shard_map/ppermute | solution.py:72
  24.7 21.7 %all-to-all-start = ((s32[32,1,128]{2,1,0:T(1,128)}), s32[32,1,128]{2,1,0:T(1,128)S(1)}, u32[]{:S(2)}, u32[]{:S(2)}) async-start(s32[32,1,128]{2,1,0:T(1,128)} %bitcast.6), calls=%async_computation.1 | async-start | bytes 32768 | tf_op jit(solution)/shard_map/all_to_all | solution.py:54
  32.2 72.1 %reduce-scatter.2.cloned.1.call-start = ((), (), s32[]{:S(2)}) async-start(), calls=%async_computation.5 | async-start | bytes 557056 | tf_op jit(solution)/shard_map/reduce_scatter | solution.py:35
  32.7 5.9 %copy-start.1 = (bf16[512,256]{1,0:T(8,128)(2,1)S(1)}, bf16[512,256]{1,0:T(8,128)(2,1)}, u32[]{:S(2)}) copy-start(bf16[512,256]{1,0:T(8,128)(2,1)} %param.11) | copy-start | bytes 786436
  36.1 125.8 %copy-start.3 = (s32[2048]{0:T(1024)}, s32[2048]{0:T(1024)S(1)}, u32[]{:S(2)}) copy-start(s32[2048]{0:T(1024)S(1)} %multiply_add_fusion) | copy-start | bytes 24580
  39.3 17.9 %collective-permute-start.2 = (bf16[512,256]{1,0:T(8,128)(2,1)}, bf16[512,256]{1,0:T(8,128)(2,1)}, u32[]{:S(2)}, u32[]{:S(2)}) collective-permute-start(bf16[512,256]{1,0:T(8,128)(2,1)} %collective-permute-done), channel_id=1, source_target_pairs={{0,1},{1,2},{2,3},{3,4},{4,5},{5,6},{6,7},{7,8},{8,9},{9,10},{10,1... | collective-permute-start | bytes 786440 | tf_op jit(solution)/shard_map/ppermute | solution.py:69
  41.3 17.9 %collective-permute-start.3 = (bf16[512,256]{1,0:T(8,128)(2,1)}, bf16[512,256]{1,0:T(8,128)(2,1)}, u32[]{:S(2)}, u32[]{:S(2)}) collective-permute-start(bf16[512,256]{1,0:T(8,128)(2,1)} %collective-permute-done.1), channel_id=1, source_target_pairs={{0,15},{1,0},{2,1},{3,2},{4,3},{5,4},{6,5},{7,6},{8,7},{9,8},{10,9... | collective-permute-start | bytes 786440 | tf_op jit(solution)/shard_map/ppermute | solution.py:72
  49.7 112.1 %all-to-all-start.1 = ((bf16[32,128,256]{2,1,0:T(8,128)(2,1)}), bf16[32,128,256]{2,1,0:T(8,128)(2,1)}, u32[]{:S(2)}, u32[]{:S(2)}) async-start(bf16[32,128,256]{2,1,0:T(8,128)(2,1)} %bitcast.42), calls=%async_computation.2 | async-start | bytes 4194304 | tf_op jit(solution)/shard_map/all_to_all | solution.py:56
  57.2 12.3 %collective-permute-start.4 = (bf16[512,256]{1,0:T(8,128)(2,1)}, bf16[512,256]{1,0:T(8,128)(2,1)S(1)}, u32[]{:S(2)}, u32[]{:S(2)}) collective-permute-start(bf16[512,256]{1,0:T(8,128)(2,1)} %collective-permute-done.2), channel_id=1, source_target_pairs={{0,1},{1,2},{2,3},{3,4},{4,5},{5,6},{6,7},{7,8},{8,9},{9,10},{10,1... | collective-permute-start | bytes 786440 | tf_op jit(solution)/shard_map/ppermute | solution.py:69
  59.1 12.3 %collective-permute-start.5 = (bf16[512,256]{1,0:T(8,128)(2,1)}, bf16[512,256]{1,0:T(8,128)(2,1)S(1)}, u32[]{:S(2)}, u32[]{:S(2)}) collective-permute-start(bf16[512,256]{1,0:T(8,128)(2,1)} %collective-permute-done.3), channel_id=1, source_target_pairs={{0,15},{1,0},{2,1},{3,2},{4,3},{5,4},{6,5},{7,6},{8,7},{9,8},{10,9... | collective-permute-start | bytes 786440 | tf_op jit(solution)/shard_map/ppermute | solution.py:72
  69.5 11.7 %collective-permute-start.6 = (bf16[512,256]{1,0:T(8,128)(2,1)S(1)}, bf16[512,256]{1,0:T(8,128)(2,1)}, u32[]{:S(2)}, u32[]{:S(2)}) collective-permute-start(bf16[512,256]{1,0:T(8,128)(2,1)S(1)} %collective-permute-done.4), channel_id=1, source_target_pairs={{0,1},{1,2},{2,3},{3,4},{4,5},{5,6},{6,7},{7,8},{8,9},{9,10},{10,1... | collective-permute-start | bytes 786440 | tf_op jit(solution)/shard_map/ppermute | solution.py:69
  71.4 11.7 %collective-permute-start.7 = (bf16[512,256]{1,0:T(8,128)(2,1)S(1)}, bf16[512,256]{1,0:T(8,128)(2,1)}, u32[]{:S(2)}, u32[]{:S(2)}) collective-permute-start(bf16[512,256]{1,0:T(8,128)(2,1)S(1)} %collective-permute-done.5), channel_id=1, source_target_pairs={{0,15},{1,0},{2,1},{3,2},{4,3},{5,4},{6,5},{7,6},{8,7},{9,8},{10,9... | collective-permute-start | bytes 786440 | tf_op jit(solution)/shard_map/ppermute | solution.py:72
  81.2 49.7 %collective-permute-start.8 = (bf16[512,256]{1,0:T(8,128)(2,1)}, bf16[512,256]{1,0:T(8,128)(2,1)}, u32[]{:S(2)}, u32[]{:S(2)}) collective-permute-start(bf16[512,256]{1,0:T(8,128)(2,1)} %collective-permute-done.6), channel_id=1, source_target_pairs={{0,1},{1,2},{2,3},{3,4},{4,5},{5,6},{6,7},{7,8},{8,9},{9,10},{10,1... | collective-permute-start | bytes 786440 | tf_op jit(solution)/shard_map/ppermute | solution.py:69
  83.1 52.2 %collective-permute-start.9 = (bf16[512,256]{1,0:T(8,128)(2,1)}, bf16[512,256]{1,0:T(8,128)(2,1)}, u32[]{:S(2)}, u32[]{:S(2)}) collective-permute-start(bf16[512,256]{1,0:T(8,128)(2,1)} %collective-permute-done.7), channel_id=1, source_target_pairs={{0,15},{1,0},{2,1},{3,2},{4,3},{5,4},{6,5},{7,6},{8,7},{9,8},{10,9... | collective-permute-start | bytes 786440 | tf_op jit(solution)/shard_map/ppermute | solution.py:72
  130.9 14.3 %collective-permute-start.10 = (bf16[512,256]{1,0:T(8,128)(2,1)}, bf16[512,256]{1,0:T(8,128)(2,1)}, u32[]{:S(2)}, u32[]{:S(2)}) collective-permute-start(bf16[512,256]{1,0:T(8,128)(2,1)} %collective-permute-done.8), channel_id=1, source_target_pairs={{0,1},{1,2},{2,3},{3,4},{4,5},{5,6},{6,7},{7,8},{8,9},{9,10},{10,1... | collective-permute-start | bytes 786440 | tf_op jit(solution)/shard_map/ppermute | solution.py:69
  135.3 13.5 %collective-permute-start.11 = (bf16[512,256]{1,0:T(8,128)(2,1)}, bf16[512,256]{1,0:T(8,128)(2,1)}, u32[]{:S(2)}, u32[]{:S(2)}) collective-permute-start(bf16[512,256]{1,0:T(8,128)(2,1)} %collective-permute-done.9), channel_id=1, source_target_pairs={{0,15},{1,0},{2,1},{3,2},{4,3},{5,4},{6,5},{7,6},{8,7},{9,8},{10,9... | collective-permute-start | bytes 786440 | tf_op jit(solution)/shard_map/ppermute | solution.py:72
  145.2 12.1 %collective-permute-start.12 = (bf16[512,256]{1,0:T(8,128)(2,1)}, bf16[512,256]{1,0:T(8,128)(2,1)}, u32[]{:S(2)}, u32[]{:S(2)}) collective-permute-start(bf16[512,256]{1,0:T(8,128)(2,1)} %collective-permute-done.10), channel_id=1, source_target_pairs={{0,1},{1,2},{2,3},{3,4},{4,5},{5,6},{6,7},{7,8},{8,9},{9,10},{10,1... | collective-permute-start | bytes 786440 | tf_op jit(solution)/shard_map/ppermute | solution.py:69
  148.8 12.3 %collective-permute-start.13 = (bf16[512,256]{1,0:T(8,128)(2,1)}, bf16[512,256]{1,0:T(8,128)(2,1)S(1)}, u32[]{:S(2)}, u32[]{:S(2)}) collective-permute-start(bf16[512,256]{1,0:T(8,128)(2,1)} %collective-permute-done.11), channel_id=1, source_target_pairs={{0,15},{1,0},{2,1},{3,2},{4,3},{5,4},{6,5},{7,6},{8,7},{9,8},{10,9... | collective-permute-start | bytes 786440 | tf_op jit(solution)/shard_map/ppermute | solution.py:72
  157.3 29.0 %collective-permute-start.14 = (bf16[512,256]{1,0:T(8,128)(2,1)}, bf16[512,256]{1,0:T(8,128)(2,1)}, u32[]{:S(2)}, u32[]{:S(2)}) collective-permute-start(bf16[512,256]{1,0:T(8,128)(2,1)} %collective-permute-done.12), channel_id=1, source_target_pairs={{0,1},{1,2},{2,3},{3,4},{4,5},{5,6},{6,7},{7,8},{8,9},{9,10},{10,1... | collective-permute-start | bytes 786440 | tf_op jit(solution)/shard_map/ppermute | solution.py:69
  177.3 23.1 %all-to-all-start.2 = ((f32[16,512,4]{1,2,0:T(4,128)}), f32[16,512,4]{1,2,0:T(4,128)S(1)}, u32[]{:S(2)}, u32[]{:S(2)}) async-start(f32[16,512,4]{1,2,0:T(4,128)} %broadcast_in_dim.4), calls=%async_computation.3 | async-start | bytes 262144 | tf_op jit(solution)/shard_map/all_to_all | solution.py:85
  196.9 10.0 %copy-start.2 = (s32[512,4]{0,1:T(4,128)S(1)}, s32[512,4]{0,1:T(4,128)}, u32[]{:S(2)}) copy-start(s32[512,4]{0,1:T(4,128)} %param.13) | copy-start | bytes 24580
  200.3 31.3 %all-to-all-start.3 = ((bf16[32,128,256]{2,1,0:T(8,128)(2,1)}), bf16[32,128,256]{2,1,0:T(8,128)(2,1)S(1)}, u32[]{:S(2)}, u32[]{:S(2)}) async-start(bf16[32,128,256]{2,1,0:T(8,128)(2,1)} %bitcast.43), calls=%async_computation.4 | async-start | bytes 4194304 | tf_op jit(solution)/shard_map/all_to_all | solution.py:78
Sparse Core Ops, SparseCore 0:
  36.2 68.0 reduce-scatter.1

commit v7 on v4

--- a/solution.py
+++ b/solution.py
@@ -57,19 +57,22 @@
     right = [(i, (i + 1) % n_wide) for i in range(n_wide)]
     left = [(i, (i - 1) % n_wide) for i in range(n_wide)]
 
-    def place(full, block, source):
-        return lax.dynamic_update_slice_in_dim(full, block, source * e_local, 1)
-
-    old_full = place(jnp.zeros((doc_shard, width), old_index.dtype), old_index, me_w)
+    blocks = {0: old_index}
     to_right, to_left = old_index, old_index
     for step in range(1, n_wide // 2 + 1):
         to_right = lax.ppermute(to_right, "wide", right)
-        old_full = place(old_full, to_right, (me_w - step) % n_wide)
+        blocks[-step] = to_right
         if step < n_wide - n_wide // 2:
             to_left = lax.ppermute(to_left, "wide", left)
-            old_full = place(old_full, to_left, (me_w + step) % n_wide)
+            blocks[step] = to_left
+    offsets = sorted(blocks)
+    old_full = jnp.concatenate([blocks[o] for o in offsets], axis=1)
+    first = (me_w + offsets[0]) % n_wide
+    rotated = lax.dynamic_slice_in_dim(
+        jnp.concatenate([masked, masked], axis=1), first * e_local, width, 1
+    )
     g_own = lax.dot_general(
-        old_full, masked, (((1,), (1,)), ((), ())), preferred_element_type=jnp.float32
+        old_full, rotated, (((1,), (1,)), ((), ())), preferred_element_type=jnp.float32
     ).astype(jnp.bfloat16)
     served_g = pick_rows(asked, g_own).reshape(n_dp, CAP, e_local)
     back_g = lax.all_to_all(served_g, "dp", 0, 0, tiled=True).reshape(n_dp * CAP, e_local)

time: 216 us -> 236 us (1.093)
  waiting for transfers between devices: 39.9 us -> 77.5 us
  local copies, waits for them, and re-layouts: 26.6 us -> 18.2 us
  starting transfers between devices: 91.7 us -> 84.1 us
  matrix products: 39.4 us -> 35 us
    ppermute x8, waiting for transfers between devices: 12.9 us -> 46.1 us  [local(): to_right = lax.ppermute(to_right, 'wide', right)]
    dynamic_update_slice x16 -> x0, local copies, waits for them, and re-layouts: 18.7 us -> none  [place(): return lax.dynamic_update_slice_in_dim(full, block, source * e_local, 1)]
    unnamed x7 -> x32, local copies, waits for them, and re-layouts: 0.24 us -> 12.9 us
    all_to_all x1, waiting for transfers between devices: 0.01 us -> 6.99 us  [local(): lax.all_to_all(served, 'dp', 0, 0, tiled=True).reshape(n_dp * CAP, e_local)]
    dot_general x4, matrix products: 28.9 us -> 23.6 us  [pick_rows(): jnp.dot(one_hot(index, table.shape[0]), table, preferred_element_type=jnp...]
    ppermute x7, starting transfers between devices: 40.7 us -> 36.1 us  [local(): to_left = lax.ppermute(to_left, 'wide', left)]
    ppermute x7, waiting for transfers between devices: 6.09 us -> 2.27 us  [local(): to_left = lax.ppermute(to_left, 'wide', left)]
    all_to_all x1, starting transfers between devices: 7.65 us -> 4.19 us  [local(): lax.all_to_all(served_g, 'dp', 0, 0, tiled=True)]
  transfers between devices with their start and end apart: 20 -> 20, of which waited for: 8 -> 12; matrix products, arithmetic and copies ran while one was open for 27% -> 20% of each run, Pallas kernels for 0% -> 0%
where the time goes in v7:
time: 236 us; the launch traced here: 235 us
  starting transfers between devices  84.1 us (36%)
  waiting for transfers between devices  77.5 us (33%)
  matrix products  35 us (15%)
  local copies, waits for them, and re-layouts  18.2 us (8%)
  between operations  14.6 us (6%)
  other arithmetic  5.26 us (2%)
    ppermute x8, waiting for transfers between devices, local(): to_right = lax.ppermute(to_right, 'wide', right)  46.1 us
    ppermute x7, starting transfers between devices, local(): to_left = lax.ppermute(to_left, 'wide', left)  36.1 us
    dot_general x4, matrix products, pick_rows(): jnp.dot(one_hot(index, table.shape[0]), table, preferred_element_type=jnp...  23.6 us
    ppermute x8, starting transfers between devices, local(): to_right = lax.ppermute(to_right, 'wide', right)  17.3 us
    all_to_all x1, waiting for transfers between devices, local(): lax.all_to_all(served_g, 'dp', 0, 0, tiled=True)  16.7 us
    all_to_all x1, starting transfers between devices, local(): gathered = lax.all_to_all(spread, 'wide', 0, 0, tiled=True)  13.1 us
    unnamed x32, local copies, waits for them, and re-layouts  12.9 us
    all_to_all x1, starting transfers between devices, local(): asked = lax.all_to_all(req, 'dp', 0, 0, tiled=True).reshape(-1)  7.27 us
  transfers between devices with their start and end apart: 20, of which 12 were waited for; matrix products, arithmetic and copies ran while one was open for 20% of the time, Pallas kernels for 0%

profile of v7, /device:TPU:32, one launch (start us, length us, event | category | flops | bytes accessed | tf_op | source)
XLA Modules:
  0.0 234.6 jit_solution(16964740080782796713)
XLA Ops:
  8.3 2.3 bitcast_multiply_fusion
  10.6 5.0 %convolution_convert_fusion = bf16[512,4096]{1,0:T(8,128)(2,1)} fusion(bf16[256,4096]{1,0:T(8,128)(2,1)S(1)} %bitcast_multiply_fusion, bf16[512,1024]{1,0:T(8,128)(2,1)S(1)} %copy-done, bf16[1024,256]{1,0:T(8,128)(2,1)} %param.8), kind=kOutput, calls=%fused_computation.10 | convolution fusion | flops 1344405504 | bytes 7864320 | tf_op jit(solution)/shard_map/dot_general | solution.py:31
  15.7 3.8 %collective-permute-start = (bf16[512,256]{1,0:T(8,128)(2,1)}, bf16[512,256]{1,0:T(8,128)(2,1)}, u32[]{:S(2)}, u32[]{:S(2)}) collective-permute-start(bf16[512,256]{1,0:T(8,128)(2,1)} %param.11), channel_id=1, source_target_pairs={{0,1},{1,2},{2,3},{3,4},{4,5},{5,6},{6,7},{7,8},{8,9},{9,10},{10,1... | collective-permute-start | bytes 786440 | tf_op jit(solution)/shard_map/ppermute | solution.py:63
  19.5 8.2 %collective-permute-done = bf16[512,256]{1,0:T(8,128)(2,1)} collective-permute-done((bf16[512,256]{1,0:T(8,128)(2,1)}, bf16[512,256]{1,0:T(8,128)(2,1)}, u32[]{:S(2)}, u32[]{:S(2)}) %collective-permute-start) | collective-permute-done | bytes 262176 | tf_op jit(solution)/shard_map/ppermute | solution.py:63
  27.7 2.0 collective-permute-start.1
  29.8 7.9 %collective-permute-start.8 = (bf16[512,256]{1,0:T(8,128)(2,1)}, bf16[512,256]{1,0:T(8,128)(2,1)}, u32[]{:S(2)}, u32[]{:S(2)}) collective-permute-start(bf16[512,256]{1,0:T(8,128)(2,1)} %param.11), channel_id=1, source_target_pairs={{0,15},{1,0},{2,1},{3,2},{4,3},{5,4},{6,5},{7,6},{8,7},{9,8},{10,9... | collective-permute-start | bytes 786440 | tf_op jit(solution)/shard_map/ppermute | solution.py:66
  38.2 7.1 %collective-permute-done.1 = bf16[512,256]{1,0:T(8,128)(2,1)} collective-permute-done((bf16[512,256]{1,0:T(8,128)(2,1)}, bf16[512,256]{1,0:T(8,128)(2,1)}, u32[]{:S(2)}, u32[]{:S(2)}) %collective-permute-start.1) | collective-permute-done | bytes 262176 | tf_op jit(solution)/shard_map/ppermute | solution.py:63
  47.2 2.2 collective-permute-done.8
  49.4 4.4 %collective-permute-start.9 = (bf16[512,256]{1,0:T(8,128)(2,1)}, bf16[512,256]{1,0:T(8,128)(2,1)S(1)}, u32[]{:S(2)}, u32[]{:S(2)}) collective-permute-start(bf16[512,256]{1,0:T(8,128)(2,1)} %collective-permute-done.8), channel_id=1, source_target_pairs={{0,15},{1,0},{2,1},{3,2},{4,3},{5,4},{6,5},{7,6},{8,7},{9,8},{10,9... | collective-permute-start | bytes 786440 | tf_op jit(solution)/shard_map/ppermute | solution.py:66
  53.8 9.3 %collective-permute-done.2 = bf16[512,256]{1,0:T(8,128)(2,1)S(1)} collective-permute-done((bf16[512,256]{1,0:T(8,128)(2,1)}, bf16[512,256]{1,0:T(8,128)(2,1)S(1)}, u32[]{:S(2)}, u32[]{:S(2)}) %collective-permute-start.2) | collective-permute-done | bytes 262176 | tf_op jit(solution)/shard_map/ppermute | solution.py:63
  65.2 4.8 %collective-permute-start.10 = (bf16[512,256]{1,0:T(8,128)(2,1)S(1)}, bf16[512,256]{1,0:T(8,128)(2,1)S(1)}, u32[]{:S(2)}, u32[]{:S(2)}) collective-permute-start(bf16[512,256]{1,0:T(8,128)(2,1)S(1)} %collective-permute-done.9), channel_id=1, source_target_pairs={{0,15},{1,0},{2,1},{3,2},{4,3},{5,4},{6,5},{7,6},{8,7},{9,8},{10,9... | collective-permute-start | bytes 786440 | tf_op jit(solution)/shard_map/ppermute | solution.py:66
  70.0 8.7 %collective-permute-done.3 = bf16[512,256]{1,0:T(8,128)(2,1)S(1)} collective-permute-done((bf16[512,256]{1,0:T(8,128)(2,1)S(1)}, bf16[512,256]{1,0:T(8,128)(2,1)S(1)}, u32[]{:S(2)}, u32[]{:S(2)}) %collective-permute-start.3) | collective-permute-done | bytes 262176 | tf_op jit(solution)/shard_map/ppermute | solution.py:63
  80.7 4.9 %collective-permute-start.11 = (bf16[512,256]{1,0:T(8,128)(2,1)S(1)}, bf16[512,256]{1,0:T(8,128)(2,1)}, u32[]{:S(2)}, u32[]{:S(2)}) collective-permute-start(bf16[512,256]{1,0:T(8,128)(2,1)S(1)} %collective-permute-done.10), channel_id=1, source_target_pairs={{0,15},{1,0},{2,1},{3,2},{4,3},{5,4},{6,5},{7,6},{8,7},{9,8},{10,9... | collective-permute-start | bytes 786440 | tf_op jit(solution)/shard_map/ppermute | solution.py:66
  85.6 8.4 %collective-permute-done.4 = bf16[512,256]{1,0:T(8,128)(2,1)S(1)} collective-permute-done((bf16[512,256]{1,0:T(8,128)(2,1)S(1)}, bf16[512,256]{1,0:T(8,128)(2,1)S(1)}, u32[]{:S(2)}, u32[]{:S(2)}) %collective-permute-start.4) | collective-permute-done | bytes 262176 | tf_op jit(solution)/shard_map/ppermute | solution.py:63
  97.5 5.3 %collective-permute-start.12 = (bf16[512,256]{1,0:T(8,128)(2,1)}, bf16[512,256]{1,0:T(8,128)(2,1)}, u32[]{:S(2)}, u32[]{:S(2)}) collective-permute-start(bf16[512,256]{1,0:T(8,128)(2,1)} %collective-permute-done.11), channel_id=1, source_target_pairs={{0,15},{1,0},{2,1},{3,2},{4,3},{5,4},{6,5},{7,6},{8,7},{9,8},{10,9... | collective-permute-start | bytes 786440 | tf_op jit(solution)/shard_map/ppermute | solution.py:66
  102.8 4.3 %collective-permute-done.5 = bf16[512,256]{1,0:T(8,128)(2,1)} collective-permute-done((bf16[512,256]{1,0:T(8,128)(2,1)S(1)}, bf16[512,256]{1,0:T(8,128)(2,1)}, u32[]{:S(2)}, u32[]{:S(2)}) %collective-permute-start.5) | collective-permute-done | bytes 262176 | tf_op jit(solution)/shard_map/ppermute | solution.py:63
  110.2 7.3 %all-to-all-start = ((s32[32,1,128]{2,1,0:T(1,128)}), s32[32,1,128]{2,1,0:T(1,128)S(1)}, u32[]{:S(2)}, u32[]{:S(2)}) async-start(s32[32,1,128]{2,1,0:T(1,128)} %bitcast.5), calls=%async_computation.1 | async-start | bytes 32768 | tf_op jit(solution)/shard_map/all_to_all | solution.py:51
  117.5 3.9 %collective-permute-start.13 = (bf16[512,256]{1,0:T(8,128)(2,1)}, bf16[512,256]{1,0:T(8,128)(2,1)}, u32[]{:S(2)}, u32[]{:S(2)}) collective-permute-start(bf16[512,256]{1,0:T(8,128)(2,1)} %collective-permute-done.12), channel_id=1, source_target_pairs={{0,15},{1,0},{2,1},{3,2},{4,3},{5,4},{6,5},{7,6},{8,7},{9,8},{10,9... | collective-permute-start | bytes 786440 | tf_op jit(solution)/shard_map/ppermute | solution.py:66
  121.4 1.9 collective-permute-start.7
  124.8 4.3 %fusion.7 = bf16[4096,256]{1,0:T(8,128)(2,1)} fusion(bf16[512,256]{1,0:T(8,128)(2,1)} %param.11, s32[4096]{0:T(1024)S(1)} %bitcast.43), kind=kOutput, calls=%fused_computation.11 | convolution fusion | flops 1076887552 | bytes 2375680 | tf_op jit(solution)/shard_map/dot_general | solution.py:18
  129.1 6.1 %all-to-all-start.1 = ((bf16[32,128,256]{2,1,0:T(8,128)(2,1)}), bf16[32,128,256]{2,1,0:T(8,128)(2,1)}, u32[]{:S(2)}, u32[]{:S(2)}) async-start(bf16[32,128,256]{2,1,0:T(8,128)(2,1)} %bitcast.39), calls=%async_computation.2 | async-start | bytes 4194304 | tf_op jit(solution)/shard_map/all_to_all | solution.py:53
  135.2 4.9 %collective-permute-start.14 = (bf16[512,256]{1,0:T(8,128)(2,1)}, bf16[512,256]{1,0:T(8,128)(2,1)S(1)}, u32[]{:S(2)}, u32[]{:S(2)}) collective-permute-start(bf16[512,256]{1,0:T(8,128)(2,1)} %collective-permute-done.13), channel_id=1, source_target_pairs={{0,15},{1,0},{2,1},{3,2},{4,3},{5,4},{6,5},{7,6},{8,7},{9,8},{10,9... | collective-permute-start | bytes 786440 | tf_op jit(solution)/shard_map/ppermute | solution.py:66
  154.8 3.3 %fusion.8 = bf16[4096,256]{1,0:T(8,128)(2,1)} fusion(bf16[512,256]{1,0:T(8,128)(2,1)S(1)} %fusion.17, s32[4096]{0:T(1024)S(1)} %bitcast.44), kind=kOutput, calls=%fused_computation.12 | convolution fusion | flops 1076887552 | bytes 2375680 | tf_op jit(solution)/shard_map/dot_general | solution.py:18
  158.1 7.0 %all-to-all-done.1 = bf16[32,128,256]{2,1,0:T(8,128)(2,1)} async-done(((bf16[32,128,256]{2,1,0:T(8,128)(2,1)}), bf16[32,128,256]{2,1,0:T(8,128)(2,1)}, u32[]{:S(2)}, u32[]{:S(2)}) %all-to-all-start.1) | async-done | bytes 2097184 | tf_op jit(solution)/shard_map/all_to_all | solution.py:53
  165.1 4.2 %all-to-all-start.3 = ((bf16[32,128,256]{2,1,0:T(8,128)(2,1)}), bf16[32,128,256]{2,1,0:T(8,128)(2,1)S(1)}, u32[]{:S(2)}, u32[]{:S(2)}) async-start(bf16[32,128,256]{2,1,0:T(8,128)(2,1)} %bitcast.41), calls=%async_computation.4 | async-start | bytes 4194304 | tf_op jit(solution)/shard_map/all_to_all | solution.py:78
  169.4 8.7 %fusion.11 = bf16[2048,256]{1,0:T(8,128)(2,1)} fusion(bf16[4096,256]{1,0:T(8,128)(2,1)} %bitcast.8, s32[2048]{0:T(1024)S(1)} %multiply_add_fusion), kind=kOutput, calls=%fused_computation.17 | convolution fusion | flops 4303880192 | bytes 3153920 | tf_op jit(solution)/shard_map/dot_general | solution.py:18
  178.1 2.2 reshape.272
  180.3 2.0 fusion.27
  182.5 16.7 %all-to-all-done.3 = bf16[32,128,256]{2,1,0:T(8,128)(2,1)S(1)} async-done(((bf16[32,128,256]{2,1,0:T(8,128)(2,1)}), bf16[32,128,256]{2,1,0:T(8,128)(2,1)S(1)}, u32[]{:S(2)}, u32[]{:S(2)}) %all-to-all-start.3) | async-done | bytes 2097184 | tf_op jit(solution)/shard_map/all_to_all | solution.py:78
  199.8 13.1 %all-to-all-start.2 = ((f32[16,512,4]{1,2,0:T(4,128)}), f32[16,512,4]{1,2,0:T(4,128)S(1)}, u32[]{:S(2)}, u32[]{:S(2)}) async-start(f32[16,512,4]{1,2,0:T(4,128)} %broadcast_in_dim.2), calls=%async_computation.3 | async-start | bytes 262144 | tf_op jit(solution)/shard_map/all_to_all | solution.py:85
  212.9 7.2 %fusion.12 = bf16[2048,256]{1,0:T(8,128)(2,1)} fusion(bf16[4096,256]{1,0:T(8,128)(2,1)S(1)} %bitcast.40, s32[2048]{0:T(1024)S(1)} %multiply_add_fusion), kind=kOutput, calls=%fused_computation.18 | convolution fusion | flops 4303880192 | bytes 3153920 | tf_op jit(solution)/shard_map/dot_general | solution.py:18
  221.5 4.0 %all-to-all-done.2 = f32[16,512,4]{1,2,0:T(4,128)S(1)} async-done(((f32[16,512,4]{1,2,0:T(4,128)}), f32[16,512,4]{1,2,0:T(4,128)S(1)}, u32[]{:S(2)}, u32[]{:S(2)}) %all-to-all-start.2) | async-done | bytes 131104 | tf_op jit(solution)/shard_map/all_to_all | solution.py:85
  (74 shorter events, 34.5 us)
Async XLA Ops:
  7.2 3.4 %copy-start = (bf16[512,1024]{1,0:T(8,128)(2,1)S(1)}, bf16[512,1024]{1,0:T(8,128)(2,1)}, u32[]{:S(2)}) copy-start(bf16[512,1024]{1,0:T(8,128)(2,1)} %param.7) | copy-start | bytes 3145732
  7.2 173.2 %reduce-scatter.2.cloned.1.call-start = ((), (), s32[]{:S(2)}) async-start(), calls=%async_computation.5 | async-start | bytes 4456448 | tf_op jit(solution)/shard_map/reduce_scatter | solution.py:32
  10.6 27.0 %copy-start.7 = (s32[512,4]{0,1:T(4,128)S(1)}, s32[512,4]{0,1:T(4,128)}, u32[]{:S(2)}) copy-start(s32[512,4]{0,1:T(4,128)} %param.12) | copy-start | bytes 24580
  15.7 12.1 %collective-permute-start = (bf16[512,256]{1,0:T(8,128)(2,1)}, bf16[512,256]{1,0:T(8,128)(2,1)}, u32[]{:S(2)}, u32[]{:S(2)}) collective-permute-start(bf16[512,256]{1,0:T(8,128)(2,1)} %param.11), channel_id=1, source_target_pairs={{0,1},{1,2},{2,3},{3,4},{4,5},{5,6},{6,7},{7,8},{8,9},{9,10},{10,1... | collective-permute-start | bytes 786440 | tf_op jit(solution)/shard_map/ppermute | solution.py:63
  27.7 17.6 %collective-permute-start.1 = (bf16[512,256]{1,0:T(8,128)(2,1)}, bf16[512,256]{1,0:T(8,128)(2,1)}, u32[]{:S(2)}, u32[]{:S(2)}) collective-permute-start(bf16[512,256]{1,0:T(8,128)(2,1)} %collective-permute-done), channel_id=1, source_target_pairs={{0,1},{1,2},{2,3},{3,4},{4,5},{5,6},{6,7},{7,8},{8,9},{9,10},{10,1... | collective-permute-start | bytes 786440 | tf_op jit(solution)/shard_map/ppermute | solution.py:63
  29.8 19.7 %collective-permute-start.8 = (bf16[512,256]{1,0:T(8,128)(2,1)}, bf16[512,256]{1,0:T(8,128)(2,1)}, u32[]{:S(2)}, u32[]{:S(2)}) collective-permute-start(bf16[512,256]{1,0:T(8,128)(2,1)} %param.11), channel_id=1, source_target_pairs={{0,15},{1,0},{2,1},{3,2},{4,3},{5,4},{6,5},{7,6},{8,7},{9,8},{10,9... | collective-permute-start | bytes 786440 | tf_op jit(solution)/shard_map/ppermute | solution.py:66
  45.3 17.8 %collective-permute-start.2 = (bf16[512,256]{1,0:T(8,128)(2,1)}, bf16[512,256]{1,0:T(8,128)(2,1)S(1)}, u32[]{:S(2)}, u32[]{:S(2)}) collective-permute-start(bf16[512,256]{1,0:T(8,128)(2,1)} %collective-permute-done.1), channel_id=1, source_target_pairs={{0,1},{1,2},{2,3},{3,4},{4,5},{5,6},{6,7},{7,8},{8,9},{9,10},{10,1... | collective-permute-start | bytes 786440 | tf_op jit(solution)/shard_map/ppermute | solution.py:63
  49.4 15.8 %collective-permute-start.9 = (bf16[512,256]{1,0:T(8,128)(2,1)}, bf16[512,256]{1,0:T(8,128)(2,1)S(1)}, u32[]{:S(2)}, u32[]{:S(2)}) collective-permute-start(bf16[512,256]{1,0:T(8,128)(2,1)} %collective-permute-done.8), channel_id=1, source_target_pairs={{0,15},{1,0},{2,1},{3,2},{4,3},{5,4},{6,5},{7,6},{8,7},{9,8},{10,9... | collective-permute-start | bytes 786440 | tf_op jit(solution)/shard_map/ppermute | solution.py:66
  63.1 17.6 %copy-start.1 = (bf16[512,256]{1,0:T(8,128)(2,1)}, bf16[512,256]{1,0:T(8,128)(2,1)S(1)}, u32[]{:S(2)}) copy-start(bf16[512,256]{1,0:T(8,128)(2,1)S(1)} %collective-permute-done.2) | copy-start | bytes 786436
  63.1 15.6 %collective-permute-start.3 = (bf16[512,256]{1,0:T(8,128)(2,1)S(1)}, bf16[512,256]{1,0:T(8,128)(2,1)S(1)}, u32[]{:S(2)}, u32[]{:S(2)}) collective-permute-start(bf16[512,256]{1,0:T(8,128)(2,1)S(1)} %collective-permute-done.2), channel_id=1, source_target_pairs={{0,1},{1,2},{2,3},{3,4},{4,5},{5,6},{6,7},{7,8},{8,9},{9,10},{10,1... | collective-permute-start | bytes 786440 | tf_op jit(solution)/shard_map/ppermute | solution.py:63
  65.2 15.5 %collective-permute-start.10 = (bf16[512,256]{1,0:T(8,128)(2,1)S(1)}, bf16[512,256]{1,0:T(8,128)(2,1)S(1)}, u32[]{:S(2)}, u32[]{:S(2)}) collective-permute-start(bf16[512,256]{1,0:T(8,128)(2,1)S(1)} %collective-permute-done.9), channel_id=1, source_target_pairs={{0,15},{1,0},{2,1},{3,2},{4,3},{5,4},{6,5},{7,6},{8,7},{9,8},{10,9... | collective-permute-start | bytes 786440 | tf_op jit(solution)/shard_map/ppermute | solution.py:66
  78.8 15.3 %copy-start.4 = (bf16[512,256]{1,0:T(8,128)(2,1)}, bf16[512,256]{1,0:T(8,128)(2,1)S(1)}, u32[]{:S(2)}) copy-start(bf16[512,256]{1,0:T(8,128)(2,1)S(1)} %collective-permute-done.3) | copy-start | bytes 786436
  78.8 15.3 %collective-permute-start.4 = (bf16[512,256]{1,0:T(8,128)(2,1)S(1)}, bf16[512,256]{1,0:T(8,128)(2,1)S(1)}, u32[]{:S(2)}, u32[]{:S(2)}) collective-permute-start(bf16[512,256]{1,0:T(8,128)(2,1)S(1)} %collective-permute-done.3), channel_id=1, source_target_pairs={{0,1},{1,2},{2,3},{3,4},{4,5},{5,6},{6,7},{7,8},{8,9},{9,10},{10,1... | collective-permute-start | bytes 786440 | tf_op jit(solution)/shard_map/ppermute | solution.py:63
  80.7 4.9 %copy-start.2 = (bf16[512,256]{1,0:T(8,128)(2,1)}, bf16[512,256]{1,0:T(8,128)(2,1)S(1)}, u32[]{:S(2)}) copy-start(bf16[512,256]{1,0:T(8,128)(2,1)S(1)} %collective-permute-done.10) | copy-start | bytes 786436
  80.7 16.8 %collective-permute-start.11 = (bf16[512,256]{1,0:T(8,128)(2,1)S(1)}, bf16[512,256]{1,0:T(8,128)(2,1)}, u32[]{:S(2)}, u32[]{:S(2)}) collective-permute-start(bf16[512,256]{1,0:T(8,128)(2,1)S(1)} %collective-permute-done.10), channel_id=1, source_target_pairs={{0,15},{1,0},{2,1},{3,2},{4,3},{5,4},{6,5},{7,6},{8,7},{9,8},{10,9... | collective-permute-start | bytes 786440 | tf_op jit(solution)/shard_map/ppermute | solution.py:66
  94.0 3.5 %copy-start.5 = (bf16[512,256]{1,0:T(8,128)(2,1)}, bf16[512,256]{1,0:T(8,128)(2,1)S(1)}, u32[]{:S(2)}) copy-start(bf16[512,256]{1,0:T(8,128)(2,1)S(1)} %collective-permute-done.4) | copy-start | bytes 786436
  94.0 13.1 %collective-permute-start.5 = (bf16[512,256]{1,0:T(8,128)(2,1)S(1)}, bf16[512,256]{1,0:T(8,128)(2,1)}, u32[]{:S(2)}, u32[]{:S(2)}) collective-permute-start(bf16[512,256]{1,0:T(8,128)(2,1)S(1)} %collective-permute-done.4), channel_id=1, source_target_pairs={{0,1},{1,2},{2,3},{3,4},{4,5},{5,6},{6,7},{7,8},{8,9},{9,10},{10,1... | collective-permute-start | bytes 786440 | tf_op jit(solution)/shard_map/ppermute | solution.py:63
  97.5 20.0 %collective-permute-start.12 = (bf16[512,256]{1,0:T(8,128)(2,1)}, bf16[512,256]{1,0:T(8,128)(2,1)}, u32[]{:S(2)}, u32[]{:S(2)}) collective-permute-start(bf16[512,256]{1,0:T(8,128)(2,1)} %collective-permute-done.11), channel_id=1, source_target_pairs={{0,15},{1,0},{2,1},{3,2},{4,3},{5,4},{6,5},{7,6},{8,7},{9,8},{10,9... | collective-permute-start | bytes 786440 | tf_op jit(solution)/shard_map/ppermute | solution.py:66
  107.2 14.3 %collective-permute-start.6 = (bf16[512,256]{1,0:T(8,128)(2,1)}, bf16[512,256]{1,0:T(8,128)(2,1)}, u32[]{:S(2)}, u32[]{:S(2)}) collective-permute-start(bf16[512,256]{1,0:T(8,128)(2,1)} %collective-permute-done.5), channel_id=1, source_target_pairs={{0,1},{1,2},{2,3},{3,4},{4,5},{5,6},{6,7},{7,8},{8,9},{9,10},{10,1... | collective-permute-start | bytes 786440 | tf_op jit(solution)/shard_map/ppermute | solution.py:63
  110.2 14.6 %all-to-all-start = ((s32[32,1,128]{2,1,0:T(1,128)}), s32[32,1,128]{2,1,0:T(1,128)S(1)}, u32[]{:S(2)}, u32[]{:S(2)}) async-start(s32[32,1,128]{2,1,0:T(1,128)} %bitcast.5), calls=%async_computation.1 | async-start | bytes 32768 | tf_op jit(solution)/shard_map/all_to_all | solution.py:51
  117.5 17.7 %collective-permute-start.13 = (bf16[512,256]{1,0:T(8,128)(2,1)}, bf16[512,256]{1,0:T(8,128)(2,1)}, u32[]{:S(2)}, u32[]{:S(2)}) collective-permute-start(bf16[512,256]{1,0:T(8,128)(2,1)} %collective-permute-done.12), channel_id=1, source_target_pairs={{0,15},{1,0},{2,1},{3,2},{4,3},{5,4},{6,5},{7,6},{8,7},{9,8},{10,9... | collective-permute-start | bytes 786440 | tf_op jit(solution)/shard_map/ppermute | solution.py:66
  121.4 18.7 %collective-permute-start.7 = (bf16[512,256]{1,0:T(8,128)(2,1)}, bf16[512,256]{1,0:T(8,128)(2,1)}, u32[]{:S(2)}, u32[]{:S(2)}) collective-permute-start(bf16[512,256]{1,0:T(8,128)(2,1)} %collective-permute-done.6), channel_id=1, source_target_pairs={{0,1},{1,2},{2,3},{3,4},{4,5},{5,6},{6,7},{7,8},{8,9},{9,10},{10,1... | collective-permute-start | bytes 786440 | tf_op jit(solution)/shard_map/ppermute | solution.py:63
  129.1 36.1 %all-to-all-start.1 = ((bf16[32,128,256]{2,1,0:T(8,128)(2,1)}), bf16[32,128,256]{2,1,0:T(8,128)(2,1)}, u32[]{:S(2)}, u32[]{:S(2)}) async-start(bf16[32,128,256]{2,1,0:T(8,128)(2,1)} %bitcast.39), calls=%async_computation.2 | async-start | bytes 4194304 | tf_op jit(solution)/shard_map/all_to_all | solution.py:53
  135.2 14.8 %copy-start.3 = (bf16[512,256]{1,0:T(8,128)(2,1)S(1)}, bf16[512,256]{1,0:T(8,128)(2,1)}, u32[]{:S(2)}) copy-start(bf16[512,256]{1,0:T(8,128)(2,1)} %copy-done.2) | copy-start | bytes 786436
  135.2 17.8 %collective-permute-start.14 = (bf16[512,256]{1,0:T(8,128)(2,1)}, bf16[512,256]{1,0:T(8,128)(2,1)S(1)}, u32[]{:S(2)}, u32[]{:S(2)}) collective-permute-start(bf16[512,256]{1,0:T(8,128)(2,1)} %collective-permute-done.13), channel_id=1, source_target_pairs={{0,15},{1,0},{2,1},{3,2},{4,3},{5,4},{6,5},{7,6},{8,7},{9,8},{10,9... | collective-permute-start | bytes 786440 | tf_op jit(solution)/shard_map/ppermute | solution.py:66
  165.1 34.0 %all-to-all-start.3 = ((bf16[32,128,256]{2,1,0:T(8,128)(2,1)}), bf16[32,128,256]{2,1,0:T(8,128)(2,1)S(1)}, u32[]{:S(2)}, u32[]{:S(2)}) async-start(bf16[32,128,256]{2,1,0:T(8,128)(2,1)} %bitcast.41), calls=%async_computation.4 | async-start | bytes 4194304 | tf_op jit(solution)/shard_map/all_to_all | solution.py:78
  199.8 25.6 %all-to-all-start.2 = ((f32[16,512,4]{1,2,0:T(4,128)}), f32[16,512,4]{1,2,0:T(4,128)S(1)}, u32[]{:S(2)}, u32[]{:S(2)}) async-start(f32[16,512,4]{1,2,0:T(4,128)} %broadcast_in_dim.2), calls=%async_computation.3 | async-start | bytes 262144 | tf_op jit(solution)/shard_map/all_to_all | solution.py:85
  212.9 12.6 %copy-start.6 = (s32[512,4]{0,1:T(4,128)S(1)}, s32[512,4]{0,1:T(4,128)}, u32[]{:S(2)}) copy-start(s32[512,4]{0,1:T(4,128)} %param.13) | copy-start | bytes 24580
Sparse Core Ops, SparseCore 0:
  15.8 94.3 reduce-scatter.1

commit v8 on v3

--- a/solution.py
+++ b/solution.py
@@ -53,7 +53,21 @@
     back = lax.all_to_all(served, "dp", 0, 0, tiled=True).reshape(n_dp * CAP, e_local)
     old_vec = pick_rows(slot, back).reshape(rows, K, e_local)
 
-    old_full = lax.all_gather(old_index, "wide", axis=1, tiled=True)
+    me_w = lax.axis_index("wide")
+
+    def place(full, block, source):
+        return lax.dynamic_update_slice_in_dim(full, block, source * e_local, 1)
+
+    old_full = place(jnp.zeros((doc_shard, width), old_index.dtype), old_index, me_w)
+    quarter = n_wide // 4
+    chains = [(1, 1, quarter), (-1, 1, quarter - 1), (1, quarter + 1, quarter), (-1, quarter, quarter)]
+    for way, jump, length in chains:
+        held, offset = old_index, 0
+        for step in range(length):
+            hop = jump if step == 0 else 1
+            held = lax.ppermute(held, "wide", [(i, (i + way * hop) % n_wide) for i in range(n_wide)])
+            offset += hop
+            old_full = place(old_full, held, (me_w - way * offset) % n_wide)
     g_own = lax.dot_general(
         old_full, masked, (((1,), (1,)), ((), ())), preferred_element_type=jnp.float32
     ).astype(jnp.bfloat16)

time: 256 us -> 227 us (0.89)
  the two profiles are of different devices: /device:TPU:6 before, /device:TPU:32 now
where the time goes in v8:
time: 227 us; the launch traced here: 225 us
  starting transfers between devices  95.3 us (42%)
  waiting for transfers between devices  42.7 us (19%)
  matrix products  39.4 us (17%)
  local copies, waits for them, and re-layouts  30.4 us (13%)
  between operations  14.4 us (6%)
  other arithmetic  2.99 us (1%)
    ppermute x15, starting transfers between devices, local(): lax.ppermute(held, 'wide', [(i, (i + way * hop) % n_wide) for i in range(...  62.6 us
    dot_general x4, matrix products, pick_rows(): jnp.dot(one_hot(index, table.shape[0]), table, preferred_element_type=jnp...  28.9 us
    dynamic_update_slice x16, local copies, waits for them, and re-layouts, place(): return lax.dynamic_update_slice_in_dim(full, block, source * e_local, 1)  22.5 us
    ppermute x15, waiting for transfers between devices, local(): lax.ppermute(held, 'wide', [(i, (i + way * hop) % n_wide) for i in range(...  22 us
    all_to_all x1, waiting for transfers between devices, local(): lax.all_to_all(served_g, 'dp', 0, 0, tiled=True)  16.7 us
    all_to_all x1, starting transfers between devices, local(): gathered = lax.all_to_all(spread, 'wide', 0, 0, tiled=True)  10.2 us
    all_to_all x1, starting transfers between devices, local(): lax.all_to_all(served_g, 'dp', 0, 0, tiled=True)  7.59 us
    all_to_all x1, starting transfers between devices, local(): lax.all_to_all(served, 'dp', 0, 0, tiled=True).reshape(n_dp * CAP, e_local)  7.51 us
  transfers between devices with their start and end apart: 20, of which 3 were waited for; matrix products, arithmetic and copies ran while one was open for 28% of the time, Pallas kernels for 0%

profile of v8, /device:TPU:32, one launch (start us, length us, event | category | flops | bytes accessed | tf_op | source)
XLA Modules:
  0.0 225.2 jit_solution(4431615159547444650)
XLA Ops:
  8.4 5.8 %convolution_convert_fusion = bf16[512,4096]{1,0:T(8,128)(2,1)} fusion(bf16[512,1024]{1,0:T(8,128)(2,1)S(1)} %copy-done, bf16[1024,256]{1,0:T(8,128)(2,1)} %param.8, bf16[256,4096]{1,0:T(8,128)(2,1)} %param.9, bf16[32,8,32,128]{3,2,1,0:T(8,128)(2,1)S(1)} %bitcast.39), kind=kOutput, calls=%fused_computation.10 | convolution fusion | flops 1345454080 | bytes 9961472 | tf_op jit(solution)/shard_map/dot_general | solution.py:31
  14.2 3.8 %collective-permute-start = (bf16[512,256]{1,0:T(8,128)(2,1)}, bf16[512,256]{1,0:T(8,128)(2,1)}, u32[]{:S(2)}, u32[]{:S(2)}) collective-permute-start(bf16[512,256]{1,0:T(8,128)(2,1)} %param.11), channel_id=1, source_target_pairs={{0,1},{1,2},{2,3},{3,4},{4,5},{5,6},{6,7},{7,8},{8,9},{9,10},{10,1... | collective-permute-start | bytes 786440 | tf_op jit(solution)/shard_map/ppermute | solution.py:68
  18.1 5.5 %collective-permute-start.4 = (bf16[512,256]{1,0:T(8,128)(2,1)}, bf16[512,256]{1,0:T(8,128)(2,1)}, u32[]{:S(2)}, u32[]{:S(2)}) collective-permute-start(bf16[512,256]{1,0:T(8,128)(2,1)} %param.11), channel_id=1, source_target_pairs={{0,15},{1,0},{2,1},{3,2},{4,3},{5,4},{6,5},{7,6},{8,7},{9,8},{10,9... | collective-permute-start | bytes 786440 | tf_op jit(solution)/shard_map/ppermute | solution.py:68
  23.6 7.0 %collective-permute-start.7 = (bf16[512,256]{1,0:T(8,128)(2,1)}, bf16[512,256]{1,0:T(8,128)(2,1)}, u32[]{:S(2)}, u32[]{:S(2)}) collective-permute-start(bf16[512,256]{1,0:T(8,128)(2,1)} %param.11), channel_id=1, source_target_pairs={{0,5},{1,6},{2,7},{3,8},{4,9},{5,10},{6,11},{7,12},{8,13},{9,14},{... | collective-permute-start | bytes 786440 | tf_op jit(solution)/shard_map/ppermute | solution.py:68
  30.6 3.3 %collective-permute-start.11 = (bf16[512,256]{1,0:T(8,128)(2,1)}, bf16[512,256]{1,0:T(8,128)(2,1)}, u32[]{:S(2)}, u32[]{:S(2)}) collective-permute-start(bf16[512,256]{1,0:T(8,128)(2,1)} %param.11), channel_id=1, source_target_pairs={{0,12},{1,13},{2,14},{3,15},{4,0},{5,1},{6,2},{7,3},{8,4},{9,5},{1... | collective-permute-start | bytes 786440 | tf_op jit(solution)/shard_map/ppermute | solution.py:68
  36.6 3.6 %collective-permute-start.1 = (bf16[512,256]{1,0:T(8,128)(2,1)}, bf16[512,256]{1,0:T(8,128)(2,1)}, u32[]{:S(2)}, u32[]{:S(2)}) collective-permute-start(bf16[512,256]{1,0:T(8,128)(2,1)} %collective-permute-done), channel_id=1, source_target_pairs={{0,1},{1,2},{2,3},{3,4},{4,5},{5,6},{6,7},{7,8},{8,9},{9,10},{10,1... | collective-permute-start | bytes 786440 | tf_op jit(solution)/shard_map/ppermute | solution.py:68
  40.2 21.9 %collective-permute-done.7 = bf16[512,256]{1,0:T(8,128)(2,1)} collective-permute-done((bf16[512,256]{1,0:T(8,128)(2,1)}, bf16[512,256]{1,0:T(8,128)(2,1)}, u32[]{:S(2)}, u32[]{:S(2)}) %collective-permute-start.7) | collective-permute-done | bytes 262176 | tf_op jit(solution)/shard_map/ppermute | solution.py:68
  62.1 4.7 %collective-permute-start.8 = (bf16[512,256]{1,0:T(8,128)(2,1)}, bf16[512,256]{1,0:T(8,128)(2,1)}, u32[]{:S(2)}, u32[]{:S(2)}) collective-permute-start(bf16[512,256]{1,0:T(8,128)(2,1)} %collective-permute-done.7), channel_id=1, source_target_pairs={{0,1},{1,2},{2,3},{3,4},{4,5},{5,6},{6,7},{7,8},{8,9},{9,10},{10,1... | collective-permute-start | bytes 786440 | tf_op jit(solution)/shard_map/ppermute | solution.py:68
  66.8 7.5 %collective-permute-start.12 = (bf16[512,256]{1,0:T(8,128)(2,1)}, bf16[512,256]{1,0:T(8,128)(2,1)S(1)}, u32[]{:S(2)}, u32[]{:S(2)}) collective-permute-start(bf16[512,256]{1,0:T(8,128)(2,1)} %collective-permute-done.11), channel_id=1, source_target_pairs={{0,15},{1,0},{2,1},{3,2},{4,3},{5,4},{6,5},{7,6},{8,7},{9,8},{10,9... | collective-permute-start | bytes 786440 | tf_op jit(solution)/shard_map/ppermute | solution.py:68
  75.0 7.3 %all-to-all-start = ((s32[32,1,128]{2,1,0:T(1,128)}), s32[32,1,128]{2,1,0:T(1,128)S(1)}, u32[]{:S(2)}, u32[]{:S(2)}) async-start(s32[32,1,128]{2,1,0:T(1,128)} %bitcast.5), calls=%async_computation.1 | async-start | bytes 32768 | tf_op jit(solution)/shard_map/all_to_all | solution.py:51
  82.3 2.5 %broadcast_in_dim.5 = bf16[512,4096]{1,0:T(8,128)(2,1)} broadcast(bf16[]{:T(256)} %constant.160.clone.1), dimensions={} | broadcast | bytes 4194306 | tf_op jit(solution)/shard_map/broadcast_in_dim | solution.py:61
  86.5 5.1 %collective-permute-start.5 = (bf16[512,256]{1,0:T(8,128)(2,1)}, bf16[512,256]{1,0:T(8,128)(2,1)}, u32[]{:S(2)}, u32[]{:S(2)}) collective-permute-start(bf16[512,256]{1,0:T(8,128)(2,1)} %collective-permute-done.4), channel_id=1, source_target_pairs={{0,15},{1,0},{2,1},{3,2},{4,3},{5,4},{6,5},{7,6},{8,7},{9,8},{10,9... | collective-permute-start | bytes 786440 | tf_op jit(solution)/shard_map/ppermute | solution.py:68
  91.6 1.9 collective-permute-start.2
  93.6 1.9 collective-permute-start.9
  95.5 3.9 %collective-permute-start.13 = (bf16[512,256]{1,0:T(8,128)(2,1)S(1)}, bf16[512,256]{1,0:T(8,128)(2,1)}, u32[]{:S(2)}, u32[]{:S(2)}) collective-permute-start(bf16[512,256]{1,0:T(8,128)(2,1)S(1)} %collective-permute-done.12), channel_id=1, source_target_pairs={{0,15},{1,0},{2,1},{3,2},{4,3},{5,4},{6,5},{7,6},{8,7},{9,8},{10,9... | collective-permute-start | bytes 786440 | tf_op jit(solution)/shard_map/ppermute | solution.py:68
  99.4 4.2 %fusion.7 = bf16[4096,256]{1,0:T(8,128)(2,1)} fusion(bf16[512,256]{1,0:T(8,128)(2,1)} %param.11, s32[4096]{0:T(1024)S(1)} %bitcast.45), kind=kOutput, calls=%fused_computation.11 | convolution fusion | flops 1076887552 | bytes 2375680 | tf_op jit(solution)/shard_map/dot_general | solution.py:18
  103.7 7.5 %all-to-all-start.1 = ((bf16[32,128,256]{2,1,0:T(8,128)(2,1)}), bf16[32,128,256]{2,1,0:T(8,128)(2,1)}, u32[]{:S(2)}, u32[]{:S(2)}) async-start(bf16[32,128,256]{2,1,0:T(8,128)(2,1)} %bitcast.41), calls=%async_computation.2 | async-start | bytes 4194304 | tf_op jit(solution)/shard_map/all_to_all | solution.py:53
  111.2 1.9 collective-permute-start.3
  114.8 5.1 %collective-permute-start.6 = (bf16[512,256]{1,0:T(8,128)(2,1)}, bf16[512,256]{1,0:T(8,128)(2,1)S(1)}, u32[]{:S(2)}, u32[]{:S(2)}) collective-permute-start(bf16[512,256]{1,0:T(8,128)(2,1)} %collective-permute-done.5), channel_id=1, source_target_pairs={{0,15},{1,0},{2,1},{3,2},{4,3},{5,4},{6,5},{7,6},{8,7},{9,8},{10,9... | collective-permute-start | bytes 786440 | tf_op jit(solution)/shard_map/ppermute | solution.py:68
  121.6 1.9 collective-permute-start.10
  123.6 5.3 %collective-permute-start.14 = (bf16[512,256]{1,0:T(8,128)(2,1)}, bf16[512,256]{1,0:T(8,128)(2,1)S(1)}, u32[]{:S(2)}, u32[]{:S(2)}) collective-permute-start(bf16[512,256]{1,0:T(8,128)(2,1)} %collective-permute-done.13), channel_id=1, source_target_pairs={{0,15},{1,0},{2,1},{3,2},{4,3},{5,4},{6,5},{7,6},{8,7},{9,8},{10,9... | collective-permute-start | bytes 786440 | tf_op jit(solution)/shard_map/ppermute | solution.py:68
  141.4 1.7 constant_dynamic-update-slice_fusion.3
  143.9 1.7 constant_dynamic-update-slice_fusion.1
  146.4 8.8 %fusion.8 = bf16[4096,256]{1,0:T(8,128)(2,1)} fusion(s32[4096]{0:T(1024)S(1)} %bitcast.46, bf16[512,4096]{1,0:T(8,128)(2,1)} %constant_dynamic-update-slice_fusion, bf16[256,4096]{1,0:T(8,128)(2,1)} %param.9, bf16[32,8,32,128]{3,2,1,0:T(8,128)(2,1)S(1)} %bitcast.40), kind=kOutput, calls=%fused_computation.12 | convolution fusion | flops 2151809024 | bytes 10502144 | tf_op jit(solution)/shard_map/dot_general | solution.py:18
  155.2 7.6 %all-to-all-start.3 = ((bf16[32,128,256]{2,1,0:T(8,128)(2,1)}), bf16[32,128,256]{2,1,0:T(8,128)(2,1)S(1)}, u32[]{:S(2)}, u32[]{:S(2)}) async-start(bf16[32,128,256]{2,1,0:T(8,128)(2,1)} %bitcast.43), calls=%async_computation.4 | async-start | bytes 4194304 | tf_op jit(solution)/shard_map/all_to_all | solution.py:75
  162.8 8.8 %fusion.11 = bf16[2048,256]{1,0:T(8,128)(2,1)} fusion(bf16[4096,256]{1,0:T(8,128)(2,1)} %bitcast.8, s32[2048]{0:T(1024)S(1)} %multiply_add_fusion), kind=kOutput, calls=%fused_computation.15 | convolution fusion | flops 4303880192 | bytes 3153920 | tf_op jit(solution)/shard_map/dot_general | solution.py:18
  171.6 2.2 reshape.272
  173.7 2.0 fusion.21
  175.8 16.7 %all-to-all-done.3 = bf16[32,128,256]{2,1,0:T(8,128)(2,1)S(1)} async-done(((bf16[32,128,256]{2,1,0:T(8,128)(2,1)}), bf16[32,128,256]{2,1,0:T(8,128)(2,1)S(1)}, u32[]{:S(2)}, u32[]{:S(2)}) %all-to-all-start.3) | async-done | bytes 2097184 | tf_op jit(solution)/shard_map/all_to_all | solution.py:75
  193.2 10.2 %all-to-all-start.2 = ((f32[16,512,4]{1,2,0:T(4,128)}), f32[16,512,4]{1,2,0:T(4,128)S(1)}, u32[]{:S(2)}, u32[]{:S(2)}) async-start(f32[16,512,4]{1,2,0:T(4,128)} %broadcast_in_dim.4), calls=%async_computation.3 | async-start | bytes 262144 | tf_op jit(solution)/shard_map/all_to_all | solution.py:82
  203.4 7.2 %fusion.12 = bf16[2048,256]{1,0:T(8,128)(2,1)} fusion(bf16[4096,256]{1,0:T(8,128)(2,1)S(1)} %bitcast.42, s32[2048]{0:T(1024)S(1)} %multiply_add_fusion), kind=kOutput, calls=%fused_computation.16 | convolution fusion | flops 4303880192 | bytes 3153920 | tf_op jit(solution)/shard_map/dot_general | solution.py:18
  212.0 4.0 %all-to-all-done.2 = f32[16,512,4]{1,2,0:T(4,128)S(1)} async-done(((f32[16,512,4]{1,2,0:T(4,128)}), f32[16,512,4]{1,2,0:T(4,128)S(1)}, u32[]{:S(2)}, u32[]{:S(2)}) %all-to-all-start.2) | async-done | bytes 131104 | tf_op jit(solution)/shard_map/all_to_all | solution.py:82
  (63 shorter events, 28.1 us)
Async XLA Ops:
  7.2 1.2 copy-start
  7.2 166.5 %reduce-scatter.2.cloned.1.call-start = ((), (), s32[]{:S(2)}) async-start(), calls=%async_computation.5 | async-start | bytes 4456448 | tf_op jit(solution)/shard_map/reduce_scatter | solution.py:32
  14.2 19.7 %copy-start.2 = (s32[512,4]{0,1:T(4,128)S(1)}, s32[512,4]{0,1:T(4,128)}, u32[]{:S(2)}) copy-start(s32[512,4]{0,1:T(4,128)} %param.12) | copy-start | bytes 24580
  14.2 22.4 %collective-permute-start = (bf16[512,256]{1,0:T(8,128)(2,1)}, bf16[512,256]{1,0:T(8,128)(2,1)}, u32[]{:S(2)}, u32[]{:S(2)}) collective-permute-start(bf16[512,256]{1,0:T(8,128)(2,1)} %param.11), channel_id=1, source_target_pairs={{0,1},{1,2},{2,3},{3,4},{4,5},{5,6},{6,7},{7,8},{8,9},{9,10},{10,1... | collective-permute-start | bytes 786440 | tf_op jit(solution)/shard_map/ppermute | solution.py:68
  18.1 68.4 %collective-permute-start.4 = (bf16[512,256]{1,0:T(8,128)(2,1)}, bf16[512,256]{1,0:T(8,128)(2,1)}, u32[]{:S(2)}, u32[]{:S(2)}) collective-permute-start(bf16[512,256]{1,0:T(8,128)(2,1)} %param.11), channel_id=1, source_target_pairs={{0,15},{1,0},{2,1},{3,2},{4,3},{5,4},{6,5},{7,6},{8,7},{9,8},{10,9... | collective-permute-start | bytes 786440 | tf_op jit(solution)/shard_map/ppermute | solution.py:68
  23.6 38.5 %collective-permute-start.7 = (bf16[512,256]{1,0:T(8,128)(2,1)}, bf16[512,256]{1,0:T(8,128)(2,1)}, u32[]{:S(2)}, u32[]{:S(2)}) collective-permute-start(bf16[512,256]{1,0:T(8,128)(2,1)} %param.11), channel_id=1, source_target_pairs={{0,5},{1,6},{2,7},{3,8},{4,9},{5,10},{6,11},{7,12},{8,13},{9,14},{... | collective-permute-start | bytes 786440 | tf_op jit(solution)/shard_map/ppermute | solution.py:68
  30.6 36.2 %collective-permute-start.11 = (bf16[512,256]{1,0:T(8,128)(2,1)}, bf16[512,256]{1,0:T(8,128)(2,1)}, u32[]{:S(2)}, u32[]{:S(2)}) collective-permute-start(bf16[512,256]{1,0:T(8,128)(2,1)} %param.11), channel_id=1, source_target_pairs={{0,12},{1,13},{2,14},{3,15},{4,0},{5,1},{6,2},{7,3},{8,4},{9,5},{1... | collective-permute-start | bytes 786440 | tf_op jit(solution)/shard_map/ppermute | solution.py:68
  36.6 55.0 %collective-permute-start.1 = (bf16[512,256]{1,0:T(8,128)(2,1)}, bf16[512,256]{1,0:T(8,128)(2,1)}, u32[]{:S(2)}, u32[]{:S(2)}) collective-permute-start(bf16[512,256]{1,0:T(8,128)(2,1)} %collective-permute-done), channel_id=1, source_target_pairs={{0,1},{1,2},{2,3},{3,4},{4,5},{5,6},{6,7},{7,8},{8,9},{9,10},{10,1... | collective-permute-start | bytes 786440 | tf_op jit(solution)/shard_map/ppermute | solution.py:68
  62.1 31.5 %collective-permute-start.8 = (bf16[512,256]{1,0:T(8,128)(2,1)}, bf16[512,256]{1,0:T(8,128)(2,1)}, u32[]{:S(2)}, u32[]{:S(2)}) collective-permute-start(bf16[512,256]{1,0:T(8,128)(2,1)} %collective-permute-done.7), channel_id=1, source_target_pairs={{0,1},{1,2},{2,3},{3,4},{4,5},{5,6},{6,7},{7,8},{8,9},{9,10},{10,1... | collective-permute-start | bytes 786440 | tf_op jit(solution)/shard_map/ppermute | solution.py:68
  66.8 28.7 %collective-permute-start.12 = (bf16[512,256]{1,0:T(8,128)(2,1)}, bf16[512,256]{1,0:T(8,128)(2,1)S(1)}, u32[]{:S(2)}, u32[]{:S(2)}) collective-permute-start(bf16[512,256]{1,0:T(8,128)(2,1)} %collective-permute-done.11), channel_id=1, source_target_pairs={{0,15},{1,0},{2,1},{3,2},{4,3},{5,4},{6,5},{7,6},{8,7},{9,8},{10,9... | collective-permute-start | bytes 786440 | tf_op jit(solution)/shard_map/ppermute | solution.py:68
  75.0 24.5 %all-to-all-start = ((s32[32,1,128]{2,1,0:T(1,128)}), s32[32,1,128]{2,1,0:T(1,128)S(1)}, u32[]{:S(2)}, u32[]{:S(2)}) async-start(s32[32,1,128]{2,1,0:T(1,128)} %bitcast.5), calls=%async_computation.1 | async-start | bytes 32768 | tf_op jit(solution)/shard_map/all_to_all | solution.py:51
  86.5 28.3 %collective-permute-start.5 = (bf16[512,256]{1,0:T(8,128)(2,1)}, bf16[512,256]{1,0:T(8,128)(2,1)}, u32[]{:S(2)}, u32[]{:S(2)}) collective-permute-start(bf16[512,256]{1,0:T(8,128)(2,1)} %collective-permute-done.4), channel_id=1, source_target_pairs={{0,15},{1,0},{2,1},{3,2},{4,3},{5,4},{6,5},{7,6},{8,7},{9,8},{10,9... | collective-permute-start | bytes 786440 | tf_op jit(solution)/shard_map/ppermute | solution.py:68
  91.6 19.6 %collective-permute-start.2 = (bf16[512,256]{1,0:T(8,128)(2,1)}, bf16[512,256]{1,0:T(8,128)(2,1)}, u32[]{:S(2)}, u32[]{:S(2)}) collective-permute-start(bf16[512,256]{1,0:T(8,128)(2,1)} %collective-permute-done.1), channel_id=1, source_target_pairs={{0,1},{1,2},{2,3},{3,4},{4,5},{5,6},{6,7},{7,8},{8,9},{9,10},{10,1... | collective-permute-start | bytes 786440 | tf_op jit(solution)/shard_map/ppermute | solution.py:68
  93.6 28.1 %collective-permute-start.9 = (bf16[512,256]{1,0:T(8,128)(2,1)}, bf16[512,256]{1,0:T(8,128)(2,1)}, u32[]{:S(2)}, u32[]{:S(2)}) collective-permute-start(bf16[512,256]{1,0:T(8,128)(2,1)} %collective-permute-done.8), channel_id=1, source_target_pairs={{0,1},{1,2},{2,3},{3,4},{4,5},{5,6},{6,7},{7,8},{8,9},{9,10},{10,1... | collective-permute-start | bytes 786440 | tf_op jit(solution)/shard_map/ppermute | solution.py:68
  95.5 28.0 %collective-permute-start.13 = (bf16[512,256]{1,0:T(8,128)(2,1)S(1)}, bf16[512,256]{1,0:T(8,128)(2,1)}, u32[]{:S(2)}, u32[]{:S(2)}) collective-permute-start(bf16[512,256]{1,0:T(8,128)(2,1)S(1)} %collective-permute-done.12), channel_id=1, source_target_pairs={{0,15},{1,0},{2,1},{3,2},{4,3},{5,4},{6,5},{7,6},{8,7},{9,8},{10,9... | collective-permute-start | bytes 786440 | tf_op jit(solution)/shard_map/ppermute | solution.py:68
  103.7 51.5 %all-to-all-start.1 = ((bf16[32,128,256]{2,1,0:T(8,128)(2,1)}), bf16[32,128,256]{2,1,0:T(8,128)(2,1)}, u32[]{:S(2)}, u32[]{:S(2)}) async-start(bf16[32,128,256]{2,1,0:T(8,128)(2,1)} %bitcast.41), calls=%async_computation.2 | async-start | bytes 4194304 | tf_op jit(solution)/shard_map/all_to_all | solution.py:53
  111.2 19.5 %collective-permute-start.3 = (bf16[512,256]{1,0:T(8,128)(2,1)}, bf16[512,256]{1,0:T(8,128)(2,1)S(1)}, u32[]{:S(2)}, u32[]{:S(2)}) collective-permute-start(bf16[512,256]{1,0:T(8,128)(2,1)} %collective-permute-done.2), channel_id=1, source_target_pairs={{0,1},{1,2},{2,3},{3,4},{4,5},{5,6},{6,7},{7,8},{8,9},{9,10},{10,1... | collective-permute-start | bytes 786440 | tf_op jit(solution)/shard_map/ppermute | solution.py:68
  114.8 20.0 %collective-permute-start.6 = (bf16[512,256]{1,0:T(8,128)(2,1)}, bf16[512,256]{1,0:T(8,128)(2,1)S(1)}, u32[]{:S(2)}, u32[]{:S(2)}) collective-permute-start(bf16[512,256]{1,0:T(8,128)(2,1)} %collective-permute-done.5), channel_id=1, source_target_pairs={{0,15},{1,0},{2,1},{3,2},{4,3},{5,4},{6,5},{7,6},{8,7},{9,8},{10,9... | collective-permute-start | bytes 786440 | tf_op jit(solution)/shard_map/ppermute | solution.py:68
  121.6 19.0 %collective-permute-start.10 = (bf16[512,256]{1,0:T(8,128)(2,1)}, bf16[512,256]{1,0:T(8,128)(2,1)S(1)}, u32[]{:S(2)}, u32[]{:S(2)}) collective-permute-start(bf16[512,256]{1,0:T(8,128)(2,1)} %collective-permute-done.9), channel_id=1, source_target_pairs={{0,1},{1,2},{2,3},{3,4},{4,5},{5,6},{6,7},{7,8},{8,9},{9,10},{10,1... | collective-permute-start | bytes 786440 | tf_op jit(solution)/shard_map/ppermute | solution.py:68
  123.6 22.1 %collective-permute-start.14 = (bf16[512,256]{1,0:T(8,128)(2,1)}, bf16[512,256]{1,0:T(8,128)(2,1)S(1)}, u32[]{:S(2)}, u32[]{:S(2)}) collective-permute-start(bf16[512,256]{1,0:T(8,128)(2,1)} %collective-permute-done.13), channel_id=1, source_target_pairs={{0,15},{1,0},{2,1},{3,2},{4,3},{5,4},{6,5},{7,6},{8,7},{9,8},{10,9... | collective-permute-start | bytes 786440 | tf_op jit(solution)/shard_map/ppermute | solution.py:68
  155.2 37.4 %all-to-all-start.3 = ((bf16[32,128,256]{2,1,0:T(8,128)(2,1)}), bf16[32,128,256]{2,1,0:T(8,128)(2,1)S(1)}, u32[]{:S(2)}, u32[]{:S(2)}) async-start(bf16[32,128,256]{2,1,0:T(8,128)(2,1)} %bitcast.43), calls=%async_computation.4 | async-start | bytes 4194304 | tf_op jit(solution)/shard_map/all_to_all | solution.py:75
  193.2 22.8 %all-to-all-start.2 = ((f32[16,512,4]{1,2,0:T(4,128)}), f32[16,512,4]{1,2,0:T(4,128)S(1)}, u32[]{:S(2)}, u32[]{:S(2)}) async-start(f32[16,512,4]{1,2,0:T(4,128)} %broadcast_in_dim.4), calls=%async_computation.3 | async-start | bytes 262144 | tf_op jit(solution)/shard_map/all_to_all | solution.py:82
  203.4 12.6 %copy-start.1 = (s32[512,4]{0,1:T(4,128)S(1)}, s32[512,4]{0,1:T(4,128)}, u32[]{:S(2)}) copy-start(s32[512,4]{0,1:T(4,128)} %param.13) | copy-start | bytes 24580
Sparse Core Ops, SparseCore 0:
  14.4 121.1 reduce-scatter.1

commit v9 on v3

--- a/solution.py
+++ b/solution.py
@@ -25,13 +25,16 @@
     local_blocks, nblocks = block_mask.shape
     side = e_local // local_blocks
     doc_shard = old_index.shape[0]
-    query = jnp.dot(trunk_out, projection, preferred_element_type=jnp.float32).astype(jnp.bfloat16)
     blocks = transform.reshape(local_blocks, side, nblocks, side)
     masked = (blocks * block_mask[:, None, :, None].astype(jnp.bfloat16)).reshape(e_local, width)
-    term = jnp.dot(query, masked, preferred_element_type=jnp.float32)
-    new = lax.psum_scatter(
-        term.astype(jnp.bfloat16), "wide", scatter_dimension=1, tiled=True
-    ).astype(jnp.float32)
+
+    chunk = trunk_out.shape[1] // n_dp
+    proj_rows = lax.dynamic_slice_in_dim(projection, lax.axis_index("dp") * chunk, chunk, 0)
+    w_part = jnp.dot(proj_rows, masked, preferred_element_type=jnp.float32)
+    w_parts = w_part.reshape(chunk, n_wide, e_local).transpose(1, 0, 2)
+    w_blk = jnp.sum(lax.all_to_all(w_parts, "wide", 0, 0, tiled=True), axis=0)
+    w_cols = lax.all_gather(w_blk.astype(jnp.bfloat16), "dp", axis=0, tiled=True)
+    new = jnp.dot(trunk_out, w_cols, preferred_element_type=jnp.float32)
 
     flat = doc_ids.reshape(-1)
     count = flat.shape[0]

time: 256 us -> 226 us (0.88)
  the two profiles are of different devices: /device:TPU:6 before, /device:TPU:32 now
where the time goes in v9:
time: 226 us; the launch traced here: 225 us
  waiting for transfers between devices  66.5 us (29%)
  blocking collectives  43.4 us (19%)
  starting transfers between devices  43.1 us (19%)
  matrix products  34.4 us (15%)
  between operations  14.2 us (6%)
  local copies, waits for them, and re-layouts  13.9 us (6%)
  other arithmetic  9.68 us (4%)
    all_gather x1, blocking collectives, local(): lax.all_gather(w_blk.astype(jnp.bfloat16), 'dp', axis=0, tiled=True)  43.4 us
    all_to_all x1, waiting for transfers between devices, local(): w_blk = jnp.sum(lax.all_to_all(w_parts, 'wide', 0, 0, tiled=True), axis=0)  29.7 us
    all_to_all x1, waiting for transfers between devices, local(): lax.all_to_all(served_g, 'dp', 0, 0, tiled=True)  28.2 us
    dot_general x4, matrix products, pick_rows(): jnp.dot(one_hot(index, table.shape[0]), table, preferred_element_type=jnp...  27.2 us
    all_to_all x1, starting transfers between devices, local(): w_blk = jnp.sum(lax.all_to_all(w_parts, 'wide', 0, 0, tiled=True), axis=0)  15.3 us
    all_to_all x1, starting transfers between devices, local(): gathered = lax.all_to_all(spread, 'wide', 0, 0, tiled=True)  8.11 us
    all_to_all x1, waiting for transfers between devices, local(): gathered = lax.all_to_all(spread, 'wide', 0, 0, tiled=True)  7.9 us
    all_to_all x1, starting transfers between devices, local(): asked = lax.all_to_all(req, 'dp', 0, 0, tiled=True).reshape(-1)  7.32 us
  transfers between devices with their start and end apart: 6, of which 3 were waited for; matrix products, arithmetic and copies ran while one was open for 21% of the time, Pallas kernels for 0%

profile of v9, /device:TPU:32, one launch (start us, length us, event | category | flops | bytes accessed | tf_op | source)
XLA Modules:
  0.0 225.3 jit_solution(13660898225473630466)
XLA Ops:
  7.2 0.7 all-gather.2.cloned.1.call-update
  7.9 0.8 copy.15
  9.3 1.5 fusion.14
  11.3 0.6 slice_add_fusion
  11.9 7.3 %all-to-all-start.1 = ((s32[32,1,128]{2,1,0:T(1,128)}), s32[32,1,128]{2,1,0:T(1,128)S(1)}, u32[]{:S(2)}, u32[]{:S(2)}) async-start(s32[32,1,128]{2,1,0:T(1,128)} %bitcast.10), calls=%async_computation.1 | async-start | bytes 32768 | tf_op jit(solution)/shard_map/all_to_all | solution.py:54
  19.6 3.6 %fusion.18 = bf16[4096,256]{0,1:T(8,128)(2,1)} fusion(bf16[256,4096]{1,0:T(8,128)(2,1)} %param.9, bf16[32,8,32,128]{3,2,1,0:T(8,128)(2,1)S(1)} %bitcast.50), kind=kLoop, calls=%fused_computation.27 | loop fusion | flops 1048576 | bytes 6291456 | tf_op jit(solution)/shard_map/dot_general | solution.py:33
  23.3 4.1 %copy.26 = bf16[4096,256]{1,0:T(8,128)(2,1)} copy(bf16[4096,256]{0,1:T(8,128)(2,1)} %fusion.18) | data formatting | bytes 4194304 | tf_op jit(solution)/shard_map/dot_general | solution.py:33
  27.4 3.2 %convolution_bitcast_fusion = f32[16,32,256]{2,1,0:T(8,128)} fusion(bf16[16,256,256]{2,1,0:T(8,128)(2,1)} %bitcast.52, bf16[1024,256]{1,0:T(8,128)(2,1)} %param.8, s32[]{:T(128)S(6)} %select_n.56), kind=kOutput, calls=%fused_computation.19 | convolution fusion | flops 67108864 | bytes 2637828 | tf_op jit(solution)/shard_map/dot_general | solution.py:33
  30.6 15.3 %all-to-all-start = ((f32[16,32,256]{2,1,0:T(8,128)}), f32[16,32,256]{2,1,0:T(8,128)}, u32[]{:S(2)}, u32[]{:S(2)}) async-start(f32[16,32,256]{2,1,0:T(8,128)} %convolution_bitcast_fusion), calls=%async_computation | async-start | bytes 1048576 | tf_op jit(solution)/shard_map/all_to_all | solution.py:35
  45.8 3.3 %fusion.7 = bf16[4096,256]{1,0:T(8,128)(2,1)} fusion(bf16[512,256]{1,0:T(8,128)(2,1)S(1)} %copy-done.1, s32[4096]{0:T(1024)S(1)} %bitcast.56), kind=kOutput, calls=%fused_computation.10 | convolution fusion | flops 1076887552 | bytes 2375680 | tf_op jit(solution)/shard_map/dot_general | solution.py:18
  49.1 29.7 %all-to-all-done = f32[16,32,256]{2,1,0:T(8,128)} async-done(((f32[16,32,256]{2,1,0:T(8,128)}), f32[16,32,256]{2,1,0:T(8,128)}, u32[]{:S(2)}, u32[]{:S(2)}) %all-to-all-start) | async-done | bytes 524320 | tf_op jit(solution)/shard_map/all_to_all | solution.py:35
  78.8 7.0 %all-to-all-start.2 = ((bf16[32,128,256]{2,1,0:T(8,128)(2,1)}), bf16[32,128,256]{2,1,0:T(8,128)(2,1)}, u32[]{:S(2)}, u32[]{:S(2)}) async-start(bf16[32,128,256]{2,1,0:T(8,128)(2,1)} %bitcast.54), calls=%async_computation.2 | async-start | bytes 4194304 | tf_op jit(solution)/shard_map/all_to_all | solution.py:56
  85.9 1.1 reduce_sum.27
  87.0 43.4 %all_gather.6 = bf16[1024,256]{1,0:T(8,128)(2,1)S(1)} all-gather(bf16[32,256]{1,0:T(8,128)(2,1)S(1)} %reduce_sum.27), channel_id=1, replica_groups=mesh['dp'=32,'wide'=16] {'dp'}, dimensions={0}, use_global_device_ids=true | all-gather | bytes 540672 | tf_op jit(solution)/shard_map/all_gather | solution.py:36
  130.4 1.3 fusion.35
  131.7 2.1 copy.28
  133.8 8.8 %fusion.11 = bf16[2048,256]{1,0:T(8,128)(2,1)} fusion(bf16[4096,256]{1,0:T(8,128)(2,1)} %bitcast.13, s32[2048]{0:T(1024)S(1)} %multiply_add_fusion), kind=kOutput, calls=%fused_computation.14 | convolution fusion | flops 4303880192 | bytes 3153920 | tf_op jit(solution)/shard_map/dot_general | solution.py:18
  142.6 2.1 reshape.274
  144.7 2.7 %multiply_reduce_fusion = f32[512,4]{1,0:T(8,128)} fusion(f32[512,256]{1,0:T(8,128)} %copy.28, bf16[512,4,256]{2,1,0:T(4,128)(2,1)} %reshape.274), kind=kLoop, calls=%fused_computation.18 | loop fusion | flops 1570816 | bytes 1581056
  147.4 1.1 copy.23
  148.5 0.7 broadcast_in_dim.2
  149.2 8.1 %all-to-all-start.3 = ((f32[16,512,4]{1,2,0:T(4,128)}), f32[16,512,4]{1,2,0:T(4,128)S(1)}, u32[]{:S(2)}, u32[]{:S(2)}) async-start(f32[16,512,4]{1,2,0:T(4,128)} %broadcast_in_dim.2), calls=%async_computation.3 | async-start | bytes 262144 | tf_op jit(solution)/shard_map/all_to_all | solution.py:71
  157.3 7.3 %fusion.8 = bf16[4096,256]{1,0:T(8,128)(2,1)} fusion(s32[4096]{0:T(1024)S(1)} %bitcast.57, bf16[512,4096]{1,0:T(8,128)(2,1)} %all-gather.2.cloned.1.call-done, bf16[256,4096]{1,0:T(8,128)(2,1)} %param.9, bf16[32,8,32,128]{3,2,1,0:T(8,128)(2,1)S(1)} %bitcast.51), kind=kOutput, calls=%fused_computation.11 | convolution fusion | flops 2151809024 | bytes 10502144 | tf_op jit(solution)/shard_map/dot_general | solution.py:18
  164.6 7.9 %all-to-all-done.3 = f32[16,512,4]{1,2,0:T(4,128)S(1)} async-done(((f32[16,512,4]{1,2,0:T(4,128)}), f32[16,512,4]{1,2,0:T(4,128)S(1)}, u32[]{:S(2)}, u32[]{:S(2)}) %all-to-all-start.3) | async-done | bytes 131104 | tf_op jit(solution)/shard_map/all_to_all | solution.py:71
  172.5 5.3 %all-to-all-start.4 = ((bf16[32,128,256]{2,1,0:T(8,128)(2,1)}), bf16[32,128,256]{2,1,0:T(8,128)(2,1)S(1)}, u32[]{:S(2)}, u32[]{:S(2)}) async-start(bf16[32,128,256]{2,1,0:T(8,128)(2,1)} %bitcast.53), calls=%async_computation.4 | async-start | bytes 4194304 | tf_op jit(solution)/shard_map/all_to_all | solution.py:64
  177.8 0.8 copy.18
  178.9 0.6 compare_select_fusion
  179.5 28.2 %all-to-all-done.4 = bf16[32,128,256]{2,1,0:T(8,128)(2,1)S(1)} async-done(((bf16[32,128,256]{2,1,0:T(8,128)(2,1)}), bf16[32,128,256]{2,1,0:T(8,128)(2,1)S(1)}, u32[]{:S(2)}, u32[]{:S(2)}) %all-to-all-start.4) | async-done | bytes 2097184 | tf_op jit(solution)/shard_map/all_to_all | solution.py:64
  207.8 7.9 %fusion.12 = bf16[2048,256]{1,0:T(8,128)(2,1)} fusion(bf16[4096,256]{1,0:T(8,128)(2,1)S(1)} %bitcast.55, s32[2048]{0:T(1024)} %copy-done.3), kind=kOutput, calls=%fused_computation.15 | convolution fusion | flops 4303880192 | bytes 3153920 | tf_op jit(solution)/shard_map/dot_general | solution.py:18
  215.6 1.3 reshape.277
  217.0 0.7 fusion.36
  217.7 0.7 fusion.19
  (29 shorter events, 1.7 us)
Async XLA Ops:
  7.2 123.2 %copy-start = (bf16[512,1024]{1,0:T(8,128)(2,1)S(1)}, bf16[512,1024]{1,0:T(8,128)(2,1)}, u32[]{:S(2)}) copy-start(bf16[512,1024]{1,0:T(8,128)(2,1)} %param.7) | copy-start | bytes 3145732
  7.2 150.1 %all-gather.2.cloned.1.call-start = ((), (), s32[]{:S(2)}) async-start(), calls=%async_computation.5 | async-start | bytes 4456448 | tf_op jit(solution)/shard_map/all_gather | solution.py:59
  9.2 10.0 %copy-start.4 = (s32[2,32]{1,0:T(2,128)S(1)}, s32[2,32]{1,0:T(2,128)}, u32[]{:S(2)}) copy-start(s32[2,32]{1,0:T(2,128)} %param.10) | copy-start | bytes 772
  11.9 18.7 %all-to-all-start.1 = ((s32[32,1,128]{2,1,0:T(1,128)}), s32[32,1,128]{2,1,0:T(1,128)S(1)}, u32[]{:S(2)}, u32[]{:S(2)}) async-start(s32[32,1,128]{2,1,0:T(1,128)} %bitcast.10), calls=%async_computation.1 | async-start | bytes 32768 | tf_op jit(solution)/shard_map/all_to_all | solution.py:54
  27.4 18.5 %copy-start.1 = (bf16[512,256]{1,0:T(8,128)(2,1)S(1)}, bf16[512,256]{1,0:T(8,128)(2,1)}, u32[]{:S(2)}) copy-start(bf16[512,256]{1,0:T(8,128)(2,1)} %param.11) | copy-start | bytes 786436
  30.6 48.2 %all-to-all-start = ((f32[16,32,256]{2,1,0:T(8,128)}), f32[16,32,256]{2,1,0:T(8,128)}, u32[]{:S(2)}, u32[]{:S(2)}) async-start(f32[16,32,256]{2,1,0:T(8,128)} %convolution_bitcast_fusion), calls=%async_computation | async-start | bytes 1048576 | tf_op jit(solution)/shard_map/all_to_all | solution.py:35
  78.8 55.0 %all-to-all-start.2 = ((bf16[32,128,256]{2,1,0:T(8,128)(2,1)}), bf16[32,128,256]{2,1,0:T(8,128)(2,1)}, u32[]{:S(2)}, u32[]{:S(2)}) async-start(bf16[32,128,256]{2,1,0:T(8,128)(2,1)} %bitcast.54), calls=%async_computation.2 | async-start | bytes 4194304 | tf_op jit(solution)/shard_map/all_to_all | solution.py:56
  85.9 47.9 %copy-start.3 = (s32[2048]{0:T(1024)}, s32[2048]{0:T(1024)S(1)}, u32[]{:S(2)}) copy-start(s32[2048]{0:T(1024)S(1)} %multiply_add_fusion) | copy-start | bytes 24580
  149.2 23.3 %all-to-all-start.3 = ((f32[16,512,4]{1,2,0:T(4,128)}), f32[16,512,4]{1,2,0:T(4,128)S(1)}, u32[]{:S(2)}, u32[]{:S(2)}) async-start(f32[16,512,4]{1,2,0:T(4,128)} %broadcast_in_dim.2), calls=%async_computation.3 | async-start | bytes 262144 | tf_op jit(solution)/shard_map/all_to_all | solution.py:71
  172.5 6.2 %copy-start.2 = (s32[512,4]{0,1:T(4,128)S(1)}, s32[512,4]{0,1:T(4,128)}, u32[]{:S(2)}) copy-start(s32[512,4]{0,1:T(4,128)} %param.13) | copy-start | bytes 24580
  172.5 35.3 %all-to-all-start.4 = ((bf16[32,128,256]{2,1,0:T(8,128)(2,1)}), bf16[32,128,256]{2,1,0:T(8,128)(2,1)S(1)}, u32[]{:S(2)}, u32[]{:S(2)}) async-start(bf16[32,128,256]{2,1,0:T(8,128)(2,1)} %bitcast.53), calls=%async_computation.4 | async-start | bytes 4194304 | tf_op jit(solution)/shard_map/all_to_all | solution.py:64
Sparse Core Ops, SparseCore 0:
  10.0 118.2 all-gather.1

commit v10 on v4

--- a/solution.py
+++ b/solution.py
@@ -73,18 +73,22 @@
     ).astype(jnp.bfloat16)
     served_g = pick_rows(asked, g_own).reshape(n_dp, CAP, e_local)
     back_g = lax.all_to_all(served_g, "dp", 0, 0, tiled=True).reshape(n_dp * CAP, e_local)
-    g_vec = pick_rows(slot, back_g).reshape(rows, K, e_local).astype(jnp.float32)
 
     old_wide = old_vec.astype(jnp.float32)
     scale = 1.0 / math.sqrt(E)
     partial_scores = jnp.einsum("re,rke->rk", new, old_wide)
-    spread = jnp.broadcast_to(partial_scores[None], (n_wide,) + partial_scores.shape)
-    gathered = lax.all_to_all(spread, "wide", 0, 0, tiled=True)
-    score = jnp.sum(gathered, axis=0) * scale
+    score = lax.psum(partial_scores, "wide") * scale
     sign = 2.0 * labels.astype(jnp.float32) - 1.0
     pair_loss = jax.nn.softplus(-sign * score)
     dscore = -sign * jax.nn.sigmoid(-sign * score)
-    trunk_grad = jnp.einsum("rk,rke->re", dscore, g_vec) * scale
+    by_slot = slot.reshape(rows, K)[:, :, None] == jnp.arange(n_dp * CAP, dtype=jnp.int32)
+    weights = jnp.sum(jnp.where(by_slot, dscore[:, :, None], 0.0), axis=1)
+    high = weights.astype(jnp.bfloat16)
+    low = (weights - high.astype(jnp.float32)).astype(jnp.bfloat16)
+    trunk_grad = (
+        jnp.dot(high, back_g, preferred_element_type=jnp.float32)
+        + jnp.dot(low, back_g, preferred_element_type=jnp.float32)
+    ) * scale
     return (new.astype(jnp.bfloat16), pair_loss, trunk_grad.astype(jnp.bfloat16))
 
 

time: 216 us -> 230 us (1.065)
  the two profiles are of different devices: /device:TPU:32 before, /device:TPU:6 now
where the time goes in v10:
time: 230 us; the launch traced here: 229 us
  starting transfers between devices  81.1 us (35%)
  matrix products  40.7 us (18%)
  blocking collectives  27.7 us (12%)
  local copies, waits for them, and re-layouts  26.6 us (12%)
  waiting for transfers between devices  23.1 us (10%)
  other arithmetic  15.2 us (7%)
  between operations  14.4 us (6%)
    ppermute x7, starting transfers between devices, local(): to_left = lax.ppermute(to_left, 'wide', left)  41.3 us
    psum x1, blocking collectives, local(): score = lax.psum(partial_scores, 'wide') * scale  27.7 us
    dot_general x3, matrix products, pick_rows(): jnp.dot(one_hot(index, table.shape[0]), table, preferred_element_type=jnp...  21.8 us
    dynamic_update_slice x16, local copies, waits for them, and re-layouts, place(): return lax.dynamic_update_slice_in_dim(full, block, source * e_local, 1)  18.7 us
    ppermute x8, waiting for transfers between devices, local(): to_right = lax.ppermute(to_right, 'wide', right)  18.7 us
    ppermute x8, starting transfers between devices, local(): to_right = lax.ppermute(to_right, 'wide', right)  17.4 us
    reduce_sum x1, other arithmetic, local(): weights = jnp.sum(jnp.where(by_slot, dscore[:, :, None], 0.0), axis=1)  11.2 us
    all_to_all x1, starting transfers between devices, local(): asked = lax.all_to_all(req, 'dp', 0, 0, tiled=True).reshape(-1)  7.57 us
  transfers between devices with their start and end apart: 19, of which 6 were waited for; matrix products, arithmetic and copies ran while one was open for 29% of the time, Pallas kernels for 0%

profile of v10, /device:TPU:6, one launch (start us, length us, event | category | flops | bytes accessed | tf_op | source)
XLA Modules:
  0.0 228.9 jit_solution(18340430571338795795)
XLA Ops:
  8.4 5.8 %convolution_convert_fusion = bf16[512,4096]{1,0:T(8,128)(2,1)} fusion(bf16[512,1024]{1,0:T(8,128)(2,1)S(1)} %copy-done, bf16[1024,256]{1,0:T(8,128)(2,1)} %param.8, bf16[256,4096]{1,0:T(8,128)(2,1)} %param.9, bf16[32,8,32,128]{3,2,1,0:T(8,128)(2,1)S(1)} %bitcast.32), kind=kOutput, calls=%fused_computation.11 | convolution fusion | flops 1345454080 | bytes 9961472 | tf_op jit(solution)/shard_map/dot_general | solution.py:31
  14.2 3.8 %collective-permute-start = (bf16[512,256]{1,0:T(8,128)(2,1)}, bf16[512,256]{1,0:T(8,128)(2,1)}, u32[]{:S(2)}, u32[]{:S(2)}) collective-permute-start(bf16[512,256]{1,0:T(8,128)(2,1)} %param.11), channel_id=1, source_target_pairs={{0,1},{1,2},{2,3},{3,4},{4,5},{5,6},{6,7},{7,8},{8,9},{9,10},{10,1... | collective-permute-start | bytes 786440 | tf_op jit(solution)/shard_map/ppermute | solution.py:66
  18.1 9.5 %collective-permute-start.1 = (bf16[512,256]{1,0:T(8,128)(2,1)}, bf16[512,256]{1,0:T(8,128)(2,1)}, u32[]{:S(2)}, u32[]{:S(2)}) collective-permute-start(bf16[512,256]{1,0:T(8,128)(2,1)} %param.11), channel_id=1, source_target_pairs={{0,15},{1,0},{2,1},{3,2},{4,3},{5,4},{6,5},{7,6},{8,7},{9,8},{10,9... | collective-permute-start | bytes 786440 | tf_op jit(solution)/shard_map/ppermute | solution.py:69
  30.9 7.6 %all-to-all-start = ((s32[32,1,128]{2,1,0:T(1,128)}), s32[32,1,128]{2,1,0:T(1,128)S(1)}, u32[]{:S(2)}, u32[]{:S(2)}) async-start(s32[32,1,128]{2,1,0:T(1,128)} %bitcast.5), calls=%async_computation.1 | async-start | bytes 32768 | tf_op jit(solution)/shard_map/all_to_all | solution.py:51
  38.5 1.9 collective-permute-start.2
  43.4 5.3 %collective-permute-start.3 = (bf16[512,256]{1,0:T(8,128)(2,1)}, bf16[512,256]{1,0:T(8,128)(2,1)}, u32[]{:S(2)}, u32[]{:S(2)}) collective-permute-start(bf16[512,256]{1,0:T(8,128)(2,1)} %collective-permute-done.1), channel_id=1, source_target_pairs={{0,15},{1,0},{2,1},{3,2},{4,3},{5,4},{6,5},{7,6},{8,7},{9,8},{10,9... | collective-permute-start | bytes 786440 | tf_op jit(solution)/shard_map/ppermute | solution.py:69
  48.7 7.6 %collective-permute-done.2 = bf16[512,256]{1,0:T(8,128)(2,1)} collective-permute-done((bf16[512,256]{1,0:T(8,128)(2,1)}, bf16[512,256]{1,0:T(8,128)(2,1)}, u32[]{:S(2)}, u32[]{:S(2)}) %collective-permute-start.2) | collective-permute-done | bytes 262176 | tf_op jit(solution)/shard_map/ppermute | solution.py:66
  56.3 1.9 collective-permute-start.4
  58.2 2.5 %broadcast_in_dim.12 = bf16[512,4096]{1,0:T(8,128)(2,1)} broadcast(bf16[]{:T(256)} %constant.146.clone.1), dimensions={} | broadcast | bytes 4194306 | tf_op jit(solution)/shard_map/broadcast_in_dim | solution.py:63
  62.6 5.1 %collective-permute-start.5 = (bf16[512,256]{1,0:T(8,128)(2,1)}, bf16[512,256]{1,0:T(8,128)(2,1)S(1)}, u32[]{:S(2)}, u32[]{:S(2)}) collective-permute-start(bf16[512,256]{1,0:T(8,128)(2,1)} %collective-permute-done.3), channel_id=1, source_target_pairs={{0,15},{1,0},{2,1},{3,2},{4,3},{5,4},{6,5},{7,6},{8,7},{9,8},{10,9... | collective-permute-start | bytes 786440 | tf_op jit(solution)/shard_map/ppermute | solution.py:69
  67.8 5.6 %collective-permute-done.4 = bf16[512,256]{1,0:T(8,128)(2,1)} collective-permute-done((bf16[512,256]{1,0:T(8,128)(2,1)}, bf16[512,256]{1,0:T(8,128)(2,1)}, u32[]{:S(2)}, u32[]{:S(2)}) %collective-permute-start.4) | collective-permute-done | bytes 262176 | tf_op jit(solution)/shard_map/ppermute | solution.py:66
  73.4 1.9 collective-permute-start.6
  75.3 4.2 %fusion.5 = bf16[4096,256]{1,0:T(8,128)(2,1)} fusion(bf16[512,256]{1,0:T(8,128)(2,1)} %param.11, s32[4096]{0:T(1024)S(1)} %bitcast.39), kind=kOutput, calls=%fused_computation.12 | convolution fusion | flops 1076887552 | bytes 2375680 | tf_op jit(solution)/shard_map/dot_general | solution.py:18
  79.5 7.4 %all-to-all-start.1 = ((bf16[32,128,256]{2,1,0:T(8,128)(2,1)}), bf16[32,128,256]{2,1,0:T(8,128)(2,1)}, u32[]{:S(2)}, u32[]{:S(2)}) async-start(bf16[32,128,256]{2,1,0:T(8,128)(2,1)} %bitcast.36), calls=%async_computation.2 | async-start | bytes 4194304 | tf_op jit(solution)/shard_map/all_to_all | solution.py:53
  88.7 5.1 %collective-permute-start.7 = (bf16[512,256]{1,0:T(8,128)(2,1)S(1)}, bf16[512,256]{1,0:T(8,128)(2,1)S(1)}, u32[]{:S(2)}, u32[]{:S(2)}) collective-permute-start(bf16[512,256]{1,0:T(8,128)(2,1)S(1)} %collective-permute-done.5), channel_id=1, source_target_pairs={{0,15},{1,0},{2,1},{3,2},{4,3},{5,4},{6,5},{7,6},{8,7},{9,8},{10,9... | collective-permute-start | bytes 786440 | tf_op jit(solution)/shard_map/ppermute | solution.py:69
  95.5 1.9 collective-permute-start.8
  100.9 4.1 %collective-permute-done.7 = bf16[512,256]{1,0:T(8,128)(2,1)S(1)} collective-permute-done((bf16[512,256]{1,0:T(8,128)(2,1)S(1)}, bf16[512,256]{1,0:T(8,128)(2,1)S(1)}, u32[]{:S(2)}, u32[]{:S(2)}) %collective-permute-start.7) | collective-permute-done | bytes 262176 | tf_op jit(solution)/shard_map/ppermute | solution.py:69
  105.0 5.6 %collective-permute-start.9 = (bf16[512,256]{1,0:T(8,128)(2,1)S(1)}, bf16[512,256]{1,0:T(8,128)(2,1)S(1)}, u32[]{:S(2)}, u32[]{:S(2)}) collective-permute-start(bf16[512,256]{1,0:T(8,128)(2,1)S(1)} %collective-permute-done.7), channel_id=1, source_target_pairs={{0,15},{1,0},{2,1},{3,2},{4,3},{5,4},{6,5},{7,6},{8,7},{9,8},{10,9... | collective-permute-start | bytes 786440 | tf_op jit(solution)/shard_map/ppermute | solution.py:69
  112.3 1.9 collective-permute-start.10
  116.7 5.1 %collective-permute-start.11 = (bf16[512,256]{1,0:T(8,128)(2,1)S(1)}, bf16[512,256]{1,0:T(8,128)(2,1)S(1)}, u32[]{:S(2)}, u32[]{:S(2)}) collective-permute-start(bf16[512,256]{1,0:T(8,128)(2,1)S(1)} %collective-permute-done.9), channel_id=1, source_target_pairs={{0,15},{1,0},{2,1},{3,2},{4,3},{5,4},{6,5},{7,6},{8,7},{9,8},{10,9... | collective-permute-start | bytes 786440 | tf_op jit(solution)/shard_map/ppermute | solution.py:69
  126.5 5.6 %collective-permute-start.13 = (bf16[512,256]{1,0:T(8,128)(2,1)S(1)}, bf16[512,256]{1,0:T(8,128)(2,1)S(1)}, u32[]{:S(2)}, u32[]{:S(2)}) collective-permute-start(bf16[512,256]{1,0:T(8,128)(2,1)S(1)} %collective-permute-done.11), channel_id=1, source_target_pairs={{0,15},{1,0},{2,1},{3,2},{4,3},{5,4},{6,5},{7,6},{8,7},{9,8},{10,9... | collective-permute-start | bytes 786440 | tf_op jit(solution)/shard_map/ppermute | solution.py:69
  132.9 2.1 collective-permute-start.14
  137.2 5.1 %collective-permute-done.14 = bf16[512,256]{1,0:T(8,128)(2,1)S(1)} collective-permute-done((bf16[512,256]{1,0:T(8,128)(2,1)S(1)}, bf16[512,256]{1,0:T(8,128)(2,1)S(1)}, u32[]{:S(2)}, u32[]{:S(2)}) %collective-permute-start.14) | collective-permute-done | bytes 262176 | tf_op jit(solution)/shard_map/ppermute | solution.py:66
  143.1 8.8 %fusion.6 = bf16[4096,256]{1,0:T(8,128)(2,1)} fusion(s32[4096]{0:T(1024)S(1)} %bitcast.40, bf16[512,4096]{1,0:T(8,128)(2,1)} %constant_dynamic-update-slice_fusion, bf16[256,4096]{1,0:T(8,128)(2,1)} %param.9, bf16[32,8,32,128]{3,2,1,0:T(8,128)(2,1)S(1)} %bitcast.33), kind=kOutput, calls=%fused_computation.13 | convolution fusion | flops 2151809024 | bytes 10502144 | tf_op jit(solution)/shard_map/dot_general | solution.py:18
  151.9 7.4 %all-to-all-start.2 = ((bf16[32,128,256]{2,1,0:T(8,128)(2,1)}), bf16[32,128,256]{2,1,0:T(8,128)(2,1)S(1)}, u32[]{:S(2)}, u32[]{:S(2)}) async-start(bf16[32,128,256]{2,1,0:T(8,128)(2,1)} %bitcast.37), calls=%async_computation.3 | async-start | bytes 4194304 | tf_op jit(solution)/shard_map/all_to_all | solution.py:75
  159.3 8.8 %fusion.10 = bf16[2048,256]{1,0:T(8,128)(2,1)} fusion(bf16[4096,256]{1,0:T(8,128)(2,1)} %bitcast.8, s32[2048]{0:T(1024)S(1)} %multiply_add_fusion), kind=kOutput, calls=%fused_computation.17 | convolution fusion | flops 4303880192 | bytes 3153920 | tf_op jit(solution)/shard_map/dot_general | solution.py:18
  168.1 2.2 reshape.292
  170.3 2.0 fusion.30
  172.4 27.7 %psum.7 = f32[512,4]{0,1:T(4,128)S(1)} all-reduce(f32[512,4]{0,1:T(4,128)S(1)} %bitcast.38), channel_id=1, replica_groups=mesh['dp'=32,'wide'=16] {'wide'}, use_global_device_ids=true, to_apply=%region_2.3 | all-reduce | flops 2048 | bytes 16384 | tf_op jit(solution)/shard_map/psum | solution.py:80
  200.8 11.2 %select_reduce_fusion = f32[512,4096]{1,0:T(8,128)} fusion(f32[512,4]{0,1:T(4,128)S(1)} %get-tuple-element.5, s32[512,4]{0,1:T(4,128)S(1)} %copy.43), kind=kLoop, calls=%fused_computation | loop fusion | flops 23068672 | bytes 8404992 | tf_op jit(solution)/shard_map/reduce_sum | solution.py:85
  211.9 7.2 %fusion.7 = f32[512,256]{1,0:T(8,128)S(1)} fusion(bf16[4096,256]{1,0:T(8,128)(2,1)S(1)} %bitcast.34, f32[512,4096]{1,0:T(8,128)} %select_reduce_fusion), kind=kOutput, calls=%fused_computation.14 | convolution fusion | flops 1082130432 | bytes 11010048 | tf_op jit(solution)/shard_map/dot_general | solution.py:90
  220.1 2.0 fusion.21
  (66 shorter events, 30.5 us)
Async XLA Ops:
  7.2 1.2 copy-start
  7.2 163.1 %reduce-scatter.2.cloned.1.call-start = ((), (), s32[]{:S(2)}) async-start(), calls=%async_computation.4 | async-start | bytes 4456448 | tf_op jit(solution)/shard_map/reduce_scatter | solution.py:32
  14.2 13.4 %copy-start.3 = (s32[512,4]{0,1:T(4,128)S(1)}, s32[512,4]{0,1:T(4,128)}, u32[]{:S(2)}) copy-start(s32[512,4]{0,1:T(4,128)} %param.12) | copy-start | bytes 24580
  14.2 24.2 %collective-permute-start = (bf16[512,256]{1,0:T(8,128)(2,1)}, bf16[512,256]{1,0:T(8,128)(2,1)}, u32[]{:S(2)}, u32[]{:S(2)}) collective-permute-start(bf16[512,256]{1,0:T(8,128)(2,1)} %param.11), channel_id=1, source_target_pairs={{0,1},{1,2},{2,3},{3,4},{4,5},{5,6},{6,7},{7,8},{8,9},{9,10},{10,1... | collective-permute-start | bytes 786440 | tf_op jit(solution)/shard_map/ppermute | solution.py:66
  18.1 25.4 %collective-permute-start.1 = (bf16[512,256]{1,0:T(8,128)(2,1)}, bf16[512,256]{1,0:T(8,128)(2,1)}, u32[]{:S(2)}, u32[]{:S(2)}) collective-permute-start(bf16[512,256]{1,0:T(8,128)(2,1)} %param.11), channel_id=1, source_target_pairs={{0,15},{1,0},{2,1},{3,2},{4,3},{5,4},{6,5},{7,6},{8,7},{9,8},{10,9... | collective-permute-start | bytes 786440 | tf_op jit(solution)/shard_map/ppermute | solution.py:69
  30.9 44.4 %all-to-all-start = ((s32[32,1,128]{2,1,0:T(1,128)}), s32[32,1,128]{2,1,0:T(1,128)S(1)}, u32[]{:S(2)}, u32[]{:S(2)}) async-start(s32[32,1,128]{2,1,0:T(1,128)} %bitcast.5), calls=%async_computation.1 | async-start | bytes 32768 | tf_op jit(solution)/shard_map/all_to_all | solution.py:51
  38.5 17.8 %collective-permute-start.2 = (bf16[512,256]{1,0:T(8,128)(2,1)}, bf16[512,256]{1,0:T(8,128)(2,1)}, u32[]{:S(2)}, u32[]{:S(2)}) collective-permute-start(bf16[512,256]{1,0:T(8,128)(2,1)} %collective-permute-done), channel_id=1, source_target_pairs={{0,1},{1,2},{2,3},{3,4},{4,5},{5,6},{6,7},{7,8},{8,9},{9,10},{10,1... | collective-permute-start | bytes 786440 | tf_op jit(solution)/shard_map/ppermute | solution.py:66
  43.4 19.0 %copy-start.2 = (s32[512,4]{1,0:T(8,128)S(1)}, s32[512,4]{1,0:T(8,128)}, u32[]{:S(2)}) copy-start(s32[512,4]{1,0:T(8,128)} %fusion.34) | copy-start | bytes 24580
  43.4 19.2 %collective-permute-start.3 = (bf16[512,256]{1,0:T(8,128)(2,1)}, bf16[512,256]{1,0:T(8,128)(2,1)}, u32[]{:S(2)}, u32[]{:S(2)}) collective-permute-start(bf16[512,256]{1,0:T(8,128)(2,1)} %collective-permute-done.1), channel_id=1, source_target_pairs={{0,15},{1,0},{2,1},{3,2},{4,3},{5,4},{6,5},{7,6},{8,7},{9,8},{10,9... | collective-permute-start | bytes 786440 | tf_op jit(solution)/shard_map/ppermute | solution.py:69
  56.3 17.1 %collective-permute-start.4 = (bf16[512,256]{1,0:T(8,128)(2,1)}, bf16[512,256]{1,0:T(8,128)(2,1)}, u32[]{:S(2)}, u32[]{:S(2)}) collective-permute-start(bf16[512,256]{1,0:T(8,128)(2,1)} %collective-permute-done.2), channel_id=1, source_target_pairs={{0,1},{1,2},{2,3},{3,4},{4,5},{5,6},{6,7},{7,8},{8,9},{9,10},{10,1... | collective-permute-start | bytes 786440 | tf_op jit(solution)/shard_map/ppermute | solution.py:66
  62.6 26.1 %collective-permute-start.5 = (bf16[512,256]{1,0:T(8,128)(2,1)}, bf16[512,256]{1,0:T(8,128)(2,1)S(1)}, u32[]{:S(2)}, u32[]{:S(2)}) collective-permute-start(bf16[512,256]{1,0:T(8,128)(2,1)} %collective-permute-done.3), channel_id=1, source_target_pairs={{0,15},{1,0},{2,1},{3,2},{4,3},{5,4},{6,5},{7,6},{8,7},{9,8},{10,9... | collective-permute-start | bytes 786440 | tf_op jit(solution)/shard_map/ppermute | solution.py:69
  73.4 22.1 %collective-permute-start.6 = (bf16[512,256]{1,0:T(8,128)(2,1)}, bf16[512,256]{1,0:T(8,128)(2,1)}, u32[]{:S(2)}, u32[]{:S(2)}) collective-permute-start(bf16[512,256]{1,0:T(8,128)(2,1)} %collective-permute-done.4), channel_id=1, source_target_pairs={{0,1},{1,2},{2,3},{3,4},{4,5},{5,6},{6,7},{7,8},{8,9},{9,10},{10,1... | collective-permute-start | bytes 786440 | tf_op jit(solution)/shard_map/ppermute | solution.py:66
  79.5 72.4 %all-to-all-start.1 = ((bf16[32,128,256]{2,1,0:T(8,128)(2,1)}), bf16[32,128,256]{2,1,0:T(8,128)(2,1)}, u32[]{:S(2)}, u32[]{:S(2)}) async-start(bf16[32,128,256]{2,1,0:T(8,128)(2,1)} %bitcast.36), calls=%async_computation.2 | async-start | bytes 4194304 | tf_op jit(solution)/shard_map/all_to_all | solution.py:53
  88.7 16.2 %collective-permute-start.7 = (bf16[512,256]{1,0:T(8,128)(2,1)S(1)}, bf16[512,256]{1,0:T(8,128)(2,1)S(1)}, u32[]{:S(2)}, u32[]{:S(2)}) collective-permute-start(bf16[512,256]{1,0:T(8,128)(2,1)S(1)} %collective-permute-done.5), channel_id=1, source_target_pairs={{0,15},{1,0},{2,1},{3,2},{4,3},{5,4},{6,5},{7,6},{8,7},{9,8},{10,9... | collective-permute-start | bytes 786440 | tf_op jit(solution)/shard_map/ppermute | solution.py:69
  95.5 16.8 %collective-permute-start.8 = (bf16[512,256]{1,0:T(8,128)(2,1)}, bf16[512,256]{1,0:T(8,128)(2,1)S(1)}, u32[]{:S(2)}, u32[]{:S(2)}) collective-permute-start(bf16[512,256]{1,0:T(8,128)(2,1)} %collective-permute-done.6), channel_id=1, source_target_pairs={{0,1},{1,2},{2,3},{3,4},{4,5},{5,6},{6,7},{7,8},{8,9},{9,10},{10,1... | collective-permute-start | bytes 786440 | tf_op jit(solution)/shard_map/ppermute | solution.py:66
  105.0 11.7 %collective-permute-start.9 = (bf16[512,256]{1,0:T(8,128)(2,1)S(1)}, bf16[512,256]{1,0:T(8,128)(2,1)S(1)}, u32[]{:S(2)}, u32[]{:S(2)}) collective-permute-start(bf16[512,256]{1,0:T(8,128)(2,1)S(1)} %collective-permute-done.7), channel_id=1, source_target_pairs={{0,15},{1,0},{2,1},{3,2},{4,3},{5,4},{6,5},{7,6},{8,7},{9,8},{10,9... | collective-permute-start | bytes 786440 | tf_op jit(solution)/shard_map/ppermute | solution.py:69
  112.3 10.6 %collective-permute-start.10 = (bf16[512,256]{1,0:T(8,128)(2,1)S(1)}, bf16[512,256]{1,0:T(8,128)(2,1)S(1)}, u32[]{:S(2)}, u32[]{:S(2)}) collective-permute-start(bf16[512,256]{1,0:T(8,128)(2,1)S(1)} %collective-permute-done.8), channel_id=1, source_target_pairs={{0,1},{1,2},{2,3},{3,4},{4,5},{5,6},{6,7},{7,8},{8,9},{9,10},{10,1... | collective-permute-start | bytes 786440 | tf_op jit(solution)/shard_map/ppermute | solution.py:66
  116.7 9.8 %collective-permute-start.11 = (bf16[512,256]{1,0:T(8,128)(2,1)S(1)}, bf16[512,256]{1,0:T(8,128)(2,1)S(1)}, u32[]{:S(2)}, u32[]{:S(2)}) collective-permute-start(bf16[512,256]{1,0:T(8,128)(2,1)S(1)} %collective-permute-done.9), channel_id=1, source_target_pairs={{0,15},{1,0},{2,1},{3,2},{4,3},{5,4},{6,5},{7,6},{8,7},{9,8},{10,9... | collective-permute-start | bytes 786440 | tf_op jit(solution)/shard_map/ppermute | solution.py:69
  122.9 10.0 %collective-permute-start.12 = (bf16[512,256]{1,0:T(8,128)(2,1)S(1)}, bf16[512,256]{1,0:T(8,128)(2,1)S(1)}, u32[]{:S(2)}, u32[]{:S(2)}) collective-permute-start(bf16[512,256]{1,0:T(8,128)(2,1)S(1)} %collective-permute-done.10), channel_id=1, source_target_pairs={{0,1},{1,2},{2,3},{3,4},{4,5},{5,6},{6,7},{7,8},{8,9},{9,10},{10,1... | collective-permute-start | bytes 786440 | tf_op jit(solution)/shard_map/ppermute | solution.py:66
  126.5 9.9 %collective-permute-start.13 = (bf16[512,256]{1,0:T(8,128)(2,1)S(1)}, bf16[512,256]{1,0:T(8,128)(2,1)S(1)}, u32[]{:S(2)}, u32[]{:S(2)}) collective-permute-start(bf16[512,256]{1,0:T(8,128)(2,1)S(1)} %collective-permute-done.11), channel_id=1, source_target_pairs={{0,15},{1,0},{2,1},{3,2},{4,3},{5,4},{6,5},{7,6},{8,7},{9,8},{10,9... | collective-permute-start | bytes 786440 | tf_op jit(solution)/shard_map/ppermute | solution.py:69
  132.9 9.5 %collective-permute-start.14 = (bf16[512,256]{1,0:T(8,128)(2,1)S(1)}, bf16[512,256]{1,0:T(8,128)(2,1)S(1)}, u32[]{:S(2)}, u32[]{:S(2)}) collective-permute-start(bf16[512,256]{1,0:T(8,128)(2,1)S(1)} %collective-permute-done.12), channel_id=1, source_target_pairs={{0,1},{1,2},{2,3},{3,4},{4,5},{5,6},{6,7},{7,8},{8,9},{9,10},{10,1... | collective-permute-start | bytes 786440 | tf_op jit(solution)/shard_map/ppermute | solution.py:66
  151.9 60.0 %all-to-all-start.2 = ((bf16[32,128,256]{2,1,0:T(8,128)(2,1)}), bf16[32,128,256]{2,1,0:T(8,128)(2,1)S(1)}, u32[]{:S(2)}, u32[]{:S(2)}) async-start(bf16[32,128,256]{2,1,0:T(8,128)(2,1)} %bitcast.37), calls=%async_computation.3 | async-start | bytes 4194304 | tf_op jit(solution)/shard_map/all_to_all | solution.py:75
  168.1 32.1 %copy-start.4 = (s32[512,4]{0,1:T(4,128)S(1)}, s32[512,4]{0,1:T(4,128)}, u32[]{:S(2)}) copy-start(s32[512,4]{0,1:T(4,128)} %param.13) | copy-start | bytes 24580
  211.9 8.2 %copy-start.1 = (f32[512,4096]{1,0:T(8,128)S(1)}, f32[512,4096]{1,0:T(8,128)}, u32[]{:S(2)}) copy-start(f32[512,4096]{1,0:T(8,128)} %select_reduce_fusion) | copy-start | bytes 25165828
Sparse Core Ops, SparseCore 0:
  14.4 96.5 reduce-scatter.1

commit v11 on v3

--- a/solution.py
+++ b/solution.py
@@ -28,10 +28,26 @@
     query = jnp.dot(trunk_out, projection, preferred_element_type=jnp.float32).astype(jnp.bfloat16)
     blocks = transform.reshape(local_blocks, side, nblocks, side)
     masked = (blocks * block_mask[:, None, :, None].astype(jnp.bfloat16)).reshape(e_local, width)
-    term = jnp.dot(query, masked, preferred_element_type=jnp.float32)
-    new = lax.psum_scatter(
-        term.astype(jnp.bfloat16), "wide", scatter_dimension=1, tiled=True
-    ).astype(jnp.float32)
+    term = jnp.dot(query, masked, preferred_element_type=jnp.float32).astype(jnp.bfloat16)
+
+    me_w = lax.axis_index("wide")
+    right = [(i, (i + 1) % n_wide) for i in range(n_wide)]
+    left = [(i, (i - 1) % n_wide) for i in range(n_wide)]
+
+    def part(block):
+        return lax.dynamic_slice_in_dim(term, (block % n_wide) * e_local, e_local, 1)
+
+    far_r, far_l = n_wide // 2, n_wide - 1 - n_wide // 2
+    run_r, run_l = part(me_w + far_r), part(me_w - far_l)
+    for step in range(1, far_r + 1):
+        run_r = lax.ppermute(run_r, "wide", right)
+        if step < far_r:
+            run_r = (run_r.astype(jnp.float32) + part(me_w - step + far_r)).astype(jnp.bfloat16)
+        if step <= far_l:
+            run_l = lax.ppermute(run_l, "wide", left)
+            if step < far_l:
+                run_l = (run_l.astype(jnp.float32) + part(me_w + step - far_l)).astype(jnp.bfloat16)
+    new = run_r.astype(jnp.float32) + run_l.astype(jnp.float32) + part(me_w).astype(jnp.float32)
 
     flat = doc_ids.reshape(-1)
     count = flat.shape[0]

time: 256 us -> 242 us (0.945)
  the two profiles are of different devices: /device:TPU:6 before, /device:TPU:32 now
where the time goes in v11:
time: 242 us; the launch traced here: 240 us
  starting transfers between devices  83.7 us (35%)
  waiting for transfers between devices  73.6 us (30%)
  matrix products  39.4 us (16%)
  other arithmetic  20.8 us (9%)
  between operations  14.7 us (6%)
  local copies, waits for them, and re-layouts  8.18 us (3%)
    ppermute x8, waiting for transfers between devices, local(): run_r = lax.ppermute(run_r, 'wide', right)  36.5 us
    ppermute x7, starting transfers between devices, local(): run_l = lax.ppermute(run_l, 'wide', left)  27.8 us
    dot_general x4, matrix products, pick_rows(): jnp.dot(one_hot(index, table.shape[0]), table, preferred_element_type=jnp...  27.2 us
    all_to_all x1, waiting for transfers between devices, local(): lax.all_to_all(served_g, 'dp', 0, 0, tiled=True)  27 us
    ppermute x8, starting transfers between devices, local(): run_r = lax.ppermute(run_r, 'wide', right)  23.9 us
    convert_element_type x7, other arithmetic, local(): (run_r.astype(jnp.float32) + part(me_w - step + far_r)).astype(jnp.bfloat16)  14.3 us
    all_to_all x1, starting transfers between devices, local(): gathered = lax.all_to_all(spread, 'wide', 0, 0, tiled=True)  8.75 us
    all_to_all x1, starting transfers between devices, local(): lax.all_to_all(served_g, 'dp', 0, 0, tiled=True)  8.17 us
  transfers between devices with their start and end apart: 20, of which 9 were waited for; matrix products, arithmetic and copies ran while one was open for 24% of the time, Pallas kernels for 0%

profile of v11, /device:TPU:32, one launch (start us, length us, event | category | flops | bytes accessed | tf_op | source)
XLA Modules:
  0.0 240.4 jit_solution(15400994253087877097)
XLA Ops:
  9.0 5.9 %convolution_convert_fusion = bf16[512,4096]{1,0:T(8,128)(2,1)} fusion(bf16[512,1024]{1,0:T(8,128)(2,1)S(1)} %copy-done, bf16[1024,256]{1,0:T(8,128)(2,1)} %param.8, bf16[256,4096]{1,0:T(8,128)(2,1)} %param.9, bf16[32,8,32,128]{3,2,1,0:T(8,128)(2,1)S(1)} %bitcast.40), kind=kOutput, calls=%fused_computation.10 | convolution fusion | flops 1345454080 | bytes 9961472 | tf_op jit(solution)/shard_map/dot_general | solution.py:31
  16.7 3.8 %collective-permute-start = (bf16[512,256]{1,0:T(8,128)(2,1)}, bf16[512,256]{1,0:T(8,128)(2,1)}, u32[]{:S(2)}, u32[]{:S(2)}) collective-permute-start(bf16[512,256]{1,0:T(8,128)(2,1)} %get-tuple-element.17), channel_id=1, source_target_pairs={{0,1},{1,2},{2,3},{3,4},{4,5},{5,6},{6,7},{7,8},{8,9},{9,10},{10,1... | collective-permute-start | bytes 786440 | tf_op jit(solution)/shard_map/ppermute | solution.py:43
  20.6 5.5 %collective-permute-start.8 = (bf16[512,256]{1,0:T(8,128)(2,1)}, bf16[512,256]{1,0:T(8,128)(2,1)}, u32[]{:S(2)}, u32[]{:S(2)}) collective-permute-start(bf16[512,256]{1,0:T(8,128)(2,1)} %get-tuple-element.18), channel_id=1, source_target_pairs={{0,15},{1,0},{2,1},{3,2},{4,3},{5,4},{6,5},{7,6},{8,7},{9,8},{10,9... | collective-permute-start | bytes 786440 | tf_op jit(solution)/shard_map/ppermute | solution.py:47
  30.6 2.2 collective-permute-start.1
  34.3 15.5 %collective-permute-done.1 = bf16[512,256]{1,0:T(8,128)(2,1)} collective-permute-done((bf16[512,256]{1,0:T(8,128)(2,1)}, bf16[512,256]{1,0:T(8,128)(2,1)}, u32[]{:S(2)}, u32[]{:S(2)}) %collective-permute-start.1) | collective-permute-done | bytes 262176 | tf_op jit(solution)/shard_map/ppermute | solution.py:43
  49.8 2.1 add_convert_fusion.11
  53.9 3.9 %collective-permute-start.9 = (bf16[512,256]{1,0:T(8,128)(2,1)}, bf16[512,256]{1,0:T(8,128)(2,1)}, u32[]{:S(2)}, u32[]{:S(2)}) collective-permute-start(bf16[512,256]{1,0:T(8,128)(2,1)} %get-tuple-element.16), channel_id=1, source_target_pairs={{0,15},{1,0},{2,1},{3,2},{4,3},{5,4},{6,5},{7,6},{8,7},{9,8},{10,9... | collective-permute-start | bytes 786440 | tf_op jit(solution)/shard_map/ppermute | solution.py:47
  59.8 7.5 %all-to-all-start = ((s32[32,1,128]{2,1,0:T(1,128)}), s32[32,1,128]{2,1,0:T(1,128)S(1)}, u32[]{:S(2)}, u32[]{:S(2)}) async-start(s32[32,1,128]{2,1,0:T(1,128)} %bitcast.5), calls=%async_computation | async-start | bytes 32768 | tf_op jit(solution)/shard_map/all_to_all | solution.py:67
  67.4 2.1 add_convert_fusion.10
  71.5 4.1 %collective-permute-start.10 = (bf16[512,256]{1,0:T(8,128)(2,1)}, bf16[512,256]{1,0:T(8,128)(2,1)}, u32[]{:S(2)}, u32[]{:S(2)}) collective-permute-start(bf16[512,256]{1,0:T(8,128)(2,1)} %get-tuple-element.14), channel_id=1, source_target_pairs={{0,15},{1,0},{2,1},{3,2},{4,3},{5,4},{6,5},{7,6},{8,7},{9,8},{10,9... | collective-permute-start | bytes 786440 | tf_op jit(solution)/shard_map/ppermute | solution.py:47
  75.6 3.3 %fusion.7 = bf16[4096,256]{1,0:T(8,128)(2,1)} fusion(bf16[512,256]{1,0:T(8,128)(2,1)S(1)} %copy-done.1, s32[4096]{0:T(1024)S(1)} %bitcast.46), kind=kOutput, calls=%fused_computation.11 | convolution fusion | flops 1076887552 | bytes 2375680 | tf_op jit(solution)/shard_map/dot_general | solution.py:18
  78.8 7.5 %all-to-all-start.1 = ((bf16[32,128,256]{2,1,0:T(8,128)(2,1)}), bf16[32,128,256]{2,1,0:T(8,128)(2,1)}, u32[]{:S(2)}, u32[]{:S(2)}) async-start(bf16[32,128,256]{2,1,0:T(8,128)(2,1)} %bitcast.42), calls=%async_computation.1 | async-start | bytes 4194304 | tf_op jit(solution)/shard_map/all_to_all | solution.py:69
  90.4 5.1 %collective-permute-start.11 = (bf16[512,256]{1,0:T(8,128)(2,1)S(1)}, bf16[512,256]{1,0:T(8,128)(2,1)}, u32[]{:S(2)}, u32[]{:S(2)}) collective-permute-start(bf16[512,256]{1,0:T(8,128)(2,1)S(1)} %get-tuple-element.12), channel_id=1, source_target_pairs={{0,15},{1,0},{2,1},{3,2},{4,3},{5,4},{6,5},{7,6},{8,7},{9,8},{10,9... | collective-permute-start | bytes 786440 | tf_op jit(solution)/shard_map/ppermute | solution.py:47
  95.5 10.5 %collective-permute-done.4 = bf16[512,256]{1,0:T(8,128)(2,1)} collective-permute-done((bf16[512,256]{1,0:T(8,128)(2,1)}, bf16[512,256]{1,0:T(8,128)(2,1)}, u32[]{:S(2)}, u32[]{:S(2)}) %collective-permute-start.4) | collective-permute-done | bytes 262176 | tf_op jit(solution)/shard_map/ppermute | solution.py:43
  110.0 3.9 %collective-permute-start.12 = (bf16[512,256]{1,0:T(8,128)(2,1)S(1)}, bf16[512,256]{1,0:T(8,128)(2,1)}, u32[]{:S(2)}, u32[]{:S(2)}) collective-permute-start(bf16[512,256]{1,0:T(8,128)(2,1)S(1)} %get-tuple-element.10), channel_id=1, source_target_pairs={{0,15},{1,0},{2,1},{3,2},{4,3},{5,4},{6,5},{7,6},{8,7},{9,8},{10,9... | collective-permute-start | bytes 786440 | tf_op jit(solution)/shard_map/ppermute | solution.py:47
  113.9 6.2 %collective-permute-done.5 = bf16[512,256]{1,0:T(8,128)(2,1)} collective-permute-done((bf16[512,256]{1,0:T(8,128)(2,1)}, bf16[512,256]{1,0:T(8,128)(2,1)}, u32[]{:S(2)}, u32[]{:S(2)}) %collective-permute-start.5) | collective-permute-done | bytes 262176 | tf_op jit(solution)/shard_map/ppermute | solution.py:43
  123.6 2.6 %collective-permute-start.6 = (bf16[512,256]{1,0:T(8,128)(2,1)}, bf16[512,256]{1,0:T(8,128)(2,1)}, u32[]{:S(2)}, u32[]{:S(2)}) collective-permute-start(bf16[512,256]{1,0:T(8,128)(2,1)} %get-tuple-element.7), channel_id=1, source_target_pairs={{0,1},{1,2},{2,3},{3,4},{4,5},{5,6},{6,7},{7,8},{8,9},{9,10},{10,1... | collective-permute-start | bytes 786440 | tf_op jit(solution)/shard_map/ppermute | solution.py:43
  126.2 3.2 %collective-permute-start.13 = (bf16[512,256]{1,0:T(8,128)(2,1)S(1)}, bf16[512,256]{1,0:T(8,128)(2,1)}, u32[]{:S(2)}, u32[]{:S(2)}) collective-permute-start(bf16[512,256]{1,0:T(8,128)(2,1)S(1)} %get-tuple-element.8), channel_id=1, source_target_pairs={{0,15},{1,0},{2,1},{3,2},{4,3},{5,4},{6,5},{7,6},{8,7},{9,8},{10,9... | collective-permute-start | bytes 786440 | tf_op jit(solution)/shard_map/ppermute | solution.py:47
  129.5 3.0 %collective-permute-done.6 = bf16[512,256]{1,0:T(8,128)(2,1)} collective-permute-done((bf16[512,256]{1,0:T(8,128)(2,1)}, bf16[512,256]{1,0:T(8,128)(2,1)}, u32[]{:S(2)}, u32[]{:S(2)}) %collective-permute-start.6) | collective-permute-done | bytes 262176 | tf_op jit(solution)/shard_map/ppermute | solution.py:43
  132.5 2.5 %collective-permute-done.13 = bf16[512,256]{1,0:T(8,128)(2,1)} collective-permute-done((bf16[512,256]{1,0:T(8,128)(2,1)S(1)}, bf16[512,256]{1,0:T(8,128)(2,1)}, u32[]{:S(2)}, u32[]{:S(2)}) %collective-permute-start.13) | collective-permute-done | bytes 262176 | tf_op jit(solution)/shard_map/ppermute | solution.py:47
  135.1 2.1 add_convert_fusion.6
  137.2 7.6 %collective-permute-start.7 = (bf16[512,256]{1,0:T(8,128)(2,1)}, bf16[512,256]{1,0:T(8,128)(2,1)S(1)}, u32[]{:S(2)}, u32[]{:S(2)}) collective-permute-start(bf16[512,256]{1,0:T(8,128)(2,1)} %get-tuple-element.5), channel_id=1, source_target_pairs={{0,1},{1,2},{2,3},{3,4},{4,5},{5,6},{6,7},{7,8},{8,9},{9,10},{10,1... | collective-permute-start | bytes 786440 | tf_op jit(solution)/shard_map/ppermute | solution.py:43
  144.8 2.1 collective-permute-start.14
  146.9 8.8 %fusion.11 = bf16[2048,256]{1,0:T(8,128)(2,1)} fusion(bf16[4096,256]{1,0:T(8,128)(2,1)} %bitcast.8, s32[2048]{0:T(1024)S(1)} %multiply_add_fusion), kind=kOutput, calls=%fused_computation.15 | convolution fusion | flops 4303880192 | bytes 3153920 | tf_op jit(solution)/shard_map/dot_general | solution.py:18
  155.7 2.2 reshape.272
  159.1 2.6 %fusion.21 = f32[512,1,4]{2,1,0:T(1,128)} fusion(bf16[512,4,256]{2,1,0:T(4,128)(2,1)} %reshape.272, bf16[512,256,1]{1,0,2:T(8,128)(2,1)S(1)} %fusion.23), kind=kOutput, calls=%fused_computation.44 | convolution fusion | flops 1048576 | bytes 1318912 | tf_op jit(solution)/shard_map/re,rke->rk/dot_general | solution.py:82
  163.4 8.7 %all-to-all-start.2 = ((f32[16,512,4]{1,2,0:T(4,128)}), f32[16,512,4]{1,2,0:T(4,128)S(1)}, u32[]{:S(2)}, u32[]{:S(2)}) async-start(f32[16,512,4]{1,2,0:T(4,128)} %broadcast_in_dim.2), calls=%async_computation.2 | async-start | bytes 262144 | tf_op jit(solution)/shard_map/all_to_all | solution.py:84
  172.2 7.3 %fusion.8 = bf16[4096,256]{1,0:T(8,128)(2,1)} fusion(s32[4096]{0:T(1024)S(1)} %bitcast.47, bf16[512,4096]{1,0:T(8,128)(2,1)} %all-gather.2.cloned.1.call-done, bf16[256,4096]{1,0:T(8,128)(2,1)} %param.9, bf16[32,8,32,128]{3,2,1,0:T(8,128)(2,1)S(1)} %bitcast.41), kind=kOutput, calls=%fused_computation.12 | convolution fusion | flops 2151809024 | bytes 10502144 | tf_op jit(solution)/shard_map/dot_general | solution.py:18
  179.5 5.4 %all-to-all-done.2 = f32[16,512,4]{1,2,0:T(4,128)S(1)} async-done(((f32[16,512,4]{1,2,0:T(4,128)}), f32[16,512,4]{1,2,0:T(4,128)S(1)}, u32[]{:S(2)}, u32[]{:S(2)}) %all-to-all-start.2) | async-done | bytes 131104 | tf_op jit(solution)/shard_map/all_to_all | solution.py:84
  184.9 8.2 %all-to-all-start.3 = ((bf16[32,128,256]{2,1,0:T(8,128)(2,1)}), bf16[32,128,256]{2,1,0:T(8,128)(2,1)S(1)}, u32[]{:S(2)}, u32[]{:S(2)}) async-start(bf16[32,128,256]{2,1,0:T(8,128)(2,1)} %bitcast.43), calls=%async_computation.3 | async-start | bytes 4194304 | tf_op jit(solution)/shard_map/all_to_all | solution.py:77
  195.8 27.0 %all-to-all-done.3 = bf16[32,128,256]{2,1,0:T(8,128)(2,1)S(1)} async-done(((bf16[32,128,256]{2,1,0:T(8,128)(2,1)}), bf16[32,128,256]{2,1,0:T(8,128)(2,1)S(1)}, u32[]{:S(2)}, u32[]{:S(2)}) %all-to-all-start.3) | async-done | bytes 2097184 | tf_op jit(solution)/shard_map/all_to_all | solution.py:77
  222.9 7.9 %fusion.12 = bf16[2048,256]{1,0:T(8,128)(2,1)} fusion(bf16[4096,256]{1,0:T(8,128)(2,1)S(1)} %bitcast.44, s32[2048]{0:T(1024)} %copy-done.4), kind=kOutput, calls=%fused_computation.16 | convolution fusion | flops 4303880192 | bytes 3153920 | tf_op jit(solution)/shard_map/dot_general | solution.py:18
  (60 shorter events, 35.2 us)
Async XLA Ops:
  7.2 1.8 copy-start
  7.2 165.0 %all-gather.2.cloned.1.call-start = ((), (), s32[]{:S(2)}) async-start(), calls=%async_computation.4 | async-start | bytes 4456448 | tf_op jit(solution)/shard_map/all_gather | solution.py:72
  9.0 17.1 %copy-start.3 = (s32[512,4]{0,1:T(4,128)S(1)}, s32[512,4]{0,1:T(4,128)}, u32[]{:S(2)}) copy-start(s32[512,4]{0,1:T(4,128)} %param.12) | copy-start | bytes 24580
  16.7 12.0 %collective-permute-start = (bf16[512,256]{1,0:T(8,128)(2,1)}, bf16[512,256]{1,0:T(8,128)(2,1)}, u32[]{:S(2)}, u32[]{:S(2)}) collective-permute-start(bf16[512,256]{1,0:T(8,128)(2,1)} %get-tuple-element.17), channel_id=1, source_target_pairs={{0,1},{1,2},{2,3},{3,4},{4,5},{5,6},{6,7},{7,8},{8,9},{9,10},{10,1... | collective-permute-start | bytes 786440 | tf_op jit(solution)/shard_map/ppermute | solution.py:43
  20.6 13.8 %collective-permute-start.8 = (bf16[512,256]{1,0:T(8,128)(2,1)}, bf16[512,256]{1,0:T(8,128)(2,1)}, u32[]{:S(2)}, u32[]{:S(2)}) collective-permute-start(bf16[512,256]{1,0:T(8,128)(2,1)} %get-tuple-element.18), channel_id=1, source_target_pairs={{0,15},{1,0},{2,1},{3,2},{4,3},{5,4},{6,5},{7,6},{8,7},{9,8},{10,9... | collective-permute-start | bytes 786440 | tf_op jit(solution)/shard_map/ppermute | solution.py:47
  30.6 45.0 %copy-start.1 = (bf16[512,256]{1,0:T(8,128)(2,1)S(1)}, bf16[512,256]{1,0:T(8,128)(2,1)}, u32[]{:S(2)}) copy-start(bf16[512,256]{1,0:T(8,128)(2,1)} %param.11) | copy-start | bytes 786436
  30.6 19.3 %collective-permute-start.1 = (bf16[512,256]{1,0:T(8,128)(2,1)}, bf16[512,256]{1,0:T(8,128)(2,1)}, u32[]{:S(2)}, u32[]{:S(2)}) collective-permute-start(bf16[512,256]{1,0:T(8,128)(2,1)} %add_convert_fusion.12), channel_id=1, source_target_pairs={{0,1},{1,2},{2,3},{3,4},{4,5},{5,6},{6,7},{7,8},{8,9},{9,10},{10,1... | collective-permute-start | bytes 786440 | tf_op jit(solution)/shard_map/ppermute | solution.py:43
  51.9 15.4 %collective-permute-start.2 = (bf16[512,256]{1,0:T(8,128)(2,1)}, bf16[512,256]{1,0:T(8,128)(2,1)}, u32[]{:S(2)}, u32[]{:S(2)}) collective-permute-start(bf16[512,256]{1,0:T(8,128)(2,1)} %get-tuple-element.15), channel_id=1, source_target_pairs={{0,1},{1,2},{2,3},{3,4},{4,5},{5,6},{6,7},{7,8},{8,9},{9,10},{10,1... | collective-permute-start | bytes 786440 | tf_op jit(solution)/shard_map/ppermute | solution.py:43
  53.9 13.5 %collective-permute-start.9 = (bf16[512,256]{1,0:T(8,128)(2,1)}, bf16[512,256]{1,0:T(8,128)(2,1)}, u32[]{:S(2)}, u32[]{:S(2)}) collective-permute-start(bf16[512,256]{1,0:T(8,128)(2,1)} %get-tuple-element.16), channel_id=1, source_target_pairs={{0,15},{1,0},{2,1},{3,2},{4,3},{5,4},{6,5},{7,6},{8,7},{9,8},{10,9... | collective-permute-start | bytes 786440 | tf_op jit(solution)/shard_map/ppermute | solution.py:47
  59.8 15.7 %all-to-all-start = ((s32[32,1,128]{2,1,0:T(1,128)}), s32[32,1,128]{2,1,0:T(1,128)S(1)}, u32[]{:S(2)}, u32[]{:S(2)}) async-start(s32[32,1,128]{2,1,0:T(1,128)} %bitcast.5), calls=%async_computation | async-start | bytes 32768 | tf_op jit(solution)/shard_map/all_to_all | solution.py:67
  69.5 16.9 %collective-permute-start.3 = (bf16[512,256]{1,0:T(8,128)(2,1)}, bf16[512,256]{1,0:T(8,128)(2,1)}, u32[]{:S(2)}, u32[]{:S(2)}) collective-permute-start(bf16[512,256]{1,0:T(8,128)(2,1)} %get-tuple-element.13), channel_id=1, source_target_pairs={{0,1},{1,2},{2,3},{3,4},{4,5},{5,6},{6,7},{7,8},{8,9},{9,10},{10,1... | collective-permute-start | bytes 786440 | tf_op jit(solution)/shard_map/ppermute | solution.py:43
  71.5 14.9 %collective-permute-start.10 = (bf16[512,256]{1,0:T(8,128)(2,1)}, bf16[512,256]{1,0:T(8,128)(2,1)}, u32[]{:S(2)}, u32[]{:S(2)}) collective-permute-start(bf16[512,256]{1,0:T(8,128)(2,1)} %get-tuple-element.14), channel_id=1, source_target_pairs={{0,15},{1,0},{2,1},{3,2},{4,3},{5,4},{6,5},{7,6},{8,7},{9,8},{10,9... | collective-permute-start | bytes 786440 | tf_op jit(solution)/shard_map/ppermute | solution.py:47
  78.8 68.1 %all-to-all-start.1 = ((bf16[32,128,256]{2,1,0:T(8,128)(2,1)}), bf16[32,128,256]{2,1,0:T(8,128)(2,1)}, u32[]{:S(2)}, u32[]{:S(2)}) async-start(bf16[32,128,256]{2,1,0:T(8,128)(2,1)} %bitcast.42), calls=%async_computation.1 | async-start | bytes 4194304 | tf_op jit(solution)/shard_map/all_to_all | solution.py:69
  88.4 17.6 %collective-permute-start.4 = (bf16[512,256]{1,0:T(8,128)(2,1)}, bf16[512,256]{1,0:T(8,128)(2,1)}, u32[]{:S(2)}, u32[]{:S(2)}) collective-permute-start(bf16[512,256]{1,0:T(8,128)(2,1)} %get-tuple-element.11), channel_id=1, source_target_pairs={{0,1},{1,2},{2,3},{3,4},{4,5},{5,6},{6,7},{7,8},{8,9},{9,10},{10,1... | collective-permute-start | bytes 786440 | tf_op jit(solution)/shard_map/ppermute | solution.py:43
  90.4 15.7 %collective-permute-start.11 = (bf16[512,256]{1,0:T(8,128)(2,1)S(1)}, bf16[512,256]{1,0:T(8,128)(2,1)}, u32[]{:S(2)}, u32[]{:S(2)}) collective-permute-start(bf16[512,256]{1,0:T(8,128)(2,1)S(1)} %get-tuple-element.12), channel_id=1, source_target_pairs={{0,15},{1,0},{2,1},{3,2},{4,3},{5,4},{6,5},{7,6},{8,7},{9,8},{10,9... | collective-permute-start | bytes 786440 | tf_op jit(solution)/shard_map/ppermute | solution.py:47
  108.1 12.1 %collective-permute-start.5 = (bf16[512,256]{1,0:T(8,128)(2,1)}, bf16[512,256]{1,0:T(8,128)(2,1)}, u32[]{:S(2)}, u32[]{:S(2)}) collective-permute-start(bf16[512,256]{1,0:T(8,128)(2,1)} %get-tuple-element.9), channel_id=1, source_target_pairs={{0,1},{1,2},{2,3},{3,4},{4,5},{5,6},{6,7},{7,8},{8,9},{9,10},{10,1... | collective-permute-start | bytes 786440 | tf_op jit(solution)/shard_map/ppermute | solution.py:43
  110.0 11.6 %collective-permute-start.12 = (bf16[512,256]{1,0:T(8,128)(2,1)S(1)}, bf16[512,256]{1,0:T(8,128)(2,1)}, u32[]{:S(2)}, u32[]{:S(2)}) collective-permute-start(bf16[512,256]{1,0:T(8,128)(2,1)S(1)} %get-tuple-element.10), channel_id=1, source_target_pairs={{0,15},{1,0},{2,1},{3,2},{4,3},{5,4},{6,5},{7,6},{8,7},{9,8},{10,9... | collective-permute-start | bytes 786440 | tf_op jit(solution)/shard_map/ppermute | solution.py:47
  123.6 9.0 %collective-permute-start.6 = (bf16[512,256]{1,0:T(8,128)(2,1)}, bf16[512,256]{1,0:T(8,128)(2,1)}, u32[]{:S(2)}, u32[]{:S(2)}) collective-permute-start(bf16[512,256]{1,0:T(8,128)(2,1)} %get-tuple-element.7), channel_id=1, source_target_pairs={{0,1},{1,2},{2,3},{3,4},{4,5},{5,6},{6,7},{7,8},{8,9},{9,10},{10,1... | collective-permute-start | bytes 786440 | tf_op jit(solution)/shard_map/ppermute | solution.py:43
  126.2 8.8 %collective-permute-start.13 = (bf16[512,256]{1,0:T(8,128)(2,1)S(1)}, bf16[512,256]{1,0:T(8,128)(2,1)}, u32[]{:S(2)}, u32[]{:S(2)}) collective-permute-start(bf16[512,256]{1,0:T(8,128)(2,1)S(1)} %get-tuple-element.8), channel_id=1, source_target_pairs={{0,15},{1,0},{2,1},{3,2},{4,3},{5,4},{6,5},{7,6},{8,7},{9,8},{10,9... | collective-permute-start | bytes 786440 | tf_op jit(solution)/shard_map/ppermute | solution.py:47
  129.5 26.2 %copy-start.4 = (s32[2048]{0:T(1024)}, s32[2048]{0:T(1024)S(1)}, u32[]{:S(2)}) copy-start(s32[2048]{0:T(1024)S(1)} %multiply_add_fusion) | copy-start | bytes 24580
  137.2 20.7 %collective-permute-start.7 = (bf16[512,256]{1,0:T(8,128)(2,1)}, bf16[512,256]{1,0:T(8,128)(2,1)S(1)}, u32[]{:S(2)}, u32[]{:S(2)}) collective-permute-start(bf16[512,256]{1,0:T(8,128)(2,1)} %get-tuple-element.5), channel_id=1, source_target_pairs={{0,1},{1,2},{2,3},{3,4},{4,5},{5,6},{6,7},{7,8},{8,9},{9,10},{10,1... | collective-permute-start | bytes 786440 | tf_op jit(solution)/shard_map/ppermute | solution.py:43
  144.8 13.1 %collective-permute-start.14 = (bf16[512,256]{1,0:T(8,128)(2,1)}, bf16[512,256]{1,0:T(8,128)(2,1)}, u32[]{:S(2)}, u32[]{:S(2)}) collective-permute-start(bf16[512,256]{1,0:T(8,128)(2,1)} %get-tuple-element.6), channel_id=1, source_target_pairs={{0,15},{1,0},{2,1},{3,2},{4,3},{5,4},{6,5},{7,6},{8,7},{9,8},{10,9... | collective-permute-start | bytes 786440 | tf_op jit(solution)/shard_map/ppermute | solution.py:47
  163.4 21.5 %all-to-all-start.2 = ((f32[16,512,4]{1,2,0:T(4,128)}), f32[16,512,4]{1,2,0:T(4,128)S(1)}, u32[]{:S(2)}, u32[]{:S(2)}) async-start(f32[16,512,4]{1,2,0:T(4,128)} %broadcast_in_dim.2), calls=%async_computation.2 | async-start | bytes 262144 | tf_op jit(solution)/shard_map/all_to_all | solution.py:84
  179.5 15.4 %copy-start.2 = (s32[512,4]{0,1:T(4,128)S(1)}, s32[512,4]{0,1:T(4,128)}, u32[]{:S(2)}) copy-start(s32[512,4]{0,1:T(4,128)} %param.13) | copy-start | bytes 24580
  184.9 37.9 %all-to-all-start.3 = ((bf16[32,128,256]{2,1,0:T(8,128)(2,1)}), bf16[32,128,256]{2,1,0:T(8,128)(2,1)S(1)}, u32[]{:S(2)}, u32[]{:S(2)}) async-start(bf16[32,128,256]{2,1,0:T(8,128)(2,1)} %bitcast.43), calls=%async_computation.3 | async-start | bytes 4194304 | tf_op jit(solution)/shard_map/all_to_all | solution.py:77
Sparse Core Ops, SparseCore 0:
  10.0 116.2 all-gather.1

commit v12 on v4

--- a/solution.py
+++ b/solution.py
@@ -73,14 +73,13 @@
     ).astype(jnp.bfloat16)
     served_g = pick_rows(asked, g_own).reshape(n_dp, CAP, e_local)
     back_g = lax.all_to_all(served_g, "dp", 0, 0, tiled=True).reshape(n_dp * CAP, e_local)
-    g_vec = pick_rows(slot, back_g).reshape(rows, K, e_local).astype(jnp.float32)
 
     old_wide = old_vec.astype(jnp.float32)
     scale = 1.0 / math.sqrt(E)
     partial_scores = jnp.einsum("re,rke->rk", new, old_wide)
-    spread = jnp.broadcast_to(partial_scores[None], (n_wide,) + partial_scores.shape)
-    gathered = lax.all_to_all(spread, "wide", 0, 0, tiled=True)
-    score = jnp.sum(gathered, axis=0) * scale
+    score = lax.psum(partial_scores, "wide") * scale
+    back_g, score = lax.optimization_barrier((back_g, score))
+    g_vec = pick_rows(slot, back_g).reshape(rows, K, e_local).astype(jnp.float32)
     sign = 2.0 * labels.astype(jnp.float32) - 1.0
     pair_loss = jax.nn.softplus(-sign * score)
     dscore = -sign * jax.nn.sigmoid(-sign * score)

time: 216 us -> 215 us (level)
  the two profiles are of different devices: /device:TPU:32 before, /device:TPU:6 now
where the time goes in v12:
time: 215 us; the launch traced here: 214 us
  starting transfers between devices  80.6 us (37%)
  matrix products  39.4 us (18%)
  blocking collectives  27.7 us (13%)
  local copies, waits for them, and re-layouts  26 us (12%)
  waiting for transfers between devices  22.7 us (11%)
  between operations  14.4 us (7%)
  other arithmetic  2.95 us (1%)
    ppermute x7, starting transfers between devices, local(): to_left = lax.ppermute(to_left, 'wide', left)  41 us
    dot_general x4, matrix products, pick_rows(): jnp.dot(one_hot(index, table.shape[0]), table, preferred_element_type=jnp...  28.9 us
    psum x1, blocking collectives, local(): score = lax.psum(partial_scores, 'wide') * scale  27.7 us
    dynamic_update_slice x16, local copies, waits for them, and re-layouts, place(): return lax.dynamic_update_slice_in_dim(full, block, source * e_local, 1)  18.7 us
    ppermute x8, starting transfers between devices, local(): to_right = lax.ppermute(to_right, 'wide', right)  17.4 us
    ppermute x8, waiting for transfers between devices, local(): to_right = lax.ppermute(to_right, 'wide', right)  16.1 us
    all_to_all x1, starting transfers between devices, local(): asked = lax.all_to_all(req, 'dp', 0, 0, tiled=True).reshape(-1)  7.72 us
    all_to_all x1, starting transfers between devices, local(): lax.all_to_all(served, 'dp', 0, 0, tiled=True).reshape(n_dp * CAP, e_local)  7.44 us
  transfers between devices with their start and end apart: 19, of which 5 were waited for; matrix products, arithmetic and copies ran while one was open for 24% of the time, Pallas kernels for 0%

profile of v12, /device:TPU:6, one launch (start us, length us, event | category | flops | bytes accessed | tf_op | source)
XLA Modules:
  0.0 213.7 jit_solution(18151226881177656934)
XLA Ops:
  8.4 5.8 %convolution_convert_fusion = bf16[512,4096]{1,0:T(8,128)(2,1)} fusion(bf16[512,1024]{1,0:T(8,128)(2,1)S(1)} %copy-done, bf16[1024,256]{1,0:T(8,128)(2,1)} %param.8, bf16[256,4096]{1,0:T(8,128)(2,1)} %param.9, bf16[32,8,32,128]{3,2,1,0:T(8,128)(2,1)S(1)} %bitcast.39), kind=kOutput, calls=%fused_computation.10 | convolution fusion | flops 1345454080 | bytes 9961472 | tf_op jit(solution)/shard_map/dot_general | solution.py:31
  14.2 3.8 %collective-permute-start = (bf16[512,256]{1,0:T(8,128)(2,1)}, bf16[512,256]{1,0:T(8,128)(2,1)}, u32[]{:S(2)}, u32[]{:S(2)}) collective-permute-start(bf16[512,256]{1,0:T(8,128)(2,1)} %param.11), channel_id=1, source_target_pairs={{0,1},{1,2},{2,3},{3,4},{4,5},{5,6},{6,7},{7,8},{8,9},{9,10},{10,1... | collective-permute-start | bytes 786440 | tf_op jit(solution)/shard_map/ppermute | solution.py:66
  18.1 9.5 %collective-permute-start.1 = (bf16[512,256]{1,0:T(8,128)(2,1)}, bf16[512,256]{1,0:T(8,128)(2,1)}, u32[]{:S(2)}, u32[]{:S(2)}) collective-permute-start(bf16[512,256]{1,0:T(8,128)(2,1)} %param.11), channel_id=1, source_target_pairs={{0,15},{1,0},{2,1},{3,2},{4,3},{5,4},{6,5},{7,6},{8,7},{9,8},{10,9... | collective-permute-start | bytes 786440 | tf_op jit(solution)/shard_map/ppermute | solution.py:69
  29.8 2.5 %collective-permute-done = bf16[512,256]{1,0:T(8,128)(2,1)} collective-permute-done((bf16[512,256]{1,0:T(8,128)(2,1)}, bf16[512,256]{1,0:T(8,128)(2,1)}, u32[]{:S(2)}, u32[]{:S(2)}) %collective-permute-start) | collective-permute-done | bytes 262176 | tf_op jit(solution)/shard_map/ppermute | solution.py:66
  32.3 1.9 collective-permute-start.2
  34.7 5.1 %collective-permute-start.3 = (bf16[512,256]{1,0:T(8,128)(2,1)}, bf16[512,256]{1,0:T(8,128)(2,1)}, u32[]{:S(2)}, u32[]{:S(2)}) collective-permute-start(bf16[512,256]{1,0:T(8,128)(2,1)} %collective-permute-done.1), channel_id=1, source_target_pairs={{0,15},{1,0},{2,1},{3,2},{4,3},{5,4},{6,5},{7,6},{8,7},{9,8},{10,9... | collective-permute-start | bytes 786440 | tf_op jit(solution)/shard_map/ppermute | solution.py:69
  39.9 8.5 %collective-permute-done.2 = bf16[512,256]{1,0:T(8,128)(2,1)S(1)} collective-permute-done((bf16[512,256]{1,0:T(8,128)(2,1)}, bf16[512,256]{1,0:T(8,128)(2,1)S(1)}, u32[]{:S(2)}, u32[]{:S(2)}) %collective-permute-start.2) | collective-permute-done | bytes 262176 | tf_op jit(solution)/shard_map/ppermute | solution.py:66
  48.3 1.9 collective-permute-start.4
  50.9 7.7 %all-to-all-start = ((s32[32,1,128]{2,1,0:T(1,128)}), s32[32,1,128]{2,1,0:T(1,128)S(1)}, u32[]{:S(2)}, u32[]{:S(2)}) async-start(s32[32,1,128]{2,1,0:T(1,128)} %bitcast.4), calls=%async_computation.1 | async-start | bytes 32768 | tf_op jit(solution)/shard_map/all_to_all | solution.py:51
  58.6 2.5 %broadcast_in_dim.2 = bf16[512,4096]{1,0:T(8,128)(2,1)} broadcast(bf16[]{:T(256)} %constant.143.clone.1), dimensions={} | broadcast | bytes 4194306 | tf_op jit(solution)/shard_map/broadcast_in_dim | solution.py:63
  62.8 5.1 %collective-permute-start.5 = (bf16[512,256]{1,0:T(8,128)(2,1)}, bf16[512,256]{1,0:T(8,128)(2,1)}, u32[]{:S(2)}, u32[]{:S(2)}) collective-permute-start(bf16[512,256]{1,0:T(8,128)(2,1)} %collective-permute-done.3), channel_id=1, source_target_pairs={{0,15},{1,0},{2,1},{3,2},{4,3},{5,4},{6,5},{7,6},{8,7},{9,8},{10,9... | collective-permute-start | bytes 786440 | tf_op jit(solution)/shard_map/ppermute | solution.py:69
  68.0 1.9 collective-permute-start.6
  69.9 4.2 %fusion.8 = bf16[4096,256]{1,0:T(8,128)(2,1)} fusion(bf16[512,256]{1,0:T(8,128)(2,1)} %param.11, s32[4096]{0:T(1024)S(1)} %bitcast.45), kind=kOutput, calls=%fused_computation.12 | convolution fusion | flops 1076887552 | bytes 2375680 | tf_op jit(solution)/shard_map/dot_general | solution.py:18
  74.1 7.4 %all-to-all-start.2 = ((bf16[32,128,256]{2,1,0:T(8,128)(2,1)}), bf16[32,128,256]{2,1,0:T(8,128)(2,1)}, u32[]{:S(2)}, u32[]{:S(2)}) async-start(bf16[32,128,256]{2,1,0:T(8,128)(2,1)} %bitcast.41), calls=%async_computation.3 | async-start | bytes 4194304 | tf_op jit(solution)/shard_map/all_to_all | solution.py:53
  83.3 5.1 %collective-permute-start.7 = (bf16[512,256]{1,0:T(8,128)(2,1)}, bf16[512,256]{1,0:T(8,128)(2,1)S(1)}, u32[]{:S(2)}, u32[]{:S(2)}) collective-permute-start(bf16[512,256]{1,0:T(8,128)(2,1)} %collective-permute-done.5), channel_id=1, source_target_pairs={{0,15},{1,0},{2,1},{3,2},{4,3},{5,4},{6,5},{7,6},{8,7},{9,8},{10,9... | collective-permute-start | bytes 786440 | tf_op jit(solution)/shard_map/ppermute | solution.py:69
  90.1 1.9 collective-permute-start.8
  94.5 6.1 %collective-permute-done.7 = bf16[512,256]{1,0:T(8,128)(2,1)S(1)} collective-permute-done((bf16[512,256]{1,0:T(8,128)(2,1)}, bf16[512,256]{1,0:T(8,128)(2,1)S(1)}, u32[]{:S(2)}, u32[]{:S(2)}) %collective-permute-start.7) | collective-permute-done | bytes 262176 | tf_op jit(solution)/shard_map/ppermute | solution.py:69
  100.6 5.5 %collective-permute-start.9 = (bf16[512,256]{1,0:T(8,128)(2,1)S(1)}, bf16[512,256]{1,0:T(8,128)(2,1)S(1)}, u32[]{:S(2)}, u32[]{:S(2)}) collective-permute-start(bf16[512,256]{1,0:T(8,128)(2,1)S(1)} %collective-permute-done.7), channel_id=1, source_target_pairs={{0,15},{1,0},{2,1},{3,2},{4,3},{5,4},{6,5},{7,6},{8,7},{9,8},{10,9... | collective-permute-start | bytes 786440 | tf_op jit(solution)/shard_map/ppermute | solution.py:69
  106.0 1.7 constant_dynamic-update-slice_fusion.10
  107.8 1.9 collective-permute-start.10
  113.1 5.1 %collective-permute-start.11 = (bf16[512,256]{1,0:T(8,128)(2,1)S(1)}, bf16[512,256]{1,0:T(8,128)(2,1)S(1)}, u32[]{:S(2)}, u32[]{:S(2)}) collective-permute-start(bf16[512,256]{1,0:T(8,128)(2,1)S(1)} %collective-permute-done.9), channel_id=1, source_target_pairs={{0,15},{1,0},{2,1},{3,2},{4,3},{5,4},{6,5},{7,6},{8,7},{9,8},{10,9... | collective-permute-start | bytes 786440 | tf_op jit(solution)/shard_map/ppermute | solution.py:69
  119.0 1.9 collective-permute-start.12
  122.9 5.6 %collective-permute-start.13 = (bf16[512,256]{1,0:T(8,128)(2,1)S(1)}, bf16[512,256]{1,0:T(8,128)(2,1)S(1)}, u32[]{:S(2)}, u32[]{:S(2)}) collective-permute-start(bf16[512,256]{1,0:T(8,128)(2,1)S(1)} %collective-permute-done.11), channel_id=1, source_target_pairs={{0,15},{1,0},{2,1},{3,2},{4,3},{5,4},{6,5},{7,6},{8,7},{9,8},{10,9... | collective-permute-start | bytes 786440 | tf_op jit(solution)/shard_map/ppermute | solution.py:69
  129.2 2.1 collective-permute-start.14
  133.5 5.1 %collective-permute-done.14 = bf16[512,256]{1,0:T(8,128)(2,1)S(1)} collective-permute-done((bf16[512,256]{1,0:T(8,128)(2,1)S(1)}, bf16[512,256]{1,0:T(8,128)(2,1)S(1)}, u32[]{:S(2)}, u32[]{:S(2)}) %collective-permute-start.14) | collective-permute-done | bytes 262176 | tf_op jit(solution)/shard_map/ppermute | solution.py:66
  139.4 8.8 %fusion.7 = bf16[4096,256]{1,0:T(8,128)(2,1)} fusion(s32[4096]{0:T(1024)S(1)} %bitcast.46, bf16[512,4096]{1,0:T(8,128)(2,1)} %constant_dynamic-update-slice_fusion, bf16[256,4096]{1,0:T(8,128)(2,1)} %param.9, bf16[32,8,32,128]{3,2,1,0:T(8,128)(2,1)S(1)} %bitcast.40), kind=kOutput, calls=%fused_computation.11 | convolution fusion | flops 2151809024 | bytes 10502144 | tf_op jit(solution)/shard_map/dot_general | solution.py:18
  148.2 7.0 %all-to-all-start.1 = ((bf16[32,128,256]{2,1,0:T(8,128)(2,1)}), bf16[32,128,256]{2,1,0:T(8,128)(2,1)S(1)}, u32[]{:S(2)}, u32[]{:S(2)}) async-start(bf16[32,128,256]{2,1,0:T(8,128)(2,1)} %bitcast.42), calls=%async_computation.2 | async-start | bytes 4194304 | tf_op jit(solution)/shard_map/all_to_all | solution.py:75
  155.2 8.8 %fusion.11 = bf16[2048,256]{1,0:T(8,128)(2,1)} fusion(bf16[4096,256]{1,0:T(8,128)(2,1)} %bitcast.10, s32[2048]{0:T(1024)S(1)} %multiply_add_fusion), kind=kOutput, calls=%fused_computation.15 | convolution fusion | flops 4303880192 | bytes 3153920 | tf_op jit(solution)/shard_map/dot_general | solution.py:18
  164.0 2.2 %reshape.273 = bf16[512,4,256]{2,1,0:T(4,128)(2,1)} reshape(bf16[2048,256]{1,0:T(8,128)(2,1)} %fusion.11) | data formatting | bytes 2097152 | tf_op jit(solution)/shard_map/reshape | solution.py:54
  166.2 2.0 fusion.21
  168.3 27.7 %psum.7 = f32[512,4]{0,1:T(4,128)S(1)} all-reduce(f32[512,4]{0,1:T(4,128)S(1)} %bitcast.44), channel_id=1, replica_groups=mesh['dp'=32,'wide'=16] {'wide'}, use_global_device_ids=true, to_apply=%region_2.3 | all-reduce | flops 2048 | bytes 16384 | tf_op jit(solution)/shard_map/psum | solution.py:80
  196.7 7.2 %fusion.12 = bf16[2048,256]{1,0:T(8,128)(2,1)} fusion(bf16[4096,256]{1,0:T(8,128)(2,1)S(1)} %bitcast.43, s32[2048]{0:T(1024)S(1)} %multiply_add_fusion), kind=kOutput, calls=%fused_computation.16 | convolution fusion | flops 4303880192 | bytes 3153920 | tf_op jit(solution)/shard_map/dot_general | solution.py:18
  (61 shorter events, 25.7 us)
Async XLA Ops:
  7.2 1.2 copy-start
  7.2 159.0 %reduce-scatter.2.cloned.1.call-start = ((), (), s32[]{:S(2)}) async-start(), calls=%async_computation.4 | async-start | bytes 4456448 | tf_op jit(solution)/shard_map/reduce_scatter | solution.py:32
  14.2 13.4 %copy-start.2 = (s32[512,4]{0,1:T(4,128)S(1)}, s32[512,4]{0,1:T(4,128)}, u32[]{:S(2)}) copy-start(s32[512,4]{0,1:T(4,128)} %param.12) | copy-start | bytes 24580
  14.2 18.0 %collective-permute-start = (bf16[512,256]{1,0:T(8,128)(2,1)}, bf16[512,256]{1,0:T(8,128)(2,1)}, u32[]{:S(2)}, u32[]{:S(2)}) collective-permute-start(bf16[512,256]{1,0:T(8,128)(2,1)} %param.11), channel_id=1, source_target_pairs={{0,1},{1,2},{2,3},{3,4},{4,5},{5,6},{6,7},{7,8},{8,9},{9,10},{10,1... | collective-permute-start | bytes 786440 | tf_op jit(solution)/shard_map/ppermute | solution.py:66
  18.1 16.6 %collective-permute-start.1 = (bf16[512,256]{1,0:T(8,128)(2,1)}, bf16[512,256]{1,0:T(8,128)(2,1)}, u32[]{:S(2)}, u32[]{:S(2)}) collective-permute-start(bf16[512,256]{1,0:T(8,128)(2,1)} %param.11), channel_id=1, source_target_pairs={{0,15},{1,0},{2,1},{3,2},{4,3},{5,4},{6,5},{7,6},{8,7},{9,8},{10,9... | collective-permute-start | bytes 786440 | tf_op jit(solution)/shard_map/ppermute | solution.py:69
  32.3 16.1 %collective-permute-start.2 = (bf16[512,256]{1,0:T(8,128)(2,1)}, bf16[512,256]{1,0:T(8,128)(2,1)S(1)}, u32[]{:S(2)}, u32[]{:S(2)}) collective-permute-start(bf16[512,256]{1,0:T(8,128)(2,1)} %collective-permute-done), channel_id=1, source_target_pairs={{0,1},{1,2},{2,3},{3,4},{4,5},{5,6},{6,7},{7,8},{8,9},{9,10},{10,1... | collective-permute-start | bytes 786440 | tf_op jit(solution)/shard_map/ppermute | solution.py:66
  34.7 28.1 %collective-permute-start.3 = (bf16[512,256]{1,0:T(8,128)(2,1)}, bf16[512,256]{1,0:T(8,128)(2,1)}, u32[]{:S(2)}, u32[]{:S(2)}) collective-permute-start(bf16[512,256]{1,0:T(8,128)(2,1)} %collective-permute-done.1), channel_id=1, source_target_pairs={{0,15},{1,0},{2,1},{3,2},{4,3},{5,4},{6,5},{7,6},{8,7},{9,8},{10,9... | collective-permute-start | bytes 786440 | tf_op jit(solution)/shard_map/ppermute | solution.py:69
  48.3 19.6 %collective-permute-start.4 = (bf16[512,256]{1,0:T(8,128)(2,1)S(1)}, bf16[512,256]{1,0:T(8,128)(2,1)}, u32[]{:S(2)}, u32[]{:S(2)}) collective-permute-start(bf16[512,256]{1,0:T(8,128)(2,1)S(1)} %collective-permute-done.2), channel_id=1, source_target_pairs={{0,1},{1,2},{2,3},{3,4},{4,5},{5,6},{6,7},{7,8},{8,9},{9,10},{10,1... | collective-permute-start | bytes 786440 | tf_op jit(solution)/shard_map/ppermute | solution.py:66
  50.9 19.0 %all-to-all-start = ((s32[32,1,128]{2,1,0:T(1,128)}), s32[32,1,128]{2,1,0:T(1,128)S(1)}, u32[]{:S(2)}, u32[]{:S(2)}) async-start(s32[32,1,128]{2,1,0:T(1,128)} %bitcast.4), calls=%async_computation.1 | async-start | bytes 32768 | tf_op jit(solution)/shard_map/all_to_all | solution.py:51
  62.8 20.5 %collective-permute-start.5 = (bf16[512,256]{1,0:T(8,128)(2,1)}, bf16[512,256]{1,0:T(8,128)(2,1)}, u32[]{:S(2)}, u32[]{:S(2)}) collective-permute-start(bf16[512,256]{1,0:T(8,128)(2,1)} %collective-permute-done.3), channel_id=1, source_target_pairs={{0,15},{1,0},{2,1},{3,2},{4,3},{5,4},{6,5},{7,6},{8,7},{9,8},{10,9... | collective-permute-start | bytes 786440 | tf_op jit(solution)/shard_map/ppermute | solution.py:69
  68.0 22.1 %collective-permute-start.6 = (bf16[512,256]{1,0:T(8,128)(2,1)}, bf16[512,256]{1,0:T(8,128)(2,1)}, u32[]{:S(2)}, u32[]{:S(2)}) collective-permute-start(bf16[512,256]{1,0:T(8,128)(2,1)} %collective-permute-done.4), channel_id=1, source_target_pairs={{0,1},{1,2},{2,3},{3,4},{4,5},{5,6},{6,7},{7,8},{8,9},{9,10},{10,1... | collective-permute-start | bytes 786440 | tf_op jit(solution)/shard_map/ppermute | solution.py:66
  74.1 74.1 %all-to-all-start.2 = ((bf16[32,128,256]{2,1,0:T(8,128)(2,1)}), bf16[32,128,256]{2,1,0:T(8,128)(2,1)}, u32[]{:S(2)}, u32[]{:S(2)}) async-start(bf16[32,128,256]{2,1,0:T(8,128)(2,1)} %bitcast.41), calls=%async_computation.3 | async-start | bytes 4194304 | tf_op jit(solution)/shard_map/all_to_all | solution.py:53
  83.3 17.3 %collective-permute-start.7 = (bf16[512,256]{1,0:T(8,128)(2,1)}, bf16[512,256]{1,0:T(8,128)(2,1)S(1)}, u32[]{:S(2)}, u32[]{:S(2)}) collective-permute-start(bf16[512,256]{1,0:T(8,128)(2,1)} %collective-permute-done.5), channel_id=1, source_target_pairs={{0,15},{1,0},{2,1},{3,2},{4,3},{5,4},{6,5},{7,6},{8,7},{9,8},{10,9... | collective-permute-start | bytes 786440 | tf_op jit(solution)/shard_map/ppermute | solution.py:69
  90.1 17.7 %collective-permute-start.8 = (bf16[512,256]{1,0:T(8,128)(2,1)}, bf16[512,256]{1,0:T(8,128)(2,1)S(1)}, u32[]{:S(2)}, u32[]{:S(2)}) collective-permute-start(bf16[512,256]{1,0:T(8,128)(2,1)} %collective-permute-done.6), channel_id=1, source_target_pairs={{0,1},{1,2},{2,3},{3,4},{4,5},{5,6},{6,7},{7,8},{8,9},{9,10},{10,1... | collective-permute-start | bytes 786440 | tf_op jit(solution)/shard_map/ppermute | solution.py:66
  100.6 12.6 %collective-permute-start.9 = (bf16[512,256]{1,0:T(8,128)(2,1)S(1)}, bf16[512,256]{1,0:T(8,128)(2,1)S(1)}, u32[]{:S(2)}, u32[]{:S(2)}) collective-permute-start(bf16[512,256]{1,0:T(8,128)(2,1)S(1)} %collective-permute-done.7), channel_id=1, source_target_pairs={{0,15},{1,0},{2,1},{3,2},{4,3},{5,4},{6,5},{7,6},{8,7},{9,8},{10,9... | collective-permute-start | bytes 786440 | tf_op jit(solution)/shard_map/ppermute | solution.py:69
  107.8 11.2 %collective-permute-start.10 = (bf16[512,256]{1,0:T(8,128)(2,1)S(1)}, bf16[512,256]{1,0:T(8,128)(2,1)S(1)}, u32[]{:S(2)}, u32[]{:S(2)}) collective-permute-start(bf16[512,256]{1,0:T(8,128)(2,1)S(1)} %collective-permute-done.8), channel_id=1, source_target_pairs={{0,1},{1,2},{2,3},{3,4},{4,5},{5,6},{6,7},{7,8},{8,9},{9,10},{10,1... | collective-permute-start | bytes 786440 | tf_op jit(solution)/shard_map/ppermute | solution.py:66
  113.1 9.7 %collective-permute-start.11 = (bf16[512,256]{1,0:T(8,128)(2,1)S(1)}, bf16[512,256]{1,0:T(8,128)(2,1)S(1)}, u32[]{:S(2)}, u32[]{:S(2)}) collective-permute-start(bf16[512,256]{1,0:T(8,128)(2,1)S(1)} %collective-permute-done.9), channel_id=1, source_target_pairs={{0,15},{1,0},{2,1},{3,2},{4,3},{5,4},{6,5},{7,6},{8,7},{9,8},{10,9... | collective-permute-start | bytes 786440 | tf_op jit(solution)/shard_map/ppermute | solution.py:69
  119.0 10.2 %collective-permute-start.12 = (bf16[512,256]{1,0:T(8,128)(2,1)S(1)}, bf16[512,256]{1,0:T(8,128)(2,1)S(1)}, u32[]{:S(2)}, u32[]{:S(2)}) collective-permute-start(bf16[512,256]{1,0:T(8,128)(2,1)S(1)} %collective-permute-done.10), channel_id=1, source_target_pairs={{0,1},{1,2},{2,3},{3,4},{4,5},{5,6},{6,7},{7,8},{8,9},{9,10},{10,1... | collective-permute-start | bytes 786440 | tf_op jit(solution)/shard_map/ppermute | solution.py:66
  122.9 9.9 %collective-permute-start.13 = (bf16[512,256]{1,0:T(8,128)(2,1)S(1)}, bf16[512,256]{1,0:T(8,128)(2,1)S(1)}, u32[]{:S(2)}, u32[]{:S(2)}) collective-permute-start(bf16[512,256]{1,0:T(8,128)(2,1)S(1)} %collective-permute-done.11), channel_id=1, source_target_pairs={{0,15},{1,0},{2,1},{3,2},{4,3},{5,4},{6,5},{7,6},{8,7},{9,8},{10,9... | collective-permute-start | bytes 786440 | tf_op jit(solution)/shard_map/ppermute | solution.py:69
  129.2 9.5 %collective-permute-start.14 = (bf16[512,256]{1,0:T(8,128)(2,1)S(1)}, bf16[512,256]{1,0:T(8,128)(2,1)S(1)}, u32[]{:S(2)}, u32[]{:S(2)}) collective-permute-start(bf16[512,256]{1,0:T(8,128)(2,1)S(1)} %collective-permute-done.12), channel_id=1, source_target_pairs={{0,1},{1,2},{2,3},{3,4},{4,5},{5,6},{6,7},{7,8},{8,9},{9,10},{10,1... | collective-permute-start | bytes 786440 | tf_op jit(solution)/shard_map/ppermute | solution.py:66
  148.2 47.8 %all-to-all-start.1 = ((bf16[32,128,256]{2,1,0:T(8,128)(2,1)}), bf16[32,128,256]{2,1,0:T(8,128)(2,1)S(1)}, u32[]{:S(2)}, u32[]{:S(2)}) async-start(bf16[32,128,256]{2,1,0:T(8,128)(2,1)} %bitcast.42), calls=%async_computation.2 | async-start | bytes 4194304 | tf_op jit(solution)/shard_map/all_to_all | solution.py:75
  164.0 32.1 %copy-start.1 = (s32[512,4]{0,1:T(4,128)S(1)}, s32[512,4]{0,1:T(4,128)}, u32[]{:S(2)}) copy-start(s32[512,4]{0,1:T(4,128)} %param.13) | copy-start | bytes 24580
Sparse Core Ops, SparseCore 0:
  14.4 94.7 reduce-scatter.1

commit v13 on v12

--- a/solution.py
+++ b/solution.py
@@ -51,7 +51,8 @@
     asked = lax.all_to_all(req, "dp", 0, 0, tiled=True).reshape(-1)
     served = pick_rows(asked, old_index).reshape(n_dp, CAP, e_local)
     back = lax.all_to_all(served, "dp", 0, 0, tiled=True).reshape(n_dp * CAP, e_local)
-    old_vec = pick_rows(slot, back).reshape(rows, K, e_local)
+    by_k = slot.reshape(rows, K).T.reshape(-1)
+    old_vec = pick_rows(by_k, back).reshape(K, rows, e_local)
 
     me_w = lax.axis_index("wide")
     right = [(i, (i + 1) % n_wide) for i in range(n_wide)]
@@ -76,14 +77,14 @@
 
     old_wide = old_vec.astype(jnp.float32)
     scale = 1.0 / math.sqrt(E)
-    partial_scores = jnp.einsum("re,rke->rk", new, old_wide)
+    partial_scores = jnp.einsum("re,kre->rk", new, old_wide)
     score = lax.psum(partial_scores, "wide") * scale
     back_g, score = lax.optimization_barrier((back_g, score))
-    g_vec = pick_rows(slot, back_g).reshape(rows, K, e_local).astype(jnp.float32)
+    g_vec = pick_rows(by_k, back_g).reshape(K, rows, e_local).astype(jnp.float32)
     sign = 2.0 * labels.astype(jnp.float32) - 1.0
     pair_loss = jax.nn.softplus(-sign * score)
     dscore = -sign * jax.nn.sigmoid(-sign * score)
-    trunk_grad = jnp.einsum("rk,rke->re", dscore, g_vec) * scale
+    trunk_grad = jnp.einsum("rk,kre->re", dscore, g_vec) * scale
     return (new.astype(jnp.bfloat16), pair_loss, trunk_grad.astype(jnp.bfloat16))
 
 

time: 215 us -> 218 us (1.014)
    reshape x2 -> x0, local copies, waits for them, and re-layouts: 3.53 us -> none  [the longest x1 2.19 us: local(): old_vec = pick_rows(slot, back).reshape(rows, K, e_local)]
  transfers between devices with their start and end apart: 19 -> 19, of which waited for: 5 -> 5; matrix products, arithmetic and copies ran while one was open for 24% -> 25% of each run, Pallas kernels for 0% -> 0%
where the time goes in v13:
time: 218 us; the launch traced here: 216 us
  starting transfers between devices  81 us (37%)
  matrix products  41.2 us (19%)
  blocking collectives  27.7 us (13%)
  local copies, waits for them, and re-layouts  25.6 us (12%)
  waiting for transfers between devices  21.7 us (10%)
  between operations  14.4 us (7%)
  other arithmetic  4.78 us (2%)
    ppermute x7, starting transfers between devices, local(): to_left = lax.ppermute(to_left, 'wide', left)  41 us
    dot_general x4, matrix products, pick_rows(): jnp.dot(one_hot(index, table.shape[0]), table, preferred_element_type=jnp...  29 us
    psum x1, blocking collectives, local(): score = lax.psum(partial_scores, 'wide') * scale  27.7 us
    dynamic_update_slice x16, local copies, waits for them, and re-layouts, place(): return lax.dynamic_update_slice_in_dim(full, block, source * e_local, 1)  19.7 us
    ppermute x8, starting transfers between devices, local(): to_right = lax.ppermute(to_right, 'wide', right)  17.4 us
    ppermute x8, waiting for transfers between devices, local(): to_right = lax.ppermute(to_right, 'wide', right)  16.2 us
    all_to_all x1, starting transfers between devices, local(): asked = lax.all_to_all(req, 'dp', 0, 0, tiled=True).reshape(-1)  7.73 us
    all_to_all x1, starting transfers between devices, local(): lax.all_to_all(served, 'dp', 0, 0, tiled=True).reshape(n_dp * CAP, e_local)  7.44 us
  transfers between devices with their start and end apart: 19, of which 5 were waited for; matrix products, arithmetic and copies ran while one was open for 25% of the time, Pallas kernels for 0%

profile of v13, /device:TPU:6, one launch (start us, length us, event | category | flops | bytes accessed | tf_op | source)
XLA Modules:
  0.0 216.4 jit_solution(6990893485246043258)
XLA Ops:
  8.4 5.8 %convolution_convert_fusion = bf16[512,4096]{1,0:T(8,128)(2,1)} fusion(bf16[512,1024]{1,0:T(8,128)(2,1)S(1)} %copy-done, bf16[1024,256]{1,0:T(8,128)(2,1)} %param.8, bf16[256,4096]{1,0:T(8,128)(2,1)} %param.9, bf16[32,8,32,128]{3,2,1,0:T(8,128)(2,1)S(1)} %bitcast.43), kind=kOutput, calls=%fused_computation.10 | convolution fusion | flops 1345454080 | bytes 9961472 | tf_op jit(solution)/shard_map/dot_general | solution.py:31
  14.2 3.8 %collective-permute-start = (bf16[512,256]{1,0:T(8,128)(2,1)}, bf16[512,256]{1,0:T(8,128)(2,1)}, u32[]{:S(2)}, u32[]{:S(2)}) collective-permute-start(bf16[512,256]{1,0:T(8,128)(2,1)} %param.11), channel_id=1, source_target_pairs={{0,1},{1,2},{2,3},{3,4},{4,5},{5,6},{6,7},{7,8},{8,9},{9,10},{10,1... | collective-permute-start | bytes 786440 | tf_op jit(solution)/shard_map/ppermute | solution.py:67
  18.1 9.5 %collective-permute-start.1 = (bf16[512,256]{1,0:T(8,128)(2,1)}, bf16[512,256]{1,0:T(8,128)(2,1)}, u32[]{:S(2)}, u32[]{:S(2)}) collective-permute-start(bf16[512,256]{1,0:T(8,128)(2,1)} %param.11), channel_id=1, source_target_pairs={{0,15},{1,0},{2,1},{3,2},{4,3},{5,4},{6,5},{7,6},{8,7},{9,8},{10,9... | collective-permute-start | bytes 786440 | tf_op jit(solution)/shard_map/ppermute | solution.py:70
  29.8 2.5 %collective-permute-done = bf16[512,256]{1,0:T(8,128)(2,1)} collective-permute-done((bf16[512,256]{1,0:T(8,128)(2,1)}, bf16[512,256]{1,0:T(8,128)(2,1)}, u32[]{:S(2)}, u32[]{:S(2)}) %collective-permute-start) | collective-permute-done | bytes 262176 | tf_op jit(solution)/shard_map/ppermute | solution.py:67
  32.3 1.9 collective-permute-start.2
  34.7 5.1 %collective-permute-start.3 = (bf16[512,256]{1,0:T(8,128)(2,1)}, bf16[512,256]{1,0:T(8,128)(2,1)}, u32[]{:S(2)}, u32[]{:S(2)}) collective-permute-start(bf16[512,256]{1,0:T(8,128)(2,1)} %collective-permute-done.1), channel_id=1, source_target_pairs={{0,15},{1,0},{2,1},{3,2},{4,3},{5,4},{6,5},{7,6},{8,7},{9,8},{10,9... | collective-permute-start | bytes 786440 | tf_op jit(solution)/shard_map/ppermute | solution.py:70
  39.9 8.6 %collective-permute-done.2 = bf16[512,256]{1,0:T(8,128)(2,1)} collective-permute-done((bf16[512,256]{1,0:T(8,128)(2,1)}, bf16[512,256]{1,0:T(8,128)(2,1)}, u32[]{:S(2)}, u32[]{:S(2)}) %collective-permute-start.2) | collective-permute-done | bytes 262176 | tf_op jit(solution)/shard_map/ppermute | solution.py:67
  48.4 1.9 collective-permute-start.4
  51.0 7.7 %all-to-all-start = ((s32[32,1,128]{2,1,0:T(1,128)}), s32[32,1,128]{2,1,0:T(1,128)S(1)}, u32[]{:S(2)}, u32[]{:S(2)}) async-start(s32[32,1,128]{2,1,0:T(1,128)} %bitcast.4), calls=%async_computation.1 | async-start | bytes 32768 | tf_op jit(solution)/shard_map/all_to_all | solution.py:51
  58.7 2.5 %broadcast_in_dim.2 = bf16[512,4096]{1,0:T(8,128)(2,1)} broadcast(bf16[]{:T(256)} %constant.143.clone.1), dimensions={} | broadcast | bytes 4194306 | tf_op jit(solution)/shard_map/broadcast_in_dim | solution.py:64
  63.9 5.1 %collective-permute-start.5 = (bf16[512,256]{1,0:T(8,128)(2,1)}, bf16[512,256]{1,0:T(8,128)(2,1)}, u32[]{:S(2)}, u32[]{:S(2)}) collective-permute-start(bf16[512,256]{1,0:T(8,128)(2,1)} %collective-permute-done.3), channel_id=1, source_target_pairs={{0,15},{1,0},{2,1},{3,2},{4,3},{5,4},{6,5},{7,6},{8,7},{9,8},{10,9... | collective-permute-start | bytes 786440 | tf_op jit(solution)/shard_map/ppermute | solution.py:70
  69.0 1.9 collective-permute-start.6
  71.0 4.2 %fusion.8 = bf16[4096,256]{1,0:T(8,128)(2,1)} fusion(bf16[512,256]{1,0:T(8,128)(2,1)} %param.11, s32[4096]{0:T(1024)S(1)} %bitcast.50), kind=kOutput, calls=%fused_computation.12 | convolution fusion | flops 1076887552 | bytes 2375680 | tf_op jit(solution)/shard_map/dot_general | solution.py:18
  75.2 7.4 %all-to-all-start.2 = ((bf16[32,128,256]{2,1,0:T(8,128)(2,1)}), bf16[32,128,256]{2,1,0:T(8,128)(2,1)}, u32[]{:S(2)}, u32[]{:S(2)}) async-start(bf16[32,128,256]{2,1,0:T(8,128)(2,1)} %bitcast.45), calls=%async_computation.3 | async-start | bytes 4194304 | tf_op jit(solution)/shard_map/all_to_all | solution.py:53
  84.4 5.1 %collective-permute-start.7 = (bf16[512,256]{1,0:T(8,128)(2,1)}, bf16[512,256]{1,0:T(8,128)(2,1)S(1)}, u32[]{:S(2)}, u32[]{:S(2)}) collective-permute-start(bf16[512,256]{1,0:T(8,128)(2,1)} %collective-permute-done.5), channel_id=1, source_target_pairs={{0,15},{1,0},{2,1},{3,2},{4,3},{5,4},{6,5},{7,6},{8,7},{9,8},{10,9... | collective-permute-start | bytes 786440 | tf_op jit(solution)/shard_map/ppermute | solution.py:70
  91.2 1.9 collective-permute-start.8
  96.5 4.9 %collective-permute-done.7 = bf16[512,256]{1,0:T(8,128)(2,1)S(1)} collective-permute-done((bf16[512,256]{1,0:T(8,128)(2,1)}, bf16[512,256]{1,0:T(8,128)(2,1)S(1)}, u32[]{:S(2)}, u32[]{:S(2)}) %collective-permute-start.7) | collective-permute-done | bytes 262176 | tf_op jit(solution)/shard_map/ppermute | solution.py:70
  101.4 5.5 %collective-permute-start.9 = (bf16[512,256]{1,0:T(8,128)(2,1)S(1)}, bf16[512,256]{1,0:T(8,128)(2,1)S(1)}, u32[]{:S(2)}, u32[]{:S(2)}) collective-permute-start(bf16[512,256]{1,0:T(8,128)(2,1)S(1)} %collective-permute-done.7), channel_id=1, source_target_pairs={{0,15},{1,0},{2,1},{3,2},{4,3},{5,4},{6,5},{7,6},{8,7},{9,8},{10,9... | collective-permute-start | bytes 786440 | tf_op jit(solution)/shard_map/ppermute | solution.py:70
  108.6 1.9 collective-permute-start.10
  114.0 5.1 %collective-permute-start.11 = (bf16[512,256]{1,0:T(8,128)(2,1)S(1)}, bf16[512,256]{1,0:T(8,128)(2,1)S(1)}, u32[]{:S(2)}, u32[]{:S(2)}) collective-permute-start(bf16[512,256]{1,0:T(8,128)(2,1)S(1)} %collective-permute-done.9), channel_id=1, source_target_pairs={{0,15},{1,0},{2,1},{3,2},{4,3},{5,4},{6,5},{7,6},{8,7},{9,8},{10,9... | collective-permute-start | bytes 786440 | tf_op jit(solution)/shard_map/ppermute | solution.py:70
  119.8 1.9 collective-permute-start.12
  123.8 5.6 %collective-permute-start.13 = (bf16[512,256]{1,0:T(8,128)(2,1)S(1)}, bf16[512,256]{1,0:T(8,128)(2,1)S(1)}, u32[]{:S(2)}, u32[]{:S(2)}) collective-permute-start(bf16[512,256]{1,0:T(8,128)(2,1)S(1)} %collective-permute-done.11), channel_id=1, source_target_pairs={{0,15},{1,0},{2,1},{3,2},{4,3},{5,4},{6,5},{7,6},{8,7},{9,8},{10,9... | collective-permute-start | bytes 786440 | tf_op jit(solution)/shard_map/ppermute | solution.py:70
  130.2 2.1 collective-permute-start.14
  134.5 5.1 %collective-permute-done.14 = bf16[512,256]{1,0:T(8,128)(2,1)S(1)} collective-permute-done((bf16[512,256]{1,0:T(8,128)(2,1)S(1)}, bf16[512,256]{1,0:T(8,128)(2,1)S(1)}, u32[]{:S(2)}, u32[]{:S(2)}) %collective-permute-start.14) | collective-permute-done | bytes 262176 | tf_op jit(solution)/shard_map/ppermute | solution.py:67
  140.4 8.8 %fusion.7 = bf16[4096,256]{1,0:T(8,128)(2,1)} fusion(s32[4096]{0:T(1024)S(1)} %bitcast.51, bf16[512,4096]{1,0:T(8,128)(2,1)} %constant_dynamic-update-slice_fusion, bf16[256,4096]{1,0:T(8,128)(2,1)} %param.9, bf16[32,8,32,128]{3,2,1,0:T(8,128)(2,1)S(1)} %bitcast.44), kind=kOutput, calls=%fused_computation.11 | convolution fusion | flops 2151809024 | bytes 10502144 | tf_op jit(solution)/shard_map/dot_general | solution.py:18
  149.2 7.3 %all-to-all-start.1 = ((bf16[32,128,256]{2,1,0:T(8,128)(2,1)}), bf16[32,128,256]{2,1,0:T(8,128)(2,1)S(1)}, u32[]{:S(2)}, u32[]{:S(2)}) async-start(bf16[32,128,256]{2,1,0:T(8,128)(2,1)} %bitcast.46), calls=%async_computation.2 | async-start | bytes 4194304 | tf_op jit(solution)/shard_map/all_to_all | solution.py:76
  156.8 1.8 fusion.29
  159.7 8.8 %fusion.11 = bf16[2048,256]{1,0:T(8,128)(2,1)} fusion(bf16[4096,256]{1,0:T(8,128)(2,1)} %bitcast.11, s32[2048]{0:T(1024)S(1)} %bitcast.52), kind=kOutput, calls=%fused_computation.15 | convolution fusion | flops 4303880192 | bytes 3153920 | tf_op jit(solution)/shard_map/dot_general | solution.py:18
  168.4 2.2 %fusion.18 = f32[512,1,4]{2,1,0:T(1,128)S(1)} fusion(bf16[4,512,256]{2,1,0:T(8,128)(2,1)} %bitcast.55, bf16[512,256,1]{1,0,2:T(8,128)(2,1)} %bitcast.54), kind=kOutput, calls=%fused_computation.27 | convolution fusion | flops 1048576 | bytes 1318912 | tf_op jit(solution)/shard_map/re,kre->rk/dot_general | solution.py:80
  170.8 27.7 %psum.7 = f32[512,4]{0,1:T(4,128)S(1)} all-reduce(f32[512,4]{0,1:T(4,128)S(1)} %bitcast.49), channel_id=1, replica_groups=mesh['dp'=32,'wide'=16] {'wide'}, use_global_device_ids=true, to_apply=%region_2.3 | all-reduce | flops 2048 | bytes 16384 | tf_op jit(solution)/shard_map/psum | solution.py:81
  199.2 7.2 %fusion.12 = bf16[2048,256]{1,0:T(8,128)(2,1)} fusion(bf16[4096,256]{1,0:T(8,128)(2,1)S(1)} %bitcast.47, s32[2048]{0:T(1024)S(1)} %bitcast.53), kind=kOutput, calls=%fused_computation.16 | convolution fusion | flops 4303880192 | bytes 3153920 | tf_op jit(solution)/shard_map/dot_general | solution.py:18
  206.6 2.2 %fusion.16 = f32[512,1,256]{2,1,0:T(1,128)S(1)} fusion(bf16[512,4,1]{1,2,0:T(2,128)(2,1)S(1)} %copy.43, bf16[4,512,256]{2,1,0:T(8,128)(2,1)} %bitcast.56), kind=kOutput, calls=%fused_computation.25 | convolution fusion | flops 1048576 | bytes 1576960 | tf_op jit(solution)/shard_map/rk,kre->re/dot_general | solution.py:87
  (64 shorter events, 28.7 us)
Async XLA Ops:
  7.2 1.2 copy-start
  7.2 161.2 %reduce-scatter.2.cloned.1.call-start = ((), (), s32[]{:S(2)}) async-start(), calls=%async_computation.4 | async-start | bytes 4456448 | tf_op jit(solution)/shard_map/reduce_scatter | solution.py:32
  14.2 13.4 %copy-start.1 = (s32[512,4]{0,1:T(4,128)S(1)}, s32[512,4]{0,1:T(4,128)}, u32[]{:S(2)}) copy-start(s32[512,4]{0,1:T(4,128)} %param.12) | copy-start | bytes 24580
  14.2 18.0 %collective-permute-start = (bf16[512,256]{1,0:T(8,128)(2,1)}, bf16[512,256]{1,0:T(8,128)(2,1)}, u32[]{:S(2)}, u32[]{:S(2)}) collective-permute-start(bf16[512,256]{1,0:T(8,128)(2,1)} %param.11), channel_id=1, source_target_pairs={{0,1},{1,2},{2,3},{3,4},{4,5},{5,6},{6,7},{7,8},{8,9},{9,10},{10,1... | collective-permute-start | bytes 786440 | tf_op jit(solution)/shard_map/ppermute | solution.py:67
  18.1 16.6 %collective-permute-start.1 = (bf16[512,256]{1,0:T(8,128)(2,1)}, bf16[512,256]{1,0:T(8,128)(2,1)}, u32[]{:S(2)}, u32[]{:S(2)}) collective-permute-start(bf16[512,256]{1,0:T(8,128)(2,1)} %param.11), channel_id=1, source_target_pairs={{0,15},{1,0},{2,1},{3,2},{4,3},{5,4},{6,5},{7,6},{8,7},{9,8},{10,9... | collective-permute-start | bytes 786440 | tf_op jit(solution)/shard_map/ppermute | solution.py:70
  32.3 16.2 %collective-permute-start.2 = (bf16[512,256]{1,0:T(8,128)(2,1)}, bf16[512,256]{1,0:T(8,128)(2,1)}, u32[]{:S(2)}, u32[]{:S(2)}) collective-permute-start(bf16[512,256]{1,0:T(8,128)(2,1)} %collective-permute-done), channel_id=1, source_target_pairs={{0,1},{1,2},{2,3},{3,4},{4,5},{5,6},{6,7},{7,8},{8,9},{9,10},{10,1... | collective-permute-start | bytes 786440 | tf_op jit(solution)/shard_map/ppermute | solution.py:67
  34.7 29.2 %collective-permute-start.3 = (bf16[512,256]{1,0:T(8,128)(2,1)}, bf16[512,256]{1,0:T(8,128)(2,1)}, u32[]{:S(2)}, u32[]{:S(2)}) collective-permute-start(bf16[512,256]{1,0:T(8,128)(2,1)} %collective-permute-done.1), channel_id=1, source_target_pairs={{0,15},{1,0},{2,1},{3,2},{4,3},{5,4},{6,5},{7,6},{8,7},{9,8},{10,9... | collective-permute-start | bytes 786440 | tf_op jit(solution)/shard_map/ppermute | solution.py:70
  48.4 20.6 %collective-permute-start.4 = (bf16[512,256]{1,0:T(8,128)(2,1)}, bf16[512,256]{1,0:T(8,128)(2,1)}, u32[]{:S(2)}, u32[]{:S(2)}) collective-permute-start(bf16[512,256]{1,0:T(8,128)(2,1)} %collective-permute-done.2), channel_id=1, source_target_pairs={{0,1},{1,2},{2,3},{3,4},{4,5},{5,6},{6,7},{7,8},{8,9},{9,10},{10,1... | collective-permute-start | bytes 786440 | tf_op jit(solution)/shard_map/ppermute | solution.py:67
  51.0 20.0 %all-to-all-start = ((s32[32,1,128]{2,1,0:T(1,128)}), s32[32,1,128]{2,1,0:T(1,128)S(1)}, u32[]{:S(2)}, u32[]{:S(2)}) async-start(s32[32,1,128]{2,1,0:T(1,128)} %bitcast.4), calls=%async_computation.1 | async-start | bytes 32768 | tf_op jit(solution)/shard_map/all_to_all | solution.py:51
  63.9 20.5 %collective-permute-start.5 = (bf16[512,256]{1,0:T(8,128)(2,1)}, bf16[512,256]{1,0:T(8,128)(2,1)}, u32[]{:S(2)}, u32[]{:S(2)}) collective-permute-start(bf16[512,256]{1,0:T(8,128)(2,1)} %collective-permute-done.3), channel_id=1, source_target_pairs={{0,15},{1,0},{2,1},{3,2},{4,3},{5,4},{6,5},{7,6},{8,7},{9,8},{10,9... | collective-permute-start | bytes 786440 | tf_op jit(solution)/shard_map/ppermute | solution.py:70
  69.0 22.1 %collective-permute-start.6 = (bf16[512,256]{1,0:T(8,128)(2,1)}, bf16[512,256]{1,0:T(8,128)(2,1)}, u32[]{:S(2)}, u32[]{:S(2)}) collective-permute-start(bf16[512,256]{1,0:T(8,128)(2,1)} %collective-permute-done.4), channel_id=1, source_target_pairs={{0,1},{1,2},{2,3},{3,4},{4,5},{5,6},{6,7},{7,8},{8,9},{9,10},{10,1... | collective-permute-start | bytes 786440 | tf_op jit(solution)/shard_map/ppermute | solution.py:67
  75.2 74.0 %all-to-all-start.2 = ((bf16[32,128,256]{2,1,0:T(8,128)(2,1)}), bf16[32,128,256]{2,1,0:T(8,128)(2,1)}, u32[]{:S(2)}, u32[]{:S(2)}) async-start(bf16[32,128,256]{2,1,0:T(8,128)(2,1)} %bitcast.45), calls=%async_computation.3 | async-start | bytes 4194304 | tf_op jit(solution)/shard_map/all_to_all | solution.py:53
  84.4 17.0 %collective-permute-start.7 = (bf16[512,256]{1,0:T(8,128)(2,1)}, bf16[512,256]{1,0:T(8,128)(2,1)S(1)}, u32[]{:S(2)}, u32[]{:S(2)}) collective-permute-start(bf16[512,256]{1,0:T(8,128)(2,1)} %collective-permute-done.5), channel_id=1, source_target_pairs={{0,15},{1,0},{2,1},{3,2},{4,3},{5,4},{6,5},{7,6},{8,7},{9,8},{10,9... | collective-permute-start | bytes 786440 | tf_op jit(solution)/shard_map/ppermute | solution.py:70
  91.2 17.4 %collective-permute-start.8 = (bf16[512,256]{1,0:T(8,128)(2,1)}, bf16[512,256]{1,0:T(8,128)(2,1)S(1)}, u32[]{:S(2)}, u32[]{:S(2)}) collective-permute-start(bf16[512,256]{1,0:T(8,128)(2,1)} %collective-permute-done.6), channel_id=1, source_target_pairs={{0,1},{1,2},{2,3},{3,4},{4,5},{5,6},{6,7},{7,8},{8,9},{9,10},{10,1... | collective-permute-start | bytes 786440 | tf_op jit(solution)/shard_map/ppermute | solution.py:67
  101.4 12.6 %collective-permute-start.9 = (bf16[512,256]{1,0:T(8,128)(2,1)S(1)}, bf16[512,256]{1,0:T(8,128)(2,1)S(1)}, u32[]{:S(2)}, u32[]{:S(2)}) collective-permute-start(bf16[512,256]{1,0:T(8,128)(2,1)S(1)} %collective-permute-done.7), channel_id=1, source_target_pairs={{0,15},{1,0},{2,1},{3,2},{4,3},{5,4},{6,5},{7,6},{8,7},{9,8},{10,9... | collective-permute-start | bytes 786440 | tf_op jit(solution)/shard_map/ppermute | solution.py:70
  108.6 11.2 %collective-permute-start.10 = (bf16[512,256]{1,0:T(8,128)(2,1)S(1)}, bf16[512,256]{1,0:T(8,128)(2,1)S(1)}, u32[]{:S(2)}, u32[]{:S(2)}) collective-permute-start(bf16[512,256]{1,0:T(8,128)(2,1)S(1)} %collective-permute-done.8), channel_id=1, source_target_pairs={{0,1},{1,2},{2,3},{3,4},{4,5},{5,6},{6,7},{7,8},{8,9},{9,10},{10,1... | collective-permute-start | bytes 786440 | tf_op jit(solution)/shard_map/ppermute | solution.py:67
  114.0 9.9 %collective-permute-start.11 = (bf16[512,256]{1,0:T(8,128)(2,1)S(1)}, bf16[512,256]{1,0:T(8,128)(2,1)S(1)}, u32[]{:S(2)}, u32[]{:S(2)}) collective-permute-start(bf16[512,256]{1,0:T(8,128)(2,1)S(1)} %collective-permute-done.9), channel_id=1, source_target_pairs={{0,15},{1,0},{2,1},{3,2},{4,3},{5,4},{6,5},{7,6},{8,7},{9,8},{10,9... | collective-permute-start | bytes 786440 | tf_op jit(solution)/shard_map/ppermute | solution.py:70
  119.8 10.4 %collective-permute-start.12 = (bf16[512,256]{1,0:T(8,128)(2,1)S(1)}, bf16[512,256]{1,0:T(8,128)(2,1)S(1)}, u32[]{:S(2)}, u32[]{:S(2)}) collective-permute-start(bf16[512,256]{1,0:T(8,128)(2,1)S(1)} %collective-permute-done.10), channel_id=1, source_target_pairs={{0,1},{1,2},{2,3},{3,4},{4,5},{5,6},{6,7},{7,8},{8,9},{9,10},{10,1... | collective-permute-start | bytes 786440 | tf_op jit(solution)/shard_map/ppermute | solution.py:67
  123.8 9.9 %collective-permute-start.13 = (bf16[512,256]{1,0:T(8,128)(2,1)S(1)}, bf16[512,256]{1,0:T(8,128)(2,1)S(1)}, u32[]{:S(2)}, u32[]{:S(2)}) collective-permute-start(bf16[512,256]{1,0:T(8,128)(2,1)S(1)} %collective-permute-done.11), channel_id=1, source_target_pairs={{0,15},{1,0},{2,1},{3,2},{4,3},{5,4},{6,5},{7,6},{8,7},{9,8},{10,9... | collective-permute-start | bytes 786440 | tf_op jit(solution)/shard_map/ppermute | solution.py:70
  130.2 9.5 %collective-permute-start.14 = (bf16[512,256]{1,0:T(8,128)(2,1)S(1)}, bf16[512,256]{1,0:T(8,128)(2,1)S(1)}, u32[]{:S(2)}, u32[]{:S(2)}) collective-permute-start(bf16[512,256]{1,0:T(8,128)(2,1)S(1)} %collective-permute-done.12), channel_id=1, source_target_pairs={{0,1},{1,2},{2,3},{3,4},{4,5},{5,6},{6,7},{7,8},{8,9},{9,10},{10,1... | collective-permute-start | bytes 786440 | tf_op jit(solution)/shard_map/ppermute | solution.py:67
  149.2 49.3 %all-to-all-start.1 = ((bf16[32,128,256]{2,1,0:T(8,128)(2,1)}), bf16[32,128,256]{2,1,0:T(8,128)(2,1)S(1)}, u32[]{:S(2)}, u32[]{:S(2)}) async-start(bf16[32,128,256]{2,1,0:T(8,128)(2,1)} %bitcast.46), calls=%async_computation.2 | async-start | bytes 4194304 | tf_op jit(solution)/shard_map/all_to_all | solution.py:76
  168.4 30.1 %copy-start.2 = (s32[512,4]{0,1:T(4,128)S(1)}, s32[512,4]{0,1:T(4,128)}, u32[]{:S(2)}) copy-start(s32[512,4]{0,1:T(4,128)} %param.13) | copy-start | bytes 24580
Sparse Core Ops, SparseCore 0:
  14.4 94.5 reduce-scatter.1

commit v14 on v12

--- a/solution.py
+++ b/solution.py
@@ -63,6 +63,8 @@
     old_full = place(jnp.zeros((doc_shard, width), old_index.dtype), old_index, me_w)
     to_right, to_left = old_index, old_index
     for step in range(1, n_wide // 2 + 1):
+        if step == n_wide // 2 - 1:
+            old_vec, to_right = lax.optimization_barrier((old_vec, to_right))
         to_right = lax.ppermute(to_right, "wide", right)
         old_full = place(old_full, to_right, (me_w - step) % n_wide)
         if step < n_wide - n_wide // 2:

time: 215 us -> 226 us (1.051)
  blocking collectives: 27.7 us -> 41.6 us
  starting transfers between devices: 80.6 us -> 70.7 us
  waiting for transfers between devices: 22.7 us -> 28.8 us
  local copies, waits for them, and re-layouts: 26 us -> 28.5 us
    all_to_all x0 -> x1, blocking collectives: none -> 14.1 us  [local(): asked = lax.all_to_all(req, 'dp', 0, 0, tiled=True).reshape(-1)]
    ppermute x8, waiting for transfers between devices: 16.1 us -> 28.7 us  [local(): to_right = lax.ppermute(to_right, 'wide', right)]
    all_to_all x1 -> x0, starting transfers between devices: 7.72 us -> none  [local(): asked = lax.all_to_all(req, 'dp', 0, 0, tiled=True).reshape(-1)]
    ppermute x7, waiting for transfers between devices: 6.55 us -> 0.02 us  [local(): to_left = lax.ppermute(to_left, 'wide', left)]
  transfers between devices with their start and end apart: 19 -> 18, of which waited for: 5 -> 4; matrix products, arithmetic and copies ran while one was open for 24% -> 23% of each run, Pallas kernels for 0% -> 0%
where the time goes in v14:
time: 226 us; the launch traced here: 225 us
  starting transfers between devices  70.7 us (31%)
  blocking collectives  41.6 us (18%)
  matrix products  38.5 us (17%)
  waiting for transfers between devices  28.8 us (13%)
  local copies, waits for them, and re-layouts  28.5 us (13%)
  between operations  14.4 us (6%)
  other arithmetic  2.35 us (1%)
    ppermute x7, starting transfers between devices, local(): to_left = lax.ppermute(to_left, 'wide', left)  40.5 us
    ppermute x8, waiting for transfers between devices, local(): to_right = lax.ppermute(to_right, 'wide', right)  28.7 us
    dot_general x4, matrix products, pick_rows(): jnp.dot(one_hot(index, table.shape[0]), table, preferred_element_type=jnp...  28.1 us
    psum x1, blocking collectives, local(): score = lax.psum(partial_scores, 'wide') * scale  27.5 us
    dynamic_update_slice x16, local copies, waits for them, and re-layouts, place(): return lax.dynamic_update_slice_in_dim(full, block, source * e_local, 1)  20.6 us
    ppermute x8, starting transfers between devices, local(): to_right = lax.ppermute(to_right, 'wide', right)  16 us
    all_to_all x1, blocking collectives, local(): asked = lax.all_to_all(req, 'dp', 0, 0, tiled=True).reshape(-1)  14.1 us
    all_to_all x1, starting transfers between devices, local(): lax.all_to_all(served_g, 'dp', 0, 0, tiled=True)  7.72 us
  transfers between devices with their start and end apart: 18, of which 4 were waited for; matrix products, arithmetic and copies ran while one was open for 23% of the time, Pallas kernels for 0%

profile of v14, /device:TPU:6, one launch (start us, length us, event | category | flops | bytes accessed | tf_op | source)
XLA Modules:
  0.0 224.9 jit_solution(201829876191982169)
XLA Ops:
  8.4 5.8 %convolution_convert_fusion = bf16[512,4096]{1,0:T(8,128)(2,1)} fusion(bf16[512,1024]{1,0:T(8,128)(2,1)S(1)} %copy-done, bf16[1024,256]{1,0:T(8,128)(2,1)} %param.8, bf16[256,4096]{1,0:T(8,128)(2,1)} %param.9, bf16[32,8,32,128]{3,2,1,0:T(8,128)(2,1)S(1)} %bitcast.39), kind=kOutput, calls=%fused_computation.10 | convolution fusion | flops 1345454080 | bytes 9961472 | tf_op jit(solution)/shard_map/dot_general | solution.py:31
  17.6 14.1 %all_to_all.16 = s32[32,1,128]{2,1,0:T(1,128)S(1)} all-to-all(s32[32,1,128]{2,1,0:T(1,128)S(1)} %bitcast.44), channel_id=1, replica_groups=mesh['dp'=32,'wide'=16] {'dp'}, dimensions={0} | all-to-all | bytes 32768 | tf_op jit(solution)/shard_map/all_to_all | solution.py:51
  31.7 3.2 %fusion.7 = bf16[4096,256]{1,0:T(8,128)(2,1)} fusion(bf16[512,256]{1,0:T(8,128)(2,1)S(1)} %copy-done.1, s32[4096]{0:T(1024)S(1)} %bitcast.46), kind=kOutput, calls=%fused_computation.11 | convolution fusion | flops 1076887552 | bytes 2375680 | tf_op jit(solution)/shard_map/dot_general | solution.py:18
  35.0 6.4 %all-to-all-start.1 = ((bf16[32,128,256]{2,1,0:T(8,128)(2,1)}), bf16[32,128,256]{2,1,0:T(8,128)(2,1)}, u32[]{:S(2)}, u32[]{:S(2)}) async-start(bf16[32,128,256]{2,1,0:T(8,128)(2,1)} %bitcast.41), calls=%async_computation.2 | async-start | bytes 4194304 | tf_op jit(solution)/shard_map/all_to_all | solution.py:53
  41.4 2.6 %collective-permute-start = (bf16[512,256]{1,0:T(8,128)(2,1)S(1)}, bf16[512,256]{1,0:T(8,128)(2,1)}, u32[]{:S(2)}, u32[]{:S(2)}) collective-permute-start(bf16[512,256]{1,0:T(8,128)(2,1)S(1)} %copy-done.1), channel_id=1, source_target_pairs={{0,1},{1,2},{2,3},{3,4},{4,5},{5,6},{6,7},{7,8},{8,9},{9,10},{10,1... | collective-permute-start | bytes 786440 | tf_op jit(solution)/shard_map/ppermute | solution.py:68
  44.1 9.5 %collective-permute-start.1 = (bf16[512,256]{1,0:T(8,128)(2,1)S(1)}, bf16[512,256]{1,0:T(8,128)(2,1)}, u32[]{:S(2)}, u32[]{:S(2)}) collective-permute-start(bf16[512,256]{1,0:T(8,128)(2,1)S(1)} %copy-done.1), channel_id=1, source_target_pairs={{0,15},{1,0},{2,1},{3,2},{4,3},{5,4},{6,5},{7,6},{8,7},{9,8},{10,9... | collective-permute-start | bytes 786440 | tf_op jit(solution)/shard_map/ppermute | solution.py:71
  53.6 10.5 %collective-permute-done = bf16[512,256]{1,0:T(8,128)(2,1)} collective-permute-done((bf16[512,256]{1,0:T(8,128)(2,1)S(1)}, bf16[512,256]{1,0:T(8,128)(2,1)}, u32[]{:S(2)}, u32[]{:S(2)}) %collective-permute-start) | collective-permute-done | bytes 262176 | tf_op jit(solution)/shard_map/ppermute | solution.py:68
  64.0 1.9 collective-permute-start.2
  66.0 5.1 %collective-permute-start.3 = (bf16[512,256]{1,0:T(8,128)(2,1)}, bf16[512,256]{1,0:T(8,128)(2,1)}, u32[]{:S(2)}, u32[]{:S(2)}) collective-permute-start(bf16[512,256]{1,0:T(8,128)(2,1)} %collective-permute-done.1), channel_id=1, source_target_pairs={{0,15},{1,0},{2,1},{3,2},{4,3},{5,4},{6,5},{7,6},{8,7},{9,8},{10,9... | collective-permute-start | bytes 786440 | tf_op jit(solution)/shard_map/ppermute | solution.py:71
  71.1 10.6 %collective-permute-done.2 = bf16[512,256]{1,0:T(8,128)(2,1)} collective-permute-done((bf16[512,256]{1,0:T(8,128)(2,1)}, bf16[512,256]{1,0:T(8,128)(2,1)}, u32[]{:S(2)}, u32[]{:S(2)}) %collective-permute-start.2) | collective-permute-done | bytes 262176 | tf_op jit(solution)/shard_map/ppermute | solution.py:68
  81.7 1.9 collective-permute-start.4
  83.6 5.1 %collective-permute-start.5 = (bf16[512,256]{1,0:T(8,128)(2,1)}, bf16[512,256]{1,0:T(8,128)(2,1)}, u32[]{:S(2)}, u32[]{:S(2)}) collective-permute-start(bf16[512,256]{1,0:T(8,128)(2,1)} %collective-permute-done.3), channel_id=1, source_target_pairs={{0,15},{1,0},{2,1},{3,2},{4,3},{5,4},{6,5},{7,6},{8,7},{9,8},{10,9... | collective-permute-start | bytes 786440 | tf_op jit(solution)/shard_map/ppermute | solution.py:71
  88.8 2.5 %broadcast_in_dim.2 = bf16[512,4096]{1,0:T(8,128)(2,1)} broadcast(bf16[]{:T(256)} %constant.143.clone.1), dimensions={} | broadcast | bytes 4194306 | tf_op jit(solution)/shard_map/broadcast_in_dim | solution.py:63
  93.7 1.7 constant_dynamic-update-slice_fusion.13
  95.4 3.4 %collective-permute-done.4 = bf16[512,256]{1,0:T(8,128)(2,1)} collective-permute-done((bf16[512,256]{1,0:T(8,128)(2,1)}, bf16[512,256]{1,0:T(8,128)(2,1)}, u32[]{:S(2)}, u32[]{:S(2)}) %collective-permute-start.4) | collective-permute-done | bytes 262176 | tf_op jit(solution)/shard_map/ppermute | solution.py:68
  98.8 1.9 collective-permute-start.6
  100.7 5.1 %collective-permute-start.7 = (bf16[512,256]{1,0:T(8,128)(2,1)}, bf16[512,256]{1,0:T(8,128)(2,1)S(1)}, u32[]{:S(2)}, u32[]{:S(2)}) collective-permute-start(bf16[512,256]{1,0:T(8,128)(2,1)} %collective-permute-done.5), channel_id=1, source_target_pairs={{0,15},{1,0},{2,1},{3,2},{4,3},{5,4},{6,5},{7,6},{8,7},{9,8},{10,9... | collective-permute-start | bytes 786440 | tf_op jit(solution)/shard_map/ppermute | solution.py:71
  111.0 1.9 collective-permute-start.8
  112.9 5.1 %collective-permute-start.9 = (bf16[512,256]{1,0:T(8,128)(2,1)S(1)}, bf16[512,256]{1,0:T(8,128)(2,1)}, u32[]{:S(2)}, u32[]{:S(2)}) collective-permute-start(bf16[512,256]{1,0:T(8,128)(2,1)S(1)} %collective-permute-done.7), channel_id=1, source_target_pairs={{0,15},{1,0},{2,1},{3,2},{4,3},{5,4},{6,5},{7,6},{8,7},{9,8},{10,9... | collective-permute-start | bytes 786440 | tf_op jit(solution)/shard_map/ppermute | solution.py:71
  121.3 1.9 collective-permute-start.10
  123.2 5.3 %collective-permute-start.11 = (bf16[512,256]{1,0:T(8,128)(2,1)}, bf16[512,256]{1,0:T(8,128)(2,1)}, u32[]{:S(2)}, u32[]{:S(2)}) collective-permute-start(bf16[512,256]{1,0:T(8,128)(2,1)} %collective-permute-done.9), channel_id=1, source_target_pairs={{0,15},{1,0},{2,1},{3,2},{4,3},{5,4},{6,5},{7,6},{8,7},{9,8},{10,9... | collective-permute-start | bytes 786440 | tf_op jit(solution)/shard_map/ppermute | solution.py:71
  128.6 8.8 %fusion.11 = bf16[2048,256]{1,0:T(8,128)(2,1)} fusion(bf16[4096,256]{1,0:T(8,128)(2,1)} %bitcast.7, s32[2048]{0:T(1024)S(1)} %multiply_add_fusion), kind=kOutput, calls=%fused_computation.15 | convolution fusion | flops 4303880192 | bytes 3153920 | tf_op jit(solution)/shard_map/dot_general | solution.py:18
  137.3 2.1 reshape.271
  139.5 1.9 collective-permute-start.12
  143.8 5.2 %collective-permute-start.13 = (bf16[512,256]{1,0:T(8,128)(2,1)}, bf16[512,256]{1,0:T(8,128)(2,1)S(1)}, u32[]{:S(2)}, u32[]{:S(2)}) collective-permute-start(bf16[512,256]{1,0:T(8,128)(2,1)} %collective-permute-done.11), channel_id=1, source_target_pairs={{0,15},{1,0},{2,1},{3,2},{4,3},{5,4},{6,5},{7,6},{8,7},{9,8},{10,9... | collective-permute-start | bytes 786440 | tf_op jit(solution)/shard_map/ppermute | solution.py:71
  150.7 1.9 collective-permute-start.14
  155.9 4.3 %collective-permute-done.14 = bf16[512,256]{1,0:T(8,128)(2,1)S(1)} collective-permute-done((bf16[512,256]{1,0:T(8,128)(2,1)S(1)}, bf16[512,256]{1,0:T(8,128)(2,1)S(1)}, u32[]{:S(2)}, u32[]{:S(2)}) %collective-permute-start.14) | collective-permute-done | bytes 262176 | tf_op jit(solution)/shard_map/ppermute | solution.py:68
  160.9 8.8 %fusion.8 = bf16[4096,256]{1,0:T(8,128)(2,1)} fusion(s32[4096]{0:T(1024)S(1)} %bitcast.47, bf16[512,4096]{1,0:T(8,128)(2,1)} %constant_dynamic-update-slice_fusion, bf16[256,4096]{1,0:T(8,128)(2,1)} %param.9, bf16[32,8,32,128]{3,2,1,0:T(8,128)(2,1)S(1)} %bitcast.40), kind=kOutput, calls=%fused_computation.12 | convolution fusion | flops 2151809024 | bytes 10502144 | tf_op jit(solution)/shard_map/dot_general | solution.py:18
  169.8 7.7 %all-to-all-start.2 = ((bf16[32,128,256]{2,1,0:T(8,128)(2,1)}), bf16[32,128,256]{2,1,0:T(8,128)(2,1)S(1)}, u32[]{:S(2)}, u32[]{:S(2)}) async-start(bf16[32,128,256]{2,1,0:T(8,128)(2,1)} %bitcast.43), calls=%async_computation.3 | async-start | bytes 4194304 | tf_op jit(solution)/shard_map/all_to_all | solution.py:77
  177.5 2.0 fusion.21
  179.6 27.5 %psum.7 = f32[512,4]{0,1:T(4,128)S(1)} all-reduce(f32[512,4]{0,1:T(4,128)S(1)} %bitcast.45), channel_id=1, replica_groups=mesh['dp'=32,'wide'=16] {'wide'}, use_global_device_ids=true, to_apply=%region_2.3 | all-reduce | flops 2048 | bytes 16384 | tf_op jit(solution)/shard_map/psum | solution.py:82
  207.9 7.2 %fusion.12 = bf16[2048,256]{1,0:T(8,128)(2,1)} fusion(bf16[4096,256]{1,0:T(8,128)(2,1)S(1)} %bitcast.42, s32[2048]{0:T(1024)S(1)} %multiply_add_fusion), kind=kOutput, calls=%fused_computation.16 | convolution fusion | flops 4303880192 | bytes 3153920 | tf_op jit(solution)/shard_map/dot_general | solution.py:18
  (62 shorter events, 27.2 us)
Async XLA Ops:
  7.2 1.2 copy-start
  7.2 170.3 %reduce-scatter.2.cloned.1.call-start = ((), (), s32[]{:S(2)}) async-start(), calls=%async_computation.4 | async-start | bytes 4456448 | tf_op jit(solution)/shard_map/reduce_scatter | solution.py:32
  14.2 0.7 copy-start.3
  15.4 16.3 %copy-start.1 = (bf16[512,256]{1,0:T(8,128)(2,1)S(1)}, bf16[512,256]{1,0:T(8,128)(2,1)}, u32[]{:S(2)}) copy-start(bf16[512,256]{1,0:T(8,128)(2,1)} %param.11) | copy-start | bytes 786436
  35.0 93.6 %all-to-all-start.1 = ((bf16[32,128,256]{2,1,0:T(8,128)(2,1)}), bf16[32,128,256]{2,1,0:T(8,128)(2,1)}, u32[]{:S(2)}, u32[]{:S(2)}) async-start(bf16[32,128,256]{2,1,0:T(8,128)(2,1)} %bitcast.41), calls=%async_computation.2 | async-start | bytes 4194304 | tf_op jit(solution)/shard_map/all_to_all | solution.py:53
  41.4 22.6 %collective-permute-start = (bf16[512,256]{1,0:T(8,128)(2,1)S(1)}, bf16[512,256]{1,0:T(8,128)(2,1)}, u32[]{:S(2)}, u32[]{:S(2)}) collective-permute-start(bf16[512,256]{1,0:T(8,128)(2,1)S(1)} %copy-done.1), channel_id=1, source_target_pairs={{0,1},{1,2},{2,3},{3,4},{4,5},{5,6},{6,7},{7,8},{8,9},{9,10},{10,1... | collective-permute-start | bytes 786440 | tf_op jit(solution)/shard_map/ppermute | solution.py:68
  44.1 21.9 %collective-permute-start.1 = (bf16[512,256]{1,0:T(8,128)(2,1)S(1)}, bf16[512,256]{1,0:T(8,128)(2,1)}, u32[]{:S(2)}, u32[]{:S(2)}) collective-permute-start(bf16[512,256]{1,0:T(8,128)(2,1)S(1)} %copy-done.1), channel_id=1, source_target_pairs={{0,15},{1,0},{2,1},{3,2},{4,3},{5,4},{6,5},{7,6},{8,7},{9,8},{10,9... | collective-permute-start | bytes 786440 | tf_op jit(solution)/shard_map/ppermute | solution.py:71
  64.0 17.6 %collective-permute-start.2 = (bf16[512,256]{1,0:T(8,128)(2,1)}, bf16[512,256]{1,0:T(8,128)(2,1)}, u32[]{:S(2)}, u32[]{:S(2)}) collective-permute-start(bf16[512,256]{1,0:T(8,128)(2,1)} %collective-permute-done), channel_id=1, source_target_pairs={{0,1},{1,2},{2,3},{3,4},{4,5},{5,6},{6,7},{7,8},{8,9},{9,10},{10,1... | collective-permute-start | bytes 786440 | tf_op jit(solution)/shard_map/ppermute | solution.py:68
  66.0 17.6 %collective-permute-start.3 = (bf16[512,256]{1,0:T(8,128)(2,1)}, bf16[512,256]{1,0:T(8,128)(2,1)}, u32[]{:S(2)}, u32[]{:S(2)}) collective-permute-start(bf16[512,256]{1,0:T(8,128)(2,1)} %collective-permute-done.1), channel_id=1, source_target_pairs={{0,15},{1,0},{2,1},{3,2},{4,3},{5,4},{6,5},{7,6},{8,7},{9,8},{10,9... | collective-permute-start | bytes 786440 | tf_op jit(solution)/shard_map/ppermute | solution.py:71
  81.7 17.1 %collective-permute-start.4 = (bf16[512,256]{1,0:T(8,128)(2,1)}, bf16[512,256]{1,0:T(8,128)(2,1)}, u32[]{:S(2)}, u32[]{:S(2)}) collective-permute-start(bf16[512,256]{1,0:T(8,128)(2,1)} %collective-permute-done.2), channel_id=1, source_target_pairs={{0,1},{1,2},{2,3},{3,4},{4,5},{5,6},{6,7},{7,8},{8,9},{9,10},{10,1... | collective-permute-start | bytes 786440 | tf_op jit(solution)/shard_map/ppermute | solution.py:68
  83.6 17.1 %collective-permute-start.5 = (bf16[512,256]{1,0:T(8,128)(2,1)}, bf16[512,256]{1,0:T(8,128)(2,1)}, u32[]{:S(2)}, u32[]{:S(2)}) collective-permute-start(bf16[512,256]{1,0:T(8,128)(2,1)} %collective-permute-done.3), channel_id=1, source_target_pairs={{0,15},{1,0},{2,1},{3,2},{4,3},{5,4},{6,5},{7,6},{8,7},{9,8},{10,9... | collective-permute-start | bytes 786440 | tf_op jit(solution)/shard_map/ppermute | solution.py:71
  98.8 12.2 %collective-permute-start.6 = (bf16[512,256]{1,0:T(8,128)(2,1)}, bf16[512,256]{1,0:T(8,128)(2,1)S(1)}, u32[]{:S(2)}, u32[]{:S(2)}) collective-permute-start(bf16[512,256]{1,0:T(8,128)(2,1)} %collective-permute-done.4), channel_id=1, source_target_pairs={{0,1},{1,2},{2,3},{3,4},{4,5},{5,6},{6,7},{7,8},{8,9},{9,10},{10,1... | collective-permute-start | bytes 786440 | tf_op jit(solution)/shard_map/ppermute | solution.py:68
  100.7 12.2 %collective-permute-start.7 = (bf16[512,256]{1,0:T(8,128)(2,1)}, bf16[512,256]{1,0:T(8,128)(2,1)S(1)}, u32[]{:S(2)}, u32[]{:S(2)}) collective-permute-start(bf16[512,256]{1,0:T(8,128)(2,1)} %collective-permute-done.5), channel_id=1, source_target_pairs={{0,15},{1,0},{2,1},{3,2},{4,3},{5,4},{6,5},{7,6},{8,7},{9,8},{10,9... | collective-permute-start | bytes 786440 | tf_op jit(solution)/shard_map/ppermute | solution.py:71
  111.0 10.3 %collective-permute-start.8 = (bf16[512,256]{1,0:T(8,128)(2,1)S(1)}, bf16[512,256]{1,0:T(8,128)(2,1)S(1)}, u32[]{:S(2)}, u32[]{:S(2)}) collective-permute-start(bf16[512,256]{1,0:T(8,128)(2,1)S(1)} %collective-permute-done.6), channel_id=1, source_target_pairs={{0,1},{1,2},{2,3},{3,4},{4,5},{5,6},{6,7},{7,8},{8,9},{9,10},{10,1... | collective-permute-start | bytes 786440 | tf_op jit(solution)/shard_map/ppermute | solution.py:68
  112.9 10.3 %collective-permute-start.9 = (bf16[512,256]{1,0:T(8,128)(2,1)S(1)}, bf16[512,256]{1,0:T(8,128)(2,1)}, u32[]{:S(2)}, u32[]{:S(2)}) collective-permute-start(bf16[512,256]{1,0:T(8,128)(2,1)S(1)} %collective-permute-done.7), channel_id=1, source_target_pairs={{0,15},{1,0},{2,1},{3,2},{4,3},{5,4},{6,5},{7,6},{8,7},{9,8},{10,9... | collective-permute-start | bytes 786440 | tf_op jit(solution)/shard_map/ppermute | solution.py:71
  121.3 18.2 %collective-permute-start.10 = (bf16[512,256]{1,0:T(8,128)(2,1)S(1)}, bf16[512,256]{1,0:T(8,128)(2,1)}, u32[]{:S(2)}, u32[]{:S(2)}) collective-permute-start(bf16[512,256]{1,0:T(8,128)(2,1)S(1)} %collective-permute-done.8), channel_id=1, source_target_pairs={{0,1},{1,2},{2,3},{3,4},{4,5},{5,6},{6,7},{7,8},{8,9},{9,10},{10,1... | collective-permute-start | bytes 786440 | tf_op jit(solution)/shard_map/ppermute | solution.py:68
  123.2 20.6 %collective-permute-start.11 = (bf16[512,256]{1,0:T(8,128)(2,1)}, bf16[512,256]{1,0:T(8,128)(2,1)}, u32[]{:S(2)}, u32[]{:S(2)}) collective-permute-start(bf16[512,256]{1,0:T(8,128)(2,1)} %collective-permute-done.9), channel_id=1, source_target_pairs={{0,15},{1,0},{2,1},{3,2},{4,3},{5,4},{6,5},{7,6},{8,7},{9,8},{10,9... | collective-permute-start | bytes 786440 | tf_op jit(solution)/shard_map/ppermute | solution.py:71
  139.5 11.2 %collective-permute-start.12 = (bf16[512,256]{1,0:T(8,128)(2,1)}, bf16[512,256]{1,0:T(8,128)(2,1)S(1)}, u32[]{:S(2)}, u32[]{:S(2)}) collective-permute-start(bf16[512,256]{1,0:T(8,128)(2,1)} %collective-permute-done.10), channel_id=1, source_target_pairs={{0,1},{1,2},{2,3},{3,4},{4,5},{5,6},{6,7},{7,8},{8,9},{9,10},{10,1... | collective-permute-start | bytes 786440 | tf_op jit(solution)/shard_map/ppermute | solution.py:68
  143.8 11.2 %collective-permute-start.13 = (bf16[512,256]{1,0:T(8,128)(2,1)}, bf16[512,256]{1,0:T(8,128)(2,1)S(1)}, u32[]{:S(2)}, u32[]{:S(2)}) collective-permute-start(bf16[512,256]{1,0:T(8,128)(2,1)} %collective-permute-done.11), channel_id=1, source_target_pairs={{0,15},{1,0},{2,1},{3,2},{4,3},{5,4},{6,5},{7,6},{8,7},{9,8},{10,9... | collective-permute-start | bytes 786440 | tf_op jit(solution)/shard_map/ppermute | solution.py:71
  150.7 9.5 %collective-permute-start.14 = (bf16[512,256]{1,0:T(8,128)(2,1)S(1)}, bf16[512,256]{1,0:T(8,128)(2,1)S(1)}, u32[]{:S(2)}, u32[]{:S(2)}) collective-permute-start(bf16[512,256]{1,0:T(8,128)(2,1)S(1)} %collective-permute-done.12), channel_id=1, source_target_pairs={{0,1},{1,2},{2,3},{3,4},{4,5},{5,6},{6,7},{7,8},{8,9},{9,10},{10,1... | collective-permute-start | bytes 786440 | tf_op jit(solution)/shard_map/ppermute | solution.py:68
  169.8 37.4 %copy-start.2 = (s32[512,4]{0,1:T(4,128)S(1)}, s32[512,4]{0,1:T(4,128)}, u32[]{:S(2)}) copy-start(s32[512,4]{0,1:T(4,128)} %param.13) | copy-start | bytes 24580
  169.8 37.4 %all-to-all-start.2 = ((bf16[32,128,256]{2,1,0:T(8,128)(2,1)}), bf16[32,128,256]{2,1,0:T(8,128)(2,1)S(1)}, u32[]{:S(2)}, u32[]{:S(2)}) async-start(bf16[32,128,256]{2,1,0:T(8,128)(2,1)} %bitcast.43), calls=%async_computation.3 | async-start | bytes 4194304 | tf_op jit(solution)/shard_map/all_to_all | solution.py:77
Sparse Core Ops, SparseCore 0:
  14.4 94.8 reduce-scatter.1
